TPU v7x, 512 devices: a whole 4x4x16 slice. The times are simulated.
512 devices in a mesh: ctx: 128 (over x, z, core), head: 4 (over y).
Axes of the slice: x: 4, y: 4, z: 16, core: 2. Of those that a mesh axis runs over, the one named last changes fastest.
Arguments:
- lin_query: bfloat16 [32768, 256], P('ctx', 'head'), may hold values from -4 to 4
- lin_key: bfloat16 [32768, 256], P('ctx', 'head'), may hold values from -3 to 3
- lin_values: bfloat16 [32768, 2048], P('ctx', 'head'), may hold values from -43 to 43
- win_query: bfloat16 [32768, 2048], P('ctx', 'head'), may hold values from -30 to 30
- win_key: bfloat16 [32768, 2048], P('ctx', 'head'), may hold values from -30 to 30
- win_value: bfloat16 [32768, 2048], P('ctx', 'head'), may hold values from -4 to 4
- conv_weight: bfloat16 [3, 2048], P(None, 'head'), may hold values from -3 to 3
- head_gain: float32 [2048], P('head'), may hold values from 0.7 to 12.6
Outputs:
- mixed_out: bfloat16 [32768, 2048], P('ctx', 'head')
All inputs are finite; a program needn't handle non-finite values.
Results may differ from a plain program's by a relative error of at most 0.0019.
Values may be sent and summed in bfloat16 or wider, within the bound.
No kernel may reach another device: no remote copies, remote signals or barrier semaphores. Data moves between devices by JAX's collectives and lax.ppermute only.
A program may use at most 192 MiB of HBM per device.

v0:
```python
import math

import jax
import jax.numpy as jnp
from jax import lax
from jax.sharding import PartitionSpec as P

FDIM = 16
VDIM = 128
WIN = 64
TAPS = 3
D = 2048


def carried_in(part, axis, combine, identity):
    place = lax.axis_index(axis)
    gathered = jax.tree.map(lambda a: lax.all_gather(a, axis), part)
    state = jax.tree.map(lambda a, e: jnp.zeros_like(a) + jnp.asarray(e, a.dtype), part, identity)

    def one(hop, state):
        return combine(
            state, jax.tree.map(lambda a: lax.dynamic_index_in_dim(a, hop, 0, False), gathered)
        )

    return lax.fori_loop(0, place, one, state)


def passed_along(shard, axis, by):
    length = lax.axis_size(axis)
    pairs = [(i, i + by) for i in range(length) if 0 <= i + by < length]
    return lax.ppermute(shard, axis, pairs)


def features_outer(x_tok):
    xt = jnp.transpose(x_tok.astype(jnp.float32), (1, 2, 0))
    heads, fdim, count = xt.shape
    ones = jnp.ones((heads, 1, count), jnp.float32)
    outer = (xt[:, :, None, :] * xt[:, None, :, :]).reshape(heads, fdim * fdim, count) * (
        1.0 / math.sqrt(32.0)
    )
    return jnp.concatenate([ones, xt * 0.5, outer], axis=1)


def add_states(earlier, later):
    return (earlier[0] + later[0], earlier[1] + later[1])


def window_slab(query, key_ext, value_ext, start):
    count, width = query.shape
    heads = width // VDIM
    blocks = count // WIN
    qb = query.reshape(blocks, WIN, heads, VDIM)
    keys = jnp.concatenate(
        [
            key_ext[:count].reshape(blocks, WIN, heads, VDIM),
            key_ext[WIN:].reshape(blocks, WIN, heads, VDIM),
        ],
        axis=1,
    )
    vals = jnp.concatenate(
        [
            value_ext[:count].reshape(blocks, WIN, heads, VDIM),
            value_ext[WIN:].reshape(blocks, WIN, heads, VDIM),
        ],
        axis=1,
    )
    scores = jnp.einsum("bihe,bjhe->bhij", qb, keys, preferred_element_type=jnp.float32) * (
        1.0 / math.sqrt(VDIM)
    )
    rows_i = jnp.arange(WIN, dtype=jnp.int32)[:, None]
    cols_j = jnp.arange(2 * WIN, dtype=jnp.int32)[None, :]
    block_ids = jnp.arange(blocks, dtype=jnp.int32)[:, None, None]
    position = start + block_ids * WIN + cols_j[None] - WIN
    allowed = (cols_j > rows_i)[None] & (cols_j <= rows_i + WIN)[None] & (position >= 0)
    allowed = allowed[:, None]
    top = jnp.max(jnp.where(allowed, scores, jnp.float32(-1e30)), axis=-1, keepdims=True)
    prob = jnp.where(allowed, jnp.exp(scores - top), jnp.float32(0.0))
    total = jnp.sum(prob, axis=-1)
    out = jnp.einsum(
        "bhij,bjhe->bihe", prob.astype(jnp.bfloat16), vals, preferred_element_type=jnp.float32
    )
    out = out / jnp.transpose(total, (0, 2, 1))[..., None]
    return out.reshape(count, width)


def inner_causal(queries, keys, values):
    count = queries.shape[0]
    block_rows = min(512, count)
    sim = jnp.einsum("thf,shf->hts", queries, keys, preferred_element_type=jnp.float32) * 0.25
    row_pos = 0 + jnp.arange(block_rows, dtype=jnp.int32)
    causal = row_pos[:, None] >= jnp.arange(block_rows, dtype=jnp.int32)[None, :]
    weights = jnp.where(causal[None], 1.0 + sim + 0.5 * sim * sim, jnp.float32(0.0))
    denom_parts = jnp.sum(weights, axis=-1)
    numer_parts = jnp.einsum(
        "hts,shv->htv", weights.astype(jnp.bfloat16), values, preferred_element_type=jnp.float32
    )
    return (numer_parts, denom_parts)


def body(lin_query, lin_key, lin_values, win_query, win_key, win_value, conv_weight, head_gain):
    count = lin_query.shape[0]
    heads = lin_query.shape[1] // FDIM
    queries = lin_query.reshape(count, heads, FDIM)
    keys = lin_key.reshape(count, heads, FDIM)
    values = lin_values.reshape(count, heads, VDIM)
    values32 = values.astype(jnp.float32)
    phi_q = features_outer(queries)
    phi_k = features_outer(keys)
    local_state = jnp.einsum("hft,thv->hfv", phi_k, values32, precision=lax.Precision.HIGHEST)
    local_norm = jnp.sum(phi_k, axis=-1)
    empty = (jnp.zeros_like(local_state), jnp.zeros_like(local_norm))
    prior_state, prior_norm = carried_in((local_state, local_norm), "ctx", add_states, empty)
    start = lax.axis_index("ctx") * count
    rims = passed_along((win_key[count - WIN :], win_value[count - WIN :]), "ctx", 1)
    key_ext = jnp.concatenate([rims[0], win_key], axis=0)
    value_ext = jnp.concatenate([rims[1], win_value], axis=0)
    window_out = window_slab(win_query, key_ext, value_ext, start)
    taps = conv_weight.astype(jnp.float32)
    value_f32 = value_ext.astype(jnp.float32)
    conv_out = jnp.zeros((count, value_ext.shape[1]), jnp.float32)
    for tap in range(TAPS):
        conv_out = conv_out + taps[tap][None, :] * value_f32[WIN - tap : WIN - tap + count]
    inner_num, inner_den = inner_causal(queries, keys, values)
    numer = inner_num + jnp.einsum(
        "hft,hfv->htv", phi_q, prior_state, precision=lax.Precision.HIGHEST
    )
    denom = inner_den + jnp.einsum("hft,hf->ht", phi_q, prior_norm, precision=lax.Precision.HIGHEST)
    lin_out = jnp.transpose(numer / denom[..., None], (1, 0, 2)).reshape(count, heads * VDIM)
    mixed = head_gain[None, :] * (lin_out + window_out + conv_out)
    squares = lax.psum(jnp.sum(mixed * mixed, axis=-1), "head")
    msq = squares / D
    return (mixed * lax.rsqrt(msq + 1e-06)[:, None]).astype(jnp.bfloat16)


def solution(mesh):
    placed = (
        P("ctx", "head"),
        P("ctx", "head"),
        P("ctx", "head"),
        P("ctx", "head"),
        P("ctx", "head"),
        P("ctx", "head"),
        P(None, "head"),
        P("head"),
    )
    return jax.shard_map(
        body, mesh=mesh, in_specs=placed, out_specs=P("ctx", "head"), check_vma=False
    )
```

profile of v0, /device:TPU:487, one launch (start us, length us, event | category | flops | bytes accessed | tf_op | source)
XLA Modules:
  0.0 579.0 jit_solution(7322867377130730)
XLA Ops:
  8.3 1.6 fusion.9
  10.6 1.3 collective-permute-start.1
  11.9 1.3 collective-permute-start
  17.5 106.5 %all-gather.2 = f32[128,4,273]{2,1,0:T(4,128)} all-gather(f32[1,4,273]{2,1,0:T(4,128)S(1)} %bitcast.83), channel_id=3, replica_groups=mesh['ctx'=128,'head'=4] {'ctx'}, dimensions={0}, use_global_device_ids=true | all-gather | bytes 563472 | tf_op jit(solution)/shard_map/all_gather | solution.py:17
  127.2 1.7 fusion.6
  129.2 190.1 %all-gather.5.cloned.1.call-done = f32[512,273,128]{2,1,0:T(8,128)} async-done(((f32[4,273,128]{2,1,0:T(8,128)}), f32[512,273,128]{2,1,0:T(8,128)}) %all-gather.5.cloned.1.call-update) | async-done | bytes 71565328 | tf_op jit(solution)/shard_map/all_gather | solution.py:17
  319.4 238.4 %while.12 = (s32[]{:T(128)}, f32[4,273,128]{2,1,0:T(8,128)S(1)}, f32[4,273]{1,0:T(4,128)S(1)}, s32[]{:T(128)}, f32[128,4,273,128]{3,2,1,0:T(8,128)}, /*index=5*/...) while((s32[]{:T(128)}, f32[4,273,128]{2,1,0:T(8,128)S(1)}, f32[4,273]{1,0:T(4,128)S(1)}, s32[]{:T(128)}, ...), condition=%wide.region_2.3_spmd, body=%wide.region_1.2_spmd.sunk | while | flops 140873 | bytes 1690551 | solution.py:25
  319.4 1.2 bitcast_add_fusion.6
  321.3 1.2 bitcast_add_fusion.6
  323.1 1.2 bitcast_add_fusion.6
  325.0 1.2 bitcast_add_fusion.6
  330.7 1.2 bitcast_add_fusion.6
  332.5 1.2 bitcast_add_fusion.6
  343.8 1.2 bitcast_add_fusion.6
  345.7 1.2 bitcast_add_fusion.6
  347.6 1.2 bitcast_add_fusion.6
  349.4 1.2 bitcast_add_fusion.6
  351.3 1.2 bitcast_add_fusion.6
  362.6 1.2 bitcast_add_fusion.6
  364.5 1.2 bitcast_add_fusion.6
  366.3 1.2 bitcast_add_fusion.6
  368.2 1.2 bitcast_add_fusion.6
  379.5 1.2 bitcast_add_fusion.6
  381.3 1.2 bitcast_add_fusion.6
  383.2 1.2 bitcast_add_fusion.6
  385.1 1.2 bitcast_add_fusion.6
  387.0 1.2 bitcast_add_fusion.6
  394.5 1.2 bitcast_add_fusion.6
  396.4 1.2 bitcast_add_fusion.6
  398.3 1.2 bitcast_add_fusion.6
  400.1 1.2 bitcast_add_fusion.6
  402.0 1.2 bitcast_add_fusion.6
  413.3 1.2 bitcast_add_fusion.6
  415.2 1.2 bitcast_add_fusion.6
  417.0 1.2 bitcast_add_fusion.6
  418.9 1.2 bitcast_add_fusion.6
  430.2 1.2 bitcast_add_fusion.6
  432.0 1.2 bitcast_add_fusion.6
  433.9 1.2 bitcast_add_fusion.6
  435.8 1.2 bitcast_add_fusion.6
  437.7 1.2 bitcast_add_fusion.6
  448.9 1.2 bitcast_add_fusion.6
  450.8 1.2 bitcast_add_fusion.6
  452.7 1.2 bitcast_add_fusion.6
  454.6 1.2 bitcast_add_fusion.6
  558.8 2.4 fusion.2
  561.2 1.2 copy.33
  562.8 8.5 %psum.7 = f32[256]{0:T(256)S(1)} all-reduce(f32[256]{0:T(256)S(1)} %get-tuple-element.53), channel_id=1, replica_groups=mesh['ctx'=128,'head'=4] {'head'}, use_global_device_ids=true, to_apply=%region_7.8 | all-reduce | flops 256 | bytes 2048 | tf_op jit(solution)/shard_map/psum | solution.py:130
  (289 shorter events, 205.9 us)
Async XLA Ops:
  6.5 1.7 copy-start
  6.5 312.8 %all-gather.5.cloned.1.call-start = ((), (), s32[]{:S(2)}) async-start(), calls=%async_computation | async-start | bytes 73973760 | tf_op jit(solution)/shard_map/all_gather | solution.py:17
  8.3 1.7 copy-start.2
  8.3 3.6 copy-start.1
  9.9 4.0 copy-start.9
  9.9 4.6 copy-start.5
  9.9 5.3 copy-start.6
  10.6 113.9 %collective-permute-start.1 = (bf16[64,512]{1,0:T(8,128)(2,1)}, bf16[64,512]{1,0:T(8,128)(2,1)}, u32[]{:S(2)}, u32[]{:S(2)}) collective-permute-start(bf16[64,512]{1,0:T(8,128)(2,1)} %slice.32), channel_id=1, source_target_pairs={{0,4},{4,8},{8,12},{12,16},{16,20},{20,24},{24,28},{28,32},{32,36}... | collective-permute-start | bytes 196616 | tf_op jit(solution)/shard_map/ppermute | solution.py:31
  11.9 112.5 %collective-permute-start = (bf16[64,512]{1,0:T(8,128)(2,1)S(1)}, bf16[64,512]{1,0:T(8,128)(2,1)S(1)}, u32[]{:S(2)}, u32[]{:S(2)}) collective-permute-start(bf16[64,512]{1,0:T(8,128)(2,1)S(1)} %slice.30), channel_id=1, source_target_pairs={{0,4},{4,8},{8,12},{12,16},{16,20},{20,24},{24,28},{28,32},{32,36}... | collective-permute-start | bytes 196616 | tf_op jit(solution)/shard_map/ppermute | solution.py:31
  17.5 106.7 %copy-start.4 = (bf16[256,512]{1,0:T(8,128)(2,1)S(1)}, bf16[256,512]{1,0:T(8,128)(2,1)}, u32[]{:S(2)}) copy-start(bf16[256,512]{1,0:T(8,128)(2,1)} %param.13) | copy-start | bytes 786436
  125.6 0.8 copy-start.8
  126.3 0.9 copy-start.12
  319.4 238.4 %copy-start.7 = (f32[4,16,256]{2,1,0:T(8,128)S(1)}, f32[4,16,256]{2,1,0:T(8,128)}, u32[]{:S(2)}) copy-start(f32[4,16,256]{2,1,0:T(8,128)} %broadcast_multiply_fusion.1) | copy-start | bytes 196612
  557.8 1.0 copy-start.10
  557.8 1.0 copy-start.3
  558.8 3.7 copy-start.11
Sparse Core Ops, SparseCore 0:
  10.5 308.7 all-gather.4
where the time goes:
time: 590 us; the launch traced here: 579 us
  other arithmetic  244 us (41%)
  waiting for transfers between devices  190 us (32%)
  blocking collectives  115 us (19%)
  between operations  13.7 us (2%)
  matrix products  9.28 us (2%)
    add x254, other arithmetic, add_states(): return (earlier[0] + later[0], earlier[1] + later[1])  238 us
    all_gather x1, waiting for transfers between devices, carried_in(): gathered = jax.tree.map(lambda a: lax.all_gather(a, axis), part)  190 us
    all_gather x1, blocking collectives, carried_in(): gathered = jax.tree.map(lambda a: lax.all_gather(a, axis), part)  107 us
  transfers between devices with their start and end apart: 3, of which 1 were waited for; matrix products, arithmetic and copies ran while one was open for 2% of the time, Pallas kernels for 0%

commit v1 on v0

--- a/solution.py
+++ b/solution.py
@@ -1,5 +1,6 @@
 import math
 
+import numpy as np
 import jax
 import jax.numpy as jnp
 from jax import lax
@@ -10,19 +11,7 @@
 WIN = 64
 TAPS = 3
 D = 2048
-
-
-def carried_in(part, axis, combine, identity):
-    place = lax.axis_index(axis)
-    gathered = jax.tree.map(lambda a: lax.all_gather(a, axis), part)
-    state = jax.tree.map(lambda a, e: jnp.zeros_like(a) + jnp.asarray(e, a.dtype), part, identity)
-
-    def one(hop, state):
-        return combine(
-            state, jax.tree.map(lambda a: lax.dynamic_index_in_dim(a, hop, 0, False), gathered)
-        )
-
-    return lax.fori_loop(0, place, one, state)
+HIGH = lax.Precision.HIGHEST
 
 
 def passed_along(shard, axis, by):
@@ -31,18 +20,30 @@
     return lax.ppermute(shard, axis, pairs)
 
 
-def features_outer(x_tok):
+def compact_features(x_tok, doubled):
     xt = jnp.transpose(x_tok.astype(jnp.float32), (1, 2, 0))
     heads, fdim, count = xt.shape
     ones = jnp.ones((heads, 1, count), jnp.float32)
-    outer = (xt[:, :, None, :] * xt[:, None, :, :]).reshape(heads, fdim * fdim, count) * (
-        1.0 / math.sqrt(32.0)
-    )
+    rows = []
+    for i in range(fdim):
+        part = xt[:, i : i + 1, :] * xt[:, i:, :]
+        if doubled:
+            scale = np.full((1, fdim - i, 1), 2.0, np.float32)
+            scale[0, 0, 0] = 1.0
+            part = part * scale
+        rows.append(part)
+    outer = jnp.concatenate(rows, axis=1) * (1.0 / math.sqrt(32.0))
     return jnp.concatenate([ones, xt * 0.5, outer], axis=1)
 
 
-def add_states(earlier, later):
-    return (earlier[0] + later[0], earlier[1] + later[1])
+def exclusive_prefix(flat, axis):
+    size = lax.axis_size(axis)
+    chunks = flat.reshape(size, -1)
+    recv = lax.all_to_all(chunks, axis, 0, 0, tiled=True)
+    lower = jnp.asarray(np.tril(np.ones((size, size), np.float32), -1))
+    pref = jnp.dot(lower, recv, precision=HIGH, preferred_element_type=jnp.float32)
+    back = lax.all_to_all(pref, axis, 0, 0, tiled=True)
+    return back.reshape(-1)
 
 
 def window_slab(query, key_ext, value_ext, start):
@@ -85,16 +86,26 @@
 
 def inner_causal(queries, keys, values):
     count = queries.shape[0]
-    block_rows = min(512, count)
     sim = jnp.einsum("thf,shf->hts", queries, keys, preferred_element_type=jnp.float32) * 0.25
-    row_pos = 0 + jnp.arange(block_rows, dtype=jnp.int32)
-    causal = row_pos[:, None] >= jnp.arange(block_rows, dtype=jnp.int32)[None, :]
+    row_pos = jnp.arange(count, dtype=jnp.int32)
+    causal = row_pos[:, None] >= row_pos[None, :]
     weights = jnp.where(causal[None], 1.0 + sim + 0.5 * sim * sim, jnp.float32(0.0))
     denom_parts = jnp.sum(weights, axis=-1)
     numer_parts = jnp.einsum(
         "hts,shv->htv", weights.astype(jnp.bfloat16), values, preferred_element_type=jnp.float32
     )
     return (numer_parts, denom_parts)
+
+
+def head_sum(part, axis):
+    size = lax.axis_size(axis)
+    total = part
+    step = 1
+    while step < size:
+        pairs = [(i, i ^ step) for i in range(size)]
+        total = total + lax.ppermute(total, axis, pairs)
+        step *= 2
+    return total
 
 
 def body(lin_query, lin_key, lin_values, win_query, win_key, win_value, conv_weight, head_gain):
@@ -104,12 +115,21 @@
     keys = lin_key.reshape(count, heads, FDIM)
     values = lin_values.reshape(count, heads, VDIM)
     values32 = values.astype(jnp.float32)
-    phi_q = features_outer(queries)
-    phi_k = features_outer(keys)
-    local_state = jnp.einsum("hft,thv->hfv", phi_k, values32, precision=lax.Precision.HIGHEST)
+    phi_q = compact_features(queries, True)
+    phi_k = compact_features(keys, False)
+    feat = phi_k.shape[1]
+    local_state = jnp.einsum("hft,thv->hfv", phi_k, values32, precision=HIGH)
     local_norm = jnp.sum(phi_k, axis=-1)
-    empty = (jnp.zeros_like(local_state), jnp.zeros_like(local_norm))
-    prior_state, prior_norm = carried_in((local_state, local_norm), "ctx", add_states, empty)
+    size = lax.axis_size("ctx")
+    packed = jnp.concatenate([local_state.reshape(-1), local_norm.reshape(-1)])
+    used = packed.shape[0]
+    quantum = size * 128
+    padded = -(-used // quantum) * quantum
+    packed = jnp.pad(packed, (0, padded - used))
+    prior = exclusive_prefix(packed, "ctx")
+    split = heads * feat * VDIM
+    prior_state = prior[:split].reshape(heads, feat, VDIM)
+    prior_norm = prior[split:used].reshape(heads, feat)
     start = lax.axis_index("ctx") * count
     rims = passed_along((win_key[count - WIN :], win_value[count - WIN :]), "ctx", 1)
     key_ext = jnp.concatenate([rims[0], win_key], axis=0)
@@ -121,13 +141,11 @@
     for tap in range(TAPS):
         conv_out = conv_out + taps[tap][None, :] * value_f32[WIN - tap : WIN - tap + count]
     inner_num, inner_den = inner_causal(queries, keys, values)
-    numer = inner_num + jnp.einsum(
-        "hft,hfv->htv", phi_q, prior_state, precision=lax.Precision.HIGHEST
-    )
-    denom = inner_den + jnp.einsum("hft,hf->ht", phi_q, prior_norm, precision=lax.Precision.HIGHEST)
+    numer = inner_num + jnp.einsum("hft,hfv->htv", phi_q, prior_state, precision=HIGH)
+    denom = inner_den + jnp.einsum("hft,hf->ht", phi_q, prior_norm, precision=HIGH)
     lin_out = jnp.transpose(numer / denom[..., None], (1, 0, 2)).reshape(count, heads * VDIM)
     mixed = head_gain[None, :] * (lin_out + window_out + conv_out)
-    squares = lax.psum(jnp.sum(mixed * mixed, axis=-1), "head")
+    squares = head_sum(jnp.sum(mixed * mixed, axis=-1), "head")
     msq = squares / D
     return (mixed * lax.rsqrt(msq + 1e-06)[:, None]).astype(jnp.bfloat16)
 

time: 590 us -> 107 us (0.18)
  the two profiles are of different devices: /device:TPU:487 before, /device:TPU:16 now
where the time goes in v1:
time: 107 us; the launch traced here: 106 us
  starting transfers between devices  40.3 us (38%)
  waiting for transfers between devices  32.1 us (30%)
  local copies, waits for them, and re-layouts  21.2 us (20%)
  matrix products  6.12 us (6%)
  other arithmetic  5.73 us (5%)
    all_to_all x1, starting transfers between devices, exclusive_prefix(): recv = lax.all_to_all(chunks, axis, 0, 0, tiled=True)  19.9 us
    all_to_all x1, waiting for transfers between devices, exclusive_prefix(): back = lax.all_to_all(pref, axis, 0, 0, tiled=True)  18.5 us
    unnamed x77, local copies, waits for them, and re-layouts  14.1 us
    all_to_all x1, starting transfers between devices, exclusive_prefix(): back = lax.all_to_all(pref, axis, 0, 0, tiled=True)  9.92 us
    ppermute x2, waiting for transfers between devices, head_sum(): total = total + lax.ppermute(total, axis, pairs)  7 us
    all_to_all x1, waiting for transfers between devices, exclusive_prefix(): recv = lax.all_to_all(chunks, axis, 0, 0, tiled=True)  6.57 us
    ppermute x2, starting transfers between devices, head_sum(): total = total + lax.ppermute(total, axis, pairs)  5.41 us
    ppermute x2, starting transfers between devices, passed_along(): return lax.ppermute(shard, axis, pairs)  5.06 us
  transfers between devices with their start and end apart: 6, of which 4 were waited for; matrix products, arithmetic and copies ran while one was open for 11% of the time, Pallas kernels for 0%

profile of v1, /device:TPU:16, one launch (start us, length us, event | category | flops | bytes accessed | tf_op | source)
XLA Modules:
  0.0 106.1 jit_solution(7228224015292637371)
XLA Ops:
  0.0 0.8 convert_bitcast_fusion
  1.2 0.7 copy-done.8
  1.9 1.3 %concatenate.29 = f32[4,136,256]{2,1,0:T(8,128)S(1)} concatenate(f32[4,16,256]{2,1,0:T(8,128)S(1)} %get-tuple-element.42, f32[4,15,256]{2,1,0:T(8,128)S(1)} %slice_multiply_fusion.9, f32[4,14,256]{2,1,0:T(8,128)S(1)} %slice_multiply_fusion.8, f32[4,13,256]{2,1,0:T(8,128)S(1)} %slice_multiply_fusion.7, f32[4,12,256]{2,1,0:T(8,128)S(1)} %slice_multiply_fusion.6, ...), dimensions={1} | concatenate | bytes 1114112 | tf_op jit(solution)/shard_map/concatenate | solution.py:35
  3.6 0.5 fusion.22
  4.3 0.8 select_maximum_fusion
  5.1 19.9 %all-to-all-start = ((f32[128,1,640]{2,1,0:T(1,128)}), f32[128,1,640]{2,1,0:T(1,128)S(1)}, u32[]{:S(2)}, u32[]{:S(2)}) async-start(f32[128,1,640]{2,1,0:T(1,128)} %bitcast.4), calls=%async_computation | async-start | bytes 655360 | tf_op jit(solution)/shard_map/all_to_all | solution.py:42
  25.0 1.5 %collective-permute-start.1 = (bf16[64,512]{1,0:T(8,128)(2,1)S(1)}, bf16[64,512]{1,0:T(8,128)(2,1)S(1)}, u32[]{:S(2)}, u32[]{:S(2)}) collective-permute-start(bf16[64,512]{1,0:T(8,128)(2,1)S(1)} %slice.282), channel_id=1, source_target_pairs={{0,4},{4,8},{8,12},{12,16},{16,20},{20,24},{24,28},{28,32},{32,36}... | collective-permute-start | bytes 196616 | tf_op jit(solution)/shard_map/ppermute | solution.py:20
  26.6 3.5 %collective-permute-start = (bf16[64,512]{1,0:T(8,128)(2,1)S(1)}, bf16[64,512]{1,0:T(8,128)(2,1)S(1)}, u32[]{:S(2)}, u32[]{:S(2)}) collective-permute-start(bf16[64,512]{1,0:T(8,128)(2,1)S(1)} %slice.280), channel_id=1, source_target_pairs={{0,4},{4,8},{8,12},{12,16},{16,20},{20,24},{24,28},{28,32},{32,36}... | collective-permute-start | bytes 196616 | tf_op jit(solution)/shard_map/ppermute | solution.py:20
  30.3 0.6 copy-done.27
  31.0 0.6 copy-done.26
  31.7 0.7 copy-done.25
  32.5 0.6 copy-done.24
  33.2 0.7 copy-done.23
  33.9 0.6 copy-done.22
  34.7 0.7 copy-done.21
  35.4 0.6 copy-done.20
  36.1 0.7 copy-done.19
  36.9 0.7 copy-done.18
  37.6 0.7 copy-done.17
  38.3 0.7 copy-done.16
  39.1 0.7 copy-done.15
  39.8 0.7 copy-done.28
  40.5 0.7 copy-done.14
  41.2 0.6 fusion.48
  41.8 1.3 %concatenate.27 = f32[4,136,256]{2,1,0:T(8,128)S(1)} concatenate(f32[4,16,256]{2,1,0:T(8,128)S(1)} %get-tuple-element.40, f32[4,15,256]{2,1,0:T(8,128)S(1)} %fusion.43, f32[4,14,256]{2,1,0:T(8,128)S(1)} %fusion.42, f32[4,13,256]{2,1,0:T(8,128)S(1)} %fusion.41, f32[4,12,256]{2,1,0:T(8,128)S(1)} %fusion.40, f32[4,11,256]{2,1,0:T(8,128)S(1)} %fusion.39, f32[4,10,256]{2,1,0:T(8,128)S(1)} %fusion.38, ...), dimensions={1} | concatenate | bytes 1114112 | tf_op jit(solution)/shard_map/concatenate | solution.py:35
  43.3 1.1 %fusion.72 = (f32[4,256]{1,0:T(4,128)}, bf16[4,256,256]{1,2,0:T(8,128)(2,1)S(1)}) fusion(bf16[256,4,16]{0,2,1:T(8,128)(2,1)S(1)} %bitcast.140, bf16[256,4,16]{0,2,1:T(8,128)(2,1)S(1)} %bitcast.141, pred[256,256]{0,1:T(8,128)(4,1)S(1)} %iota_compare_fusion.1), kind=kOutput, calls=%fused_computation.159 | convolution fusion | flops 10484736 | bytes 659456 | tf_op jit(solution)/shard_map/thf,shf->hts/dot_general | solution.py:89
  44.7 6.6 %all-to-all-done = f32[128,1,640]{2,1,0:T(1,128)S(1)} async-done(((f32[128,1,640]{2,1,0:T(1,128)}), f32[128,1,640]{2,1,0:T(1,128)S(1)}, u32[]{:S(2)}, u32[]{:S(2)}) %all-to-all-start) | async-done | bytes 327712 | tf_op jit(solution)/shard_map/all_to_all | solution.py:42
  51.3 0.4 convolution_bitcast_fusion.1
  51.7 1.1 %copy.44 = f32[128,1,640]{2,1,0:T(1,128)} copy(f32[128,1,640]{2,0,1:T(8,128)S(1)} %convolution_bitcast_fusion.1) | data formatting | bytes 655360 | tf_op jit(solution)/shard_map/all_to_all | solution.py:45
  52.8 9.9 %all-to-all-start.1 = ((f32[128,1,640]{2,1,0:T(1,128)}), f32[128,1,640]{2,1,0:T(1,128)S(1)}, u32[]{:S(2)}, u32[]{:S(2)}) async-start(f32[128,1,640]{2,1,0:T(1,128)} %copy.44), calls=%async_computation.1 | async-start | bytes 655360 | tf_op jit(solution)/shard_map/all_to_all | solution.py:45
  63.0 0.9 copy-done.3
  63.9 0.8 reshape.156
  64.7 0.8 copy.46
  65.8 0.7 copy.45
  66.7 0.4 fusion.7
  67.2 0.4 fusion.73
  67.6 0.4 copy-done.29
  68.4 1.6 %fusion.6 = f32[4,64,4,128]{3,1,2,0:T(8,128)S(1)} fusion(bf16[4,64,4,128]{3,1,2,0:T(8,128)(2,1)S(1)} %copy-done.4, bf16[4,64,4,128]{3,1,2,0:T(8,128)(2,1)S(1)} %copy-done.6, f32[4,64,4]{1,2,0:T(4,128)S(1)} %bitcast.147, f32[4,4,64,128]{3,2,1,0:T(8,128)} %copy-done.29, pred[4,64,128]{2,1,0:T(8,128)(4,1)S(1)} %broadcast_and_fusion), kind=kOutput, calls=%fused_computation.8 | convolution fusion | flops 35259520 | bytes 1609728 | tf_op jit(solution)/shard_map/bhij,bjhe->bihe/dot_general | solution.py:80
  70.4 18.5 %all-to-all-done.1 = f32[128,1,640]{2,1,0:T(1,128)S(1)} async-done(((f32[128,1,640]{2,1,0:T(1,128)}), f32[128,1,640]{2,1,0:T(1,128)S(1)}, u32[]{:S(2)}, u32[]{:S(2)}) %all-to-all-start.1) | async-done | bytes 327712 | tf_op jit(solution)/shard_map/all_to_all | solution.py:45
  89.0 0.8 copy-done.9
  89.8 0.6 fusion.23
  90.5 1.1 %fusion.2 = f32[256,4,128]{0,2,1:T(8,128)S(1)} fusion(f32[4,256,128]{1,2,0:T(8,128)S(1)} %fusion.19, f32[4,153,128]{2,1,0:T(8,128)S(1)} %reshape.149, f32[4,136,256]{2,1,0:T(8,128)S(1)} %broadcast_multiply_fusion.1, f32[4,16,256]{2,1,0:T(8,128)S(1)} %copy-done.9, f32[153]{0:T(256)S(1)} %pad.16.clone, f32[256,4]{0,1:T(4,128)S(1)} %fusion.59), kind=kOutput, calls=%fused_computation.4 | convolution fusion | flops 241223680 | bytes 1989220 | tf_op jit(solution)/shard_map/hft,hfv->htv/dot_general | solution.py:144
  91.9 0.7 copy-done.13
  92.9 3.2 %collective-permute-start.2 = (f32[256]{0:T(256)S(1)}, f32[256]{0:T(256)S(1)}, u32[]{:S(2)}, u32[]{:S(2)}) collective-permute-start(f32[256]{0:T(256)S(1)} %get-tuple-element.5), channel_id=1, source_target_pairs={{0,1},{1,0},{2,3},{3,2},{4,5},{5,4},{6,7},{7,6},{8,9},{9,8},{10,11... | collective-permute-start | bytes 3080 | tf_op jit(solution)/shard_map/ppermute | solution.py:106
  96.1 2.3 %collective-permute-done.2 = f32[256]{0:T(256)S(1)} collective-permute-done((f32[256]{0:T(256)S(1)}, f32[256]{0:T(256)S(1)}, u32[]{:S(2)}, u32[]{:S(2)}) %collective-permute-start.2) | collective-permute-done | bytes 1056 | tf_op jit(solution)/shard_map/ppermute | solution.py:106
  98.3 2.2 %collective-permute-start.3 = (f32[256]{0:T(256)S(1)}, f32[256]{0:T(256)S(1)}, u32[]{:S(2)}, u32[]{:S(2)}) collective-permute-start(f32[256]{0:T(256)S(1)} %add.113), channel_id=1, source_target_pairs={{0,2},{1,3},{2,0},{3,1},{4,6},{5,7},{6,4},{7,5},{8,10},{9,11},{10,... | collective-permute-start | bytes 3080 | tf_op jit(solution)/shard_map/ppermute | solution.py:106
  100.6 4.7 %collective-permute-done.3 = f32[256]{0:T(256)S(1)} collective-permute-done((f32[256]{0:T(256)S(1)}, f32[256]{0:T(256)S(1)}, u32[]{:S(2)}, u32[]{:S(2)}) %collective-permute-start.3) | collective-permute-done | bytes 1056 | tf_op jit(solution)/shard_map/ppermute | solution.py:106
  105.3 0.8 multiply_convert_fusion
  (127 shorter events, 4.7 us)
Async XLA Ops:
  0.0 3.6 %copy-start = (bf16[256,512]{1,0:T(8,128)(2,1)S(1)}, bf16[256,512]{1,0:T(8,128)(2,1)}, u32[]{:S(2)}) copy-start(bf16[256,512]{1,0:T(8,128)(2,1)} %param.27) | copy-start | bytes 786436
  1.2 0.8 copy-start.8
  5.1 19.9 %copy-start.2 = (bf16[256,512]{1,0:T(8,128)(2,1)S(1)}, bf16[256,512]{1,0:T(8,128)(2,1)}, u32[]{:S(2)}) copy-start(bf16[256,512]{1,0:T(8,128)(2,1)} %param.29) | copy-start | bytes 786436
  5.1 21.5 %copy-start.1 = (bf16[256,512]{1,0:T(8,128)(2,1)S(1)}, bf16[256,512]{1,0:T(8,128)(2,1)}, u32[]{:S(2)}) copy-start(bf16[256,512]{1,0:T(8,128)(2,1)} %param.30) | copy-start | bytes 786436
  5.1 46.2 %all-to-all-start = ((f32[128,1,640]{2,1,0:T(1,128)}), f32[128,1,640]{2,1,0:T(1,128)S(1)}, u32[]{:S(2)}, u32[]{:S(2)}) async-start(f32[128,1,640]{2,1,0:T(1,128)} %bitcast.4), calls=%async_computation | async-start | bytes 655360 | tf_op jit(solution)/shard_map/all_to_all | solution.py:42
  25.0 40.6 %collective-permute-start.1 = (bf16[64,512]{1,0:T(8,128)(2,1)S(1)}, bf16[64,512]{1,0:T(8,128)(2,1)S(1)}, u32[]{:S(2)}, u32[]{:S(2)}) collective-permute-start(bf16[64,512]{1,0:T(8,128)(2,1)S(1)} %slice.282), channel_id=1, source_target_pairs={{0,4},{4,8},{8,12},{12,16},{16,20},{20,24},{24,28},{28,32},{32,36}... | collective-permute-start | bytes 196616 | tf_op jit(solution)/shard_map/ppermute | solution.py:20
  26.6 3.6 %copy-start.7 = (bf16[256,64]{0,1:T(8,128)(2,1)S(1)}, bf16[256,64]{0,1:T(8,128)(2,1)}, u32[]{:S(2)}) copy-start(bf16[256,64]{0,1:T(8,128)(2,1)} %param.25) | copy-start | bytes 98308
  26.6 38.9 %collective-permute-start = (bf16[64,512]{1,0:T(8,128)(2,1)S(1)}, bf16[64,512]{1,0:T(8,128)(2,1)S(1)}, u32[]{:S(2)}, u32[]{:S(2)}) collective-permute-start(bf16[64,512]{1,0:T(8,128)(2,1)S(1)} %slice.280), channel_id=1, source_target_pairs={{0,4},{4,8},{8,12},{12,16},{16,20},{20,24},{24,28},{28,32},{32,36}... | collective-permute-start | bytes 196616 | tf_op jit(solution)/shard_map/ppermute | solution.py:20
  30.3 0.7 copy-start.27
  31.0 0.7 copy-start.26
  31.7 0.7 copy-start.25
  32.5 0.7 copy-start.24
  33.2 0.7 copy-start.23
  33.9 0.7 copy-start.22
  34.7 0.7 copy-start.21
  35.4 0.7 copy-start.20
  36.1 0.7 copy-start.19
  36.9 0.7 copy-start.18
  37.6 0.7 copy-start.17
  38.3 0.7 copy-start.16
  39.1 0.7 copy-start.15
  39.8 0.7 copy-start.28
  40.5 0.7 copy-start.14
  44.4 6.9 %copy-start.10 = (f32[128,128]{1,0:T(8,128)S(1)}, f32[128,128]{1,0:T(8,128)}, u32[]{:S(2)}) copy-start(f32[128,128]{1,0:T(8,128)} %constant.93.clone) | copy-start | bytes 196612
  52.8 10.0 %copy-start.11 = (bf16[3,512]{1,0:T(4,128)(2,1)S(1)}, bf16[3,512]{1,0:T(4,128)(2,1)}, u32[]{:S(2)}) copy-start(bf16[3,512]{1,0:T(4,128)(2,1)} %param.31) | copy-start | bytes 9220
  52.8 36.1 %all-to-all-start.1 = ((f32[128,1,640]{2,1,0:T(1,128)}), f32[128,1,640]{2,1,0:T(1,128)S(1)}, u32[]{:S(2)}, u32[]{:S(2)}) async-start(f32[128,1,640]{2,1,0:T(1,128)} %copy.44), calls=%async_computation.1 | async-start | bytes 655360 | tf_op jit(solution)/shard_map/all_to_all | solution.py:45
  62.9 1.0 copy-start.3
  65.8 1.0 copy-start.5
  67.2 0.8 copy-start.29
  67.2 1.1 %copy-start.4 = (bf16[4,64,4,128]{3,1,2,0:T(8,128)(2,1)S(1)}, bf16[4,64,4,128]{3,1,2,0:T(8,128)(2,1)}, u32[]{:S(2)}) copy-start(bf16[4,64,4,128]{3,1,2,0:T(8,128)(2,1)} %copy.46) | copy-start | bytes 786436
  67.2 1.2 %copy-start.6 = (bf16[4,64,4,128]{3,1,2,0:T(8,128)(2,1)S(1)}, bf16[4,64,4,128]{3,1,2,0:T(8,128)(2,1)}, u32[]{:S(2)}) copy-start(bf16[4,64,4,128]{3,1,2,0:T(8,128)(2,1)} %copy.45) | copy-start | bytes 786436
  89.0 0.8 copy-start.9
  89.8 0.7 copy-start.12
  91.9 0.7 copy-start.13
  92.9 5.5 %collective-permute-start.2 = (f32[256]{0:T(256)S(1)}, f32[256]{0:T(256)S(1)}, u32[]{:S(2)}, u32[]{:S(2)}) collective-permute-start(f32[256]{0:T(256)S(1)} %get-tuple-element.5), channel_id=1, source_target_pairs={{0,1},{1,0},{2,3},{3,2},{4,5},{5,4},{6,7},{7,6},{8,9},{9,8},{10,11... | collective-permute-start | bytes 3080 | tf_op jit(solution)/shard_map/ppermute | solution.py:106
  98.3 7.0 %collective-permute-start.3 = (f32[256]{0:T(256)S(1)}, f32[256]{0:T(256)S(1)}, u32[]{:S(2)}, u32[]{:S(2)}) collective-permute-start(f32[256]{0:T(256)S(1)} %add.113), channel_id=1, source_target_pairs={{0,2},{1,3},{2,0},{3,1},{4,6},{5,7},{6,4},{7,5},{8,10},{9,11},{10,... | collective-permute-start | bytes 3080 | tf_op jit(solution)/shard_map/ppermute | solution.py:106

commit v2 on v1

--- a/solution.py
+++ b/solution.py
@@ -20,20 +20,33 @@
     return lax.ppermute(shard, axis, pairs)
 
 
-def compact_features(x_tok, doubled):
+def features_outer(x_tok):
     xt = jnp.transpose(x_tok.astype(jnp.float32), (1, 2, 0))
     heads, fdim, count = xt.shape
     ones = jnp.ones((heads, 1, count), jnp.float32)
-    rows = []
-    for i in range(fdim):
-        part = xt[:, i : i + 1, :] * xt[:, i:, :]
-        if doubled:
-            scale = np.full((1, fdim - i, 1), 2.0, np.float32)
-            scale[0, 0, 0] = 1.0
-            part = part * scale
-        rows.append(part)
-    outer = jnp.concatenate(rows, axis=1) * (1.0 / math.sqrt(32.0))
+    outer = (xt[:, :, None, :] * xt[:, None, :, :]).reshape(heads, fdim * fdim, count) * (
+        1.0 / math.sqrt(32.0)
+    )
     return jnp.concatenate([ones, xt * 0.5, outer], axis=1)
+
+
+def fold_matrix(fdim, doubled):
+    full = 1 + fdim + fdim * fdim
+    pairs = [(i, j) for i in range(fdim) for j in range(i, fdim)]
+    fold = np.zeros((1 + fdim + len(pairs), full), np.float32)
+    for r in range(1 + fdim):
+        fold[r, r] = 1.0
+    for r, (i, j) in enumerate(pairs):
+        fold[1 + fdim + r, 1 + fdim + i * fdim + j] = 1.0
+        if doubled and i != j:
+            fold[1 + fdim + r, 1 + fdim + j * fdim + i] = 1.0
+    return jnp.asarray(fold)
+
+
+def compact_features(x_tok, doubled):
+    full = features_outer(x_tok)
+    fold = fold_matrix(x_tok.shape[-1], doubled)
+    return jnp.einsum("cf,hft->hct", fold, full, precision=HIGH)
 
 
 def exclusive_prefix(flat, axis):

time: 107 us -> 103 us (0.963)
  the two profiles are of different devices: /device:TPU:16 before, /device:TPU:8 now
where the time goes in v2:
time: 103 us
  waiting for transfers between devices  41.4 us (40%)
  starting transfers between devices  37.8 us (37%)
  matrix products  10.3 us (10%)
  local copies, waits for them, and re-layouts  7.66 us (7%)
  other arithmetic  5.04 us (5%)
    all_to_all x1, starting transfers between devices, exclusive_prefix(): recv = lax.all_to_all(chunks, axis, 0, 0, tiled=True)  19.8 us
    all_to_all x1, waiting for transfers between devices, exclusive_prefix(): back = lax.all_to_all(pref, axis, 0, 0, tiled=True)  18.4 us
    all_to_all x1, waiting for transfers between devices, exclusive_prefix(): recv = lax.all_to_all(chunks, axis, 0, 0, tiled=True)  17.1 us
    ppermute x2, starting transfers between devices, head_sum(): total = total + lax.ppermute(total, axis, pairs)  6.54 us
    all_to_all x1, starting transfers between devices, exclusive_prefix(): back = lax.all_to_all(pref, axis, 0, 0, tiled=True)  6.46 us
    ppermute x2, waiting for transfers between devices, head_sum(): total = total + lax.ppermute(total, axis, pairs)  5.86 us
    ppermute x2, starting transfers between devices, passed_along(): return lax.ppermute(shard, axis, pairs)  5.05 us
    dot_general x2, matrix products, compact_features(): return jnp.einsum('cf,hft->hct', fold, full, precision=HIGH)  3.08 us
  transfers between devices with their start and end apart: 6, of which 4 were waited for; matrix products, arithmetic and copies ran while one was open for 11% of the time, Pallas kernels for 0%

profile of v2, /device:TPU:8, one launch (start us, length us, event | category | flops | bytes accessed | tf_op | source)
XLA Modules:
  0.0 102.6 jit_solution(6364895853134926957)
XLA Ops:
  0.0 0.8 convert_bitcast_fusion
  0.8 0.8 broadcast_multiply_fusion
  1.6 0.1 multiply_multiply_fusion
  1.8 1.6 %fusion.61 = (f32[4,153]{1,0:T(4,128)S(1)}, f32[4,256,153]{1,2,0:T(8,128)S(1)}) fusion(f32[153,273,1]{1,0,2:T(8,128)S(1)} %copy-done.7, f32[4,256,256]{2,1,0:T(8,128)S(1)} %bitcast.79, f32[4,16,256]{2,1,0:T(8,128)S(1)} %broadcast_multiply_fusion, f32[273]{0:T(512)S(1)} %pad.16.clone), kind=kOutput, calls=%fused_computation.87 | convolution fusion | flops 513972640 | bytes 1911416 | tf_op jit(solution)/shard_map/cf,hft->hct/dot_general | solution.py:49
  3.4 0.4 fusion.36
  3.9 0.1 reshape.161
  4.0 0.7 select_maximum_fusion
  4.8 19.8 %all-to-all-start = ((f32[128,1,640]{2,1,0:T(1,128)}), f32[128,1,640]{2,1,0:T(1,128)S(1)}, u32[]{:S(2)}, u32[]{:S(2)}) async-start(f32[128,1,640]{2,1,0:T(1,128)} %bitcast.8), calls=%async_computation | async-start | bytes 655360 | tf_op jit(solution)/shard_map/all_to_all | solution.py:55
  24.6 0.6 slice.40
  25.2 1.5 %collective-permute-start.1 = (bf16[64,512]{1,0:T(8,128)(2,1)}, bf16[64,512]{1,0:T(8,128)(2,1)S(1)}, u32[]{:S(2)}, u32[]{:S(2)}) collective-permute-start(bf16[64,512]{1,0:T(8,128)(2,1)} %slice.40), channel_id=1, source_target_pairs={{0,4},{4,8},{8,12},{12,16},{16,20},{20,24},{24,28},{28,32},{32,36}... | collective-permute-start | bytes 196616 | tf_op jit(solution)/shard_map/ppermute | solution.py:20
  26.7 3.5 %collective-permute-start = (bf16[64,512]{1,0:T(8,128)(2,1)S(1)}, bf16[64,512]{1,0:T(8,128)(2,1)S(1)}, u32[]{:S(2)}, u32[]{:S(2)}) collective-permute-start(bf16[64,512]{1,0:T(8,128)(2,1)S(1)} %slice.38), channel_id=1, source_target_pairs={{0,4},{4,8},{8,12},{12,16},{16,20},{20,24},{24,28},{28,32},{32,36}... | collective-permute-start | bytes 196616 | tf_op jit(solution)/shard_map/ppermute | solution.py:20
  30.3 0.1 fusion.48
  30.4 0.1 add_compare_fusion
  30.5 0.5 fusion.62
  31.1 0.1 multiply_multiply_fusion.1
  31.2 0.8 copy-done.6
  32.0 1.4 %fusion.8 = f32[4,256,153]{1,2,0:T(8,128)S(1)} fusion(f32[153,273,1]{1,0,2:T(8,128)S(1)} %copy-done.6, f32[4,256,256]{2,1,0:T(8,128)S(1)} %bitcast.80, f32[4,16,256]{2,1,0:T(8,128)S(1)} %broadcast_multiply_fusion.1, f32[273]{0:T(512)S(1)} %pad.16.clone), kind=kOutput, calls=%fused_computation.12 | convolution fusion | flops 513816576 | bytes 1908968 | tf_op jit(solution)/shard_map/cf,hft->hct/dot_general | solution.py:49
  33.5 0.3 fusion.31
  33.8 17.1 %all-to-all-done = f32[128,1,640]{2,1,0:T(1,128)S(1)} async-done(((f32[128,1,640]{2,1,0:T(1,128)}), f32[128,1,640]{2,1,0:T(1,128)S(1)}, u32[]{:S(2)}, u32[]{:S(2)}) %all-to-all-start) | async-done | bytes 327712 | tf_op jit(solution)/shard_map/all_to_all | solution.py:55
  50.9 0.4 convolution_bitcast_fusion.1
  51.3 1.1 %copy.30 = f32[128,1,640]{2,1,0:T(1,128)} copy(f32[128,1,640]{2,0,1:T(8,128)S(1)} %convolution_bitcast_fusion.1) | data formatting | bytes 655360 | tf_op jit(solution)/shard_map/all_to_all | solution.py:58
  52.4 6.5 %all-to-all-start.1 = ((f32[128,1,640]{2,1,0:T(1,128)}), f32[128,1,640]{2,1,0:T(1,128)S(1)}, u32[]{:S(2)}, u32[]{:S(2)}) async-start(f32[128,1,640]{2,1,0:T(1,128)} %copy.30), calls=%async_computation.1 | async-start | bytes 655360 | tf_op jit(solution)/shard_map/all_to_all | solution.py:58
  58.8 0.6 broadcast_and_fusion
  59.5 0.1 reshape.169
  59.5 0.1 reshape.167
  59.7 0.8 reshape.170
  60.4 0.8 copy.32
  61.4 0.1 reshape.168
  61.5 0.8 copy.33
  62.2 0.1 reshape.166
  62.4 1.4 %fusion.7 = f32[4,4,64,128]{3,2,1,0:T(8,128)S(1)} fusion(bf16[4,64,4,128]{3,1,2,0:T(8,128)(2,1)S(1)} %copy.34, bf16[4,64,4,128]{3,1,2,0:T(8,128)(2,1)} %copy.33, bf16[4,64,4,128]{3,2,1,0:T(4,128)(2,1)S(1)} %copy-done.5), kind=kOutput, calls=%fused_computation.10 | convolution fusion | flops 34734080 | bytes 1310720 | tf_op jit(solution)/shard_map/bihe,bjhe->bhij/dot_general | solution.py:81
  63.9 0.4 fusion.63
  64.2 0.4 copy-done.14
  64.7 1.6 %fusion.6 = f32[4,64,4,128]{3,1,2,0:T(8,128)S(1)} fusion(bf16[4,64,4,128]{3,1,2,0:T(8,128)(2,1)S(1)} %copy-done.4, bf16[4,64,4,128]{3,1,2,0:T(8,128)(2,1)S(1)} %copy.31, f32[4,64,4]{1,2,0:T(4,128)S(1)} %bitcast.90, f32[4,4,64,128]{3,2,1,0:T(8,128)} %copy-done.14, pred[4,64,128]{2,1,0:T(8,128)(4,1)S(1)} %copy-done.11), kind=kOutput, calls=%fused_computation.8 | convolution fusion | flops 35259520 | bytes 1609728 | tf_op jit(solution)/shard_map/bhij,bjhe->bihe/dot_general | solution.py:93
  66.2 0.3 copy.36
  66.6 18.4 %all-to-all-done.1 = f32[128,1,640]{2,1,0:T(1,128)S(1)} async-done(((f32[128,1,640]{2,1,0:T(1,128)}), f32[128,1,640]{2,1,0:T(1,128)S(1)}, u32[]{:S(2)}, u32[]{:S(2)}) %all-to-all-start.1) | async-done | bytes 327712 | tf_op jit(solution)/shard_map/all_to_all | solution.py:58
  85.0 0.1 reshape.177
  85.1 0.7 reshape.163
  85.8 0.5 fusion.64
  86.3 2.0 %fusion.2 = f32[256,4,128]{0,2,1:T(8,128)S(1)} fusion(f32[4,256,128]{1,2,0:T(8,128)S(1)} %fusion.31, f32[4,256,153]{1,2,0:T(8,128)S(1)} %fusion.8, f32[4,153,128]{2,1,0:T(8,128)} %reshape.163, f32[256,4]{0,1:T(4,128)S(1)} %fusion.49), kind=kOutput, calls=%fused_computation.4 | convolution fusion | flops 240910336 | bytes 1992704 | tf_op jit(solution)/shard_map/hft,hfv->htv/dot_general | solution.py:157
  88.4 0.2 copy.37
  88.6 0.5 copy-done.13
  89.0 0.3 multiply_reduce_fusion
  89.4 2.4 %collective-permute-start.2 = (f32[256]{0:T(256)S(1)}, f32[256]{0:T(256)S(1)}, u32[]{:S(2)}, u32[]{:S(2)}) collective-permute-start(f32[256]{0:T(256)S(1)} %get-tuple-element.5), channel_id=1, source_target_pairs={{0,1},{1,0},{2,3},{3,2},{4,5},{5,4},{6,7},{7,6},{8,9},{9,8},{10,11... | collective-permute-start | bytes 3080 | tf_op jit(solution)/shard_map/ppermute | solution.py:119
  91.7 3.1 %collective-permute-done.2 = f32[256]{0:T(256)S(1)} collective-permute-done((f32[256]{0:T(256)S(1)}, f32[256]{0:T(256)S(1)}, u32[]{:S(2)}, u32[]{:S(2)}) %collective-permute-start.2) | collective-permute-done | bytes 1056 | tf_op jit(solution)/shard_map/ppermute | solution.py:119
  94.8 4.2 %collective-permute-start.3 = (f32[256]{0:T(256)S(1)}, f32[256]{0:T(256)S(1)}, u32[]{:S(2)}, u32[]{:S(2)}) collective-permute-start(f32[256]{0:T(256)S(1)} %add.113), channel_id=1, source_target_pairs={{0,2},{1,3},{2,0},{3,1},{4,6},{5,7},{6,4},{7,5},{8,10},{9,11},{10,... | collective-permute-start | bytes 3080 | tf_op jit(solution)/shard_map/ppermute | solution.py:119
  99.0 2.8 %collective-permute-done.3 = f32[256]{0:T(256)S(1)} collective-permute-done((f32[256]{0:T(256)S(1)}, f32[256]{0:T(256)S(1)}, u32[]{:S(2)}, u32[]{:S(2)}) %collective-permute-start.3) | collective-permute-done | bytes 1056 | tf_op jit(solution)/shard_map/ppermute | solution.py:119
  101.8 0.8 multiply_convert_fusion
  (50 shorter events, 0.5 us)
Async XLA Ops:
  0.0 3.4 %copy-start = (bf16[256,512]{1,0:T(8,128)(2,1)S(1)}, bf16[256,512]{1,0:T(8,128)(2,1)}, u32[]{:S(2)}) copy-start(bf16[256,512]{1,0:T(8,128)(2,1)} %param.13) | copy-start | bytes 786436
  0.0 1.7 %copy-start.7 = (f32[153,273,1]{1,0,2:T(8,128)S(1)}, f32[153,273,1]{1,0,2:T(8,128)}, u32[]{:S(2)}) copy-start(f32[153,273,1]{1,0,2:T(8,128)} %constant.55) | copy-start | bytes 501232
  3.9 20.7 %copy-start.2 = (bf16[256,512]{1,0:T(8,128)(2,1)S(1)}, bf16[256,512]{1,0:T(8,128)(2,1)}, u32[]{:S(2)}) copy-start(bf16[256,512]{1,0:T(8,128)(2,1)} %param.15) | copy-start | bytes 786436
  3.9 22.8 %copy-start.1 = (bf16[256,512]{1,0:T(8,128)(2,1)S(1)}, bf16[256,512]{1,0:T(8,128)(2,1)}, u32[]{:S(2)}) copy-start(bf16[256,512]{1,0:T(8,128)(2,1)} %param.16) | copy-start | bytes 786436
  3.9 26.4 %copy-start.8 = (bf16[256,64]{0,1:T(8,128)(2,1)S(1)}, bf16[256,64]{0,1:T(8,128)(2,1)}, u32[]{:S(2)}) copy-start(bf16[256,64]{0,1:T(8,128)(2,1)} %param.11) | copy-start | bytes 98308
  3.9 26.6 %copy-start.9 = (bf16[256,64]{0,1:T(8,128)(2,1)S(1)}, bf16[256,64]{0,1:T(8,128)(2,1)}, u32[]{:S(2)}) copy-start(bf16[256,64]{0,1:T(8,128)(2,1)} %param.12) | copy-start | bytes 98308
  4.8 46.1 %all-to-all-start = ((f32[128,1,640]{2,1,0:T(1,128)}), f32[128,1,640]{2,1,0:T(1,128)S(1)}, u32[]{:S(2)}, u32[]{:S(2)}) async-start(f32[128,1,640]{2,1,0:T(1,128)} %bitcast.8), calls=%async_computation | async-start | bytes 655360 | tf_op jit(solution)/shard_map/all_to_all | solution.py:55
  25.2 36.2 %collective-permute-start.1 = (bf16[64,512]{1,0:T(8,128)(2,1)}, bf16[64,512]{1,0:T(8,128)(2,1)S(1)}, u32[]{:S(2)}, u32[]{:S(2)}) collective-permute-start(bf16[64,512]{1,0:T(8,128)(2,1)} %slice.40), channel_id=1, source_target_pairs={{0,4},{4,8},{8,12},{12,16},{16,20},{20,24},{24,28},{28,32},{32,36}... | collective-permute-start | bytes 196616 | tf_op jit(solution)/shard_map/ppermute | solution.py:20
  26.7 34.5 %collective-permute-start = (bf16[64,512]{1,0:T(8,128)(2,1)S(1)}, bf16[64,512]{1,0:T(8,128)(2,1)S(1)}, u32[]{:S(2)}, u32[]{:S(2)}) collective-permute-start(bf16[64,512]{1,0:T(8,128)(2,1)S(1)} %slice.38), channel_id=1, source_target_pairs={{0,4},{4,8},{8,12},{12,16},{16,20},{20,24},{24,28},{28,32},{32,36}... | collective-permute-start | bytes 196616 | tf_op jit(solution)/shard_map/ppermute | solution.py:20
  31.1 0.9 copy-start.6
  33.5 17.4 %copy-start.10 = (f32[128,128]{1,0:T(8,128)S(1)}, f32[128,128]{1,0:T(8,128)}, u32[]{:S(2)}) copy-start(f32[128,128]{1,0:T(8,128)} %constant.51.clone) | copy-start | bytes 196612
  33.8 25.7 %copy-start.12 = (bf16[3,512]{1,0:T(4,128)(2,1)S(1)}, bf16[3,512]{1,0:T(4,128)(2,1)}, u32[]{:S(2)}) copy-start(bf16[3,512]{1,0:T(4,128)(2,1)} %param.17) | copy-start | bytes 9220
  52.4 7.3 %copy-start.3 = (bf16[256,512]{1,0:T(8,128)(2,1)S(1)}, bf16[256,512]{1,0:T(8,128)(2,1)}, u32[]{:S(2)}) copy-start(bf16[256,512]{1,0:T(8,128)(2,1)} %param.14) | copy-start | bytes 786436
  52.4 32.6 %all-to-all-start.1 = ((f32[128,1,640]{2,1,0:T(1,128)}), f32[128,1,640]{2,1,0:T(1,128)S(1)}, u32[]{:S(2)}, u32[]{:S(2)}) async-start(f32[128,1,640]{2,1,0:T(1,128)} %copy.30), calls=%async_computation.1 | async-start | bytes 655360 | tf_op jit(solution)/shard_map/all_to_all | solution.py:58
  61.4 1.0 copy-start.5
  62.3 1.6 %copy-start.11 = (pred[4,64,128]{2,1,0:T(8,128)(4,1)S(1)}, pred[4,64,128]{2,1,0:T(8,128)(4,1)}, u32[]{:S(2)}) copy-start(pred[4,64,128]{2,1,0:T(8,128)(4,1)} %broadcast_and_fusion) | copy-start | bytes 98308
  62.4 2.3 %copy-start.4 = (bf16[4,64,4,128]{3,1,2,0:T(8,128)(2,1)S(1)}, bf16[4,64,4,128]{3,1,2,0:T(8,128)(2,1)}, u32[]{:S(2)}) copy-start(bf16[4,64,4,128]{3,1,2,0:T(8,128)(2,1)} %copy.32) | copy-start | bytes 786436
  63.9 0.8 copy-start.14
  88.4 0.7 copy-start.13
  89.4 5.5 %collective-permute-start.2 = (f32[256]{0:T(256)S(1)}, f32[256]{0:T(256)S(1)}, u32[]{:S(2)}, u32[]{:S(2)}) collective-permute-start(f32[256]{0:T(256)S(1)} %get-tuple-element.5), channel_id=1, source_target_pairs={{0,1},{1,0},{2,3},{3,2},{4,5},{5,4},{6,7},{7,6},{8,9},{9,8},{10,11... | collective-permute-start | bytes 3080 | tf_op jit(solution)/shard_map/ppermute | solution.py:119
  94.8 7.0 %collective-permute-start.3 = (f32[256]{0:T(256)S(1)}, f32[256]{0:T(256)S(1)}, u32[]{:S(2)}, u32[]{:S(2)}) collective-permute-start(f32[256]{0:T(256)S(1)} %add.113), channel_id=1, source_target_pairs={{0,2},{1,3},{2,0},{3,1},{4,6},{5,7},{6,4},{7,5},{8,10},{9,11},{10,... | collective-permute-start | bytes 3080 | tf_op jit(solution)/shard_map/ppermute | solution.py:119

commit v3 on v2

--- a/solution.py
+++ b/solution.py
@@ -4,7 +4,7 @@
 import jax
 import jax.numpy as jnp
 from jax import lax
-from jax.sharding import PartitionSpec as P
+from jax.sharding import Mesh, PartitionSpec as P
 
 FDIM = 16
 VDIM = 128
@@ -14,8 +14,11 @@
 HIGH = lax.Precision.HIGHEST
 
 
+CTX = ("cx", "cz", "cc")
+
+
 def passed_along(shard, axis, by):
-    length = lax.axis_size(axis)
+    length = math.prod(lax.axis_size(a) for a in axis)
     pairs = [(i, i + by) for i in range(length) if 0 <= i + by < length]
     return lax.ppermute(shard, axis, pairs)
 
@@ -49,14 +52,24 @@
     return jnp.einsum("cf,hft->hct", fold, full, precision=HIGH)
 
 
-def exclusive_prefix(flat, axis):
-    size = lax.axis_size(axis)
-    chunks = flat.reshape(size, -1)
-    recv = lax.all_to_all(chunks, axis, 0, 0, tiled=True)
-    lower = jnp.asarray(np.tril(np.ones((size, size), np.float32), -1))
-    pref = jnp.dot(lower, recv, precision=HIGH, preferred_element_type=jnp.float32)
-    back = lax.all_to_all(pref, axis, 0, 0, tiled=True)
-    return back.reshape(-1)
+def masked_rows(rows, upto):
+    keep = jnp.arange(rows.shape[0], dtype=jnp.int32)[:, None] < upto
+    return jnp.sum(jnp.where(keep, rows, jnp.float32(0.0)), axis=0)
+
+
+def exclusive_prefix(flat):
+    cores = lax.axis_size("cc")
+    core = lax.axis_index("cc")
+    pair = lax.all_gather(flat, "cc")
+    below_core = masked_rows(pair, core)
+    chip = jnp.sum(pair, axis=0)
+    share = lax.dynamic_index_in_dim(chip.reshape(cores, -1), core, 0, False)
+    along_z = lax.all_gather(share, "cz")
+    below_z = masked_rows(along_z, lax.axis_index("cz"))
+    along_x = lax.all_gather(jnp.sum(along_z, axis=0), "cx")
+    below_x = masked_rows(along_x, lax.axis_index("cx"))
+    shares = lax.all_gather(below_x + below_z, "cc")
+    return shares.reshape(-1) + below_core
 
 
 def window_slab(query, key_ext, value_ext, start):
@@ -133,18 +146,18 @@
     feat = phi_k.shape[1]
     local_state = jnp.einsum("hft,thv->hfv", phi_k, values32, precision=HIGH)
     local_norm = jnp.sum(phi_k, axis=-1)
-    size = lax.axis_size("ctx")
+    size = lax.axis_size("cc") * 128
     packed = jnp.concatenate([local_state.reshape(-1), local_norm.reshape(-1)])
     used = packed.shape[0]
     quantum = size * 128
     padded = -(-used // quantum) * quantum
     packed = jnp.pad(packed, (0, padded - used))
-    prior = exclusive_prefix(packed, "ctx")
+    prior = exclusive_prefix(packed)
     split = heads * feat * VDIM
     prior_state = prior[:split].reshape(heads, feat, VDIM)
     prior_norm = prior[split:used].reshape(heads, feat)
-    start = lax.axis_index("ctx") * count
-    rims = passed_along((win_key[count - WIN :], win_value[count - WIN :]), "ctx", 1)
+    start = lax.axis_index(CTX) * count
+    rims = passed_along((win_key[count - WIN :], win_value[count - WIN :]), CTX, 1)
     key_ext = jnp.concatenate([rims[0], win_key], axis=0)
     value_ext = jnp.concatenate([rims[1], win_value], axis=0)
     window_out = window_slab(win_query, key_ext, value_ext, start)
@@ -163,17 +176,27 @@
     return (mixed * lax.rsqrt(msq + 1e-06)[:, None]).astype(jnp.bfloat16)
 
 
+def split_ctx(mesh):
+    column = mesh.devices[:, 0]
+    xs = len({d.coords[0] for d in column})
+    cores = len({d.core_on_chip for d in column})
+    zs = column.shape[0] // (xs * cores)
+    grid = mesh.devices.reshape(xs, zs, cores, mesh.devices.shape[1])
+    return Mesh(grid, ("cx", "cz", "cc", "head"))
+
+
 def solution(mesh):
+    mesh = split_ctx(mesh)
     placed = (
-        P("ctx", "head"),
-        P("ctx", "head"),
-        P("ctx", "head"),
-        P("ctx", "head"),
-        P("ctx", "head"),
-        P("ctx", "head"),
+        P(CTX, "head"),
+        P(CTX, "head"),
+        P(CTX, "head"),
+        P(CTX, "head"),
+        P(CTX, "head"),
+        P(CTX, "head"),
         P(None, "head"),
         P("head"),
     )
     return jax.shard_map(
-        body, mesh=mesh, in_specs=placed, out_specs=P("ctx", "head"), check_vma=False
-    )
+        body, mesh=mesh, in_specs=placed, out_specs=P(CTX, "head"), check_vma=False
+    )

time: 103 us -> 150 us (1.46)
  the two profiles are of different devices: /device:TPU:8 before, /device:TPU:6 now
where the time goes in v3:
time: 150 us; the launch traced here: 148 us
  waiting for transfers between devices  68.7 us (46%)
  blocking collectives  19.1 us (13%)
  other arithmetic  15.4 us (10%)
  starting transfers between devices  14.3 us (10%)
  between operations  13.9 us (9%)
  matrix products  8.36 us (6%)
  local copies, waits for them, and re-layouts  8.03 us (5%)
    all_gather x1, waiting for transfers between devices, exclusive_prefix(): along_z = lax.all_gather(share, 'cz')  61.1 us
    all_gather x1, blocking collectives, exclusive_prefix(): along_x = lax.all_gather(jnp.sum(along_z, axis=0), 'cx')  14.5 us
    ppermute x2, starting transfers between devices, head_sum(): total = total + lax.ppermute(total, axis, pairs)  8.3 us
    reduce_sum x3, other arithmetic, masked_rows(): return jnp.sum(jnp.where(keep, rows, jnp.float32(0.0)), axis=0)  6.18 us
    ppermute x2, starting transfers between devices, passed_along(): return lax.ppermute(shard, axis, pairs)  6.03 us
    reduce_sum x1, other arithmetic, exclusive_prefix(): along_x = lax.all_gather(jnp.sum(along_z, axis=0), 'cx')  4.6 us
    ppermute x2, waiting for transfers between devices, head_sum(): total = total + lax.ppermute(total, axis, pairs)  4.1 us
    dot_general x2, matrix products, compact_features(): return jnp.einsum('cf,hft->hct', fold, full, precision=HIGH)  3.95 us
  transfers between devices with their start and end apart: 5, of which 4 were waited for; matrix products, arithmetic and copies ran while one was open for 6% of the time, Pallas kernels for 0%

profile of v3, /device:TPU:6, one launch (start us, length us, event | category | flops | bytes accessed | tf_op | source)
XLA Modules:
  0.0 147.8 jit_solution(13863586936270479396)
XLA Ops:
  6.5 0.8 convert_bitcast_fusion
  7.4 0.8 broadcast_multiply_fusion
  8.1 0.1 multiply_multiply_fusion
  8.3 1.6 %fusion.60 = (f32[4,153]{1,0:T(4,128)S(1)}, f32[4,256,153]{1,2,0:T(8,128)S(1)}) fusion(f32[153,273,1]{1,0,2:T(8,128)S(1)} %copy-done.11, f32[4,256,256]{2,1,0:T(8,128)S(1)} %bitcast.77, f32[4,16,256]{2,1,0:T(8,128)S(1)} %broadcast_multiply_fusion, f32[273]{0:T(512)S(1)} %pad.16.clone), kind=kOutput, calls=%fused_computation.92 | convolution fusion | flops 513972640 | bytes 1911416 | tf_op jit(solution)/shard_map/cf,hft->hct/dot_general | solution.py:52
  9.9 0.4 fusion.35
  10.4 0.1 reshape.184
  10.5 2.4 %all-gather = f32[196608]{0:T(1024)S(1)} all-gather(f32[98304]{0:T(1024)S(1)} %select_maximum_fusion), channel_id=2, replica_groups=mesh['cx'=4,'cz'=16,'cc'=2,'head'=4] {'cc'}, dimensions={0}, use_global_device_ids=true | all-gather | bytes 1179648 | tf_op jit(solution)/shard_map/all_gather | solution.py:63
  12.9 0.5 reshape.196
  13.4 2.1 %select_reduce_fusion = (f32[98304]{0:T(1024)}, f32[98304]{0:T(1024)S(1)}) fusion(f32[2,98304]{1,0:T(2,128)S(1)} %reshape.196, pred[2]{0:T(512)(128)(4,1)S(1)} %iota_compare_fusion.4), kind=kLoop, calls=%fused_computation.26 | loop fusion | flops 393216 | bytes 1572866 | tf_op jit(solution)/shard_map/reduce_sum | solution.py:57
  15.5 0.2 reshape.185
  15.8 0.9 dynamic-slice_bitcast_fusion
  16.7 2.0 %collective-permute-start.1 = (bf16[64,512]{1,0:T(8,128)(2,1)S(1)}, bf16[64,512]{1,0:T(8,128)(2,1)S(1)}, u32[]{:S(2)}, u32[]{:S(2)}) collective-permute-start(bf16[64,512]{1,0:T(8,128)(2,1)S(1)} %slice.40), channel_id=1, source_target_pairs={{0,4},{4,8},{8,12},{12,16},{16,20},{20,24},{24,28},{28,32},{32,36}... | collective-permute-start | bytes 196616 | tf_op jit(solution)/shard_map/ppermute | solution.py:23
  18.8 4.0 %collective-permute-start = (bf16[64,512]{1,0:T(8,128)(2,1)S(1)}, bf16[64,512]{1,0:T(8,128)(2,1)S(1)}, u32[]{:S(2)}, u32[]{:S(2)}) collective-permute-start(bf16[64,512]{1,0:T(8,128)(2,1)S(1)} %slice.38), channel_id=1, source_target_pairs={{0,4},{4,8},{8,12},{12,16},{16,20},{20,24},{24,28},{28,32},{32,36}... | collective-permute-start | bytes 196616 | tf_op jit(solution)/shard_map/ppermute | solution.py:23
  22.8 0.1 reshape.193
  22.9 0.1 reshape.191
  23.0 0.1 reshape.194
  23.2 0.1 add_compare_fusion
  23.3 0.1 fusion.47
  23.4 0.1 copy-done.14
  23.7 0.5 fusion.61
  24.2 0.1 multiply_multiply_fusion.1
  24.3 0.8 copy-done.10
  25.1 2.3 %fusion.9 = f32[4,256,153]{1,2,0:T(8,128)} fusion(f32[153,273,1]{1,0,2:T(8,128)S(1)} %copy-done.10, f32[4,256,256]{2,1,0:T(8,128)S(1)} %bitcast.78, f32[4,16,256]{2,1,0:T(8,128)S(1)} %broadcast_multiply_fusion.1, f32[273]{0:T(512)S(1)} %pad.16.clone), kind=kOutput, calls=%fused_computation.13 | convolution fusion | flops 513816576 | bytes 1908968 | tf_op jit(solution)/shard_map/cf,hft->hct/dot_general | solution.py:52
  27.4 1.1 fusion.32
  28.5 3.5 %collective-permute-done = bf16[64,512]{1,0:T(8,128)(2,1)S(1)} collective-permute-done((bf16[64,512]{1,0:T(8,128)(2,1)S(1)}, bf16[64,512]{1,0:T(8,128)(2,1)S(1)}, u32[]{:S(2)}, u32[]{:S(2)}) %collective-permute-start) | collective-permute-done | bytes 65568 | tf_op jit(solution)/shard_map/ppermute | solution.py:23
  32.1 0.9 convert_element_type.23
  33.3 0.5 fusion.8
  33.7 0.4 fusion.62
  34.1 0.4 fusion.7
  34.5 1.1 copy.44
  35.6 61.1 %all-gather.6.cloned.1.call-done = f32[16,1,49152]{2,1,0:T(1,128)} async-done(((f32[1,1,49152]{2,1,0:T(1,128)}), f32[16,1,49152]{2,1,0:T(1,128)}) %all-gather.6.cloned.1.call-update) | async-done | bytes 3145744 | tf_op jit(solution)/shard_map/all_gather | solution.py:67
  96.7 4.6 %reduce_sum.83 = f32[49152]{0:T(1024)} reduce(f32[16,1,49152]{2,1,0:T(1,128)} %all-gather.6.cloned.1.call-done, f32[]{:T(128)} %constant.27.clone.1), dimensions={0,1}, to_apply=%region_2.3 | reduce | flops 737280 | bytes 3342340 | tf_op jit(solution)/shard_map/reduce_sum | solution.py:69
  101.3 14.5 %all-gather.1 = f32[196608]{0:T(1024)} all-gather(f32[49152]{0:T(1024)} %reduce_sum.83), channel_id=3, replica_groups=mesh['cx'=4,'cz'=16,'cc'=2,'head'=4] {'cx'}, dimensions={0}, use_global_device_ids=true | all-gather | bytes 983040 | tf_op jit(solution)/shard_map/all_gather | solution.py:69
  115.8 2.4 %reshape.197 = f32[4,49152]{1,0:T(4,128)} reshape(f32[196608]{0:T(1024)} %all-gather.1) | data formatting | bytes 1572864 | tf_op jit(solution)/shard_map/all_gather | solution.py:69
  118.2 1.7 %select_reduce_fusion.1 = f32[49152]{0:T(1024)S(1)} fusion(f32[4,49152]{1,0:T(4,128)} %reshape.197, pred[4]{0:T(512)(128)(4,1)S(1)} %iota_compare_fusion.6), kind=kLoop, calls=%fused_computation.27 | loop fusion | flops 344064 | bytes 983044 | tf_op jit(solution)/shard_map/reduce_sum | solution.py:57
  119.9 2.3 %fusion.1 = f32[49152]{0:T(1024)S(1)} fusion(f32[16,1,49152]{2,1,0:T(1,128)S(1)} %copy-done.1, pred[16]{0:T(512)(128)(4,1)S(1)} %iota_compare_fusion.5), kind=kLoop, calls=%fused_computation.2 | loop fusion | flops 1523712 | bytes 3342352 | tf_op jit(solution)/shard_map/reduce_sum | solution.py:57
  122.3 2.2 %all-gather.2 = f32[98304]{0:T(1024)S(1)} all-gather(f32[49152]{0:T(1024)S(1)} %add.125), channel_id=4, replica_groups=mesh['cx'=4,'cz'=16,'cc'=2,'head'=4] {'cc'}, dimensions={0}, use_global_device_ids=true | all-gather | bytes 589824 | tf_op jit(solution)/shard_map/all_gather | solution.py:71
  124.6 0.1 reshape.207
  124.7 0.9 copy-done.3
  125.6 0.5 fusion.63
  126.1 1.1 fusion.3
  127.2 0.2 copy.45
  127.4 0.3 multiply_reduce_fusion
  127.7 3.4 %collective-permute-start.2 = (f32[256]{0:T(256)S(1)}, f32[256]{0:T(256)S(1)}, u32[]{:S(2)}, u32[]{:S(2)}) collective-permute-start(f32[256]{0:T(256)S(1)} %get-tuple-element.7), channel_id=1, source_target_pairs={{0,1},{1,0},{2,3},{3,2},{4,5},{5,4},{6,7},{7,6},{8,9},{9,8},{10,11... | collective-permute-start | bytes 3080 | tf_op jit(solution)/shard_map/ppermute | solution.py:132
  131.1 2.1 %collective-permute-done.2 = f32[256]{0:T(256)S(1)} collective-permute-done((f32[256]{0:T(256)S(1)}, f32[256]{0:T(256)S(1)}, u32[]{:S(2)}, u32[]{:S(2)}) %collective-permute-start.2) | collective-permute-done | bytes 1056 | tf_op jit(solution)/shard_map/ppermute | solution.py:132
  133.2 4.9 %collective-permute-start.3 = (f32[256]{0:T(256)S(1)}, f32[256]{0:T(256)S(1)}, u32[]{:S(2)}, u32[]{:S(2)}) collective-permute-start(f32[256]{0:T(256)S(1)} %add.145), channel_id=1, source_target_pairs={{0,2},{1,3},{2,0},{3,1},{4,6},{5,7},{6,4},{7,5},{8,10},{9,11},{10,... | collective-permute-start | bytes 3080 | tf_op jit(solution)/shard_map/ppermute | solution.py:132
  138.1 2.0 %collective-permute-done.3 = f32[256]{0:T(256)S(1)} collective-permute-done((f32[256]{0:T(256)S(1)}, f32[256]{0:T(256)S(1)}, u32[]{:S(2)}, u32[]{:S(2)}) %collective-permute-start.3) | collective-permute-done | bytes 1056 | tf_op jit(solution)/shard_map/ppermute | solution.py:132
  140.2 0.8 multiply_convert_fusion
  (65 shorter events, 0.8 us)
Async XLA Ops:
  6.5 3.4 %copy-start = (bf16[256,512]{1,0:T(8,128)(2,1)S(1)}, bf16[256,512]{1,0:T(8,128)(2,1)}, u32[]{:S(2)}) copy-start(bf16[256,512]{1,0:T(8,128)(2,1)} %param.12) | copy-start | bytes 786436
  6.5 1.8 %copy-start.11 = (f32[153,273,1]{1,0,2:T(8,128)S(1)}, f32[153,273,1]{1,0,2:T(8,128)}, u32[]{:S(2)}) copy-start(f32[153,273,1]{1,0,2:T(8,128)} %constant.70) | copy-start | bytes 501232
  6.5 90.1 %all-gather.6.cloned.1.call-start = ((), (), s32[]{:S(2)}) async-start(), calls=%async_computation | async-start | bytes 3342336 | tf_op jit(solution)/shard_map/all_gather | solution.py:67
  13.4 3.3 %copy-start.7 = (bf16[256,512]{1,0:T(8,128)(2,1)S(1)}, bf16[256,512]{1,0:T(8,128)(2,1)}, u32[]{:S(2)}) copy-start(bf16[256,512]{1,0:T(8,128)(2,1)} %param.14) | copy-start | bytes 786436
  15.5 3.2 %copy-start.6 = (bf16[256,512]{1,0:T(8,128)(2,1)S(1)}, bf16[256,512]{1,0:T(8,128)(2,1)}, u32[]{:S(2)}) copy-start(bf16[256,512]{1,0:T(8,128)(2,1)} %param.15) | copy-start | bytes 786436
  15.8 7.2 %copy-start.9 = (bf16[256,512]{1,0:T(8,128)(2,1)S(1)}, bf16[256,512]{1,0:T(8,128)(2,1)}, u32[]{:S(2)}) copy-start(bf16[256,512]{1,0:T(8,128)(2,1)} %param.13) | copy-start | bytes 786436
  16.7 16.3 %collective-permute-start.1 = (bf16[64,512]{1,0:T(8,128)(2,1)S(1)}, bf16[64,512]{1,0:T(8,128)(2,1)S(1)}, u32[]{:S(2)}, u32[]{:S(2)}) collective-permute-start(bf16[64,512]{1,0:T(8,128)(2,1)S(1)} %slice.40), channel_id=1, source_target_pairs={{0,4},{4,8},{8,12},{12,16},{16,20},{20,24},{24,28},{28,32},{32,36}... | collective-permute-start | bytes 196616 | tf_op jit(solution)/shard_map/ppermute | solution.py:23
  18.8 13.2 %collective-permute-start = (bf16[64,512]{1,0:T(8,128)(2,1)S(1)}, bf16[64,512]{1,0:T(8,128)(2,1)S(1)}, u32[]{:S(2)}, u32[]{:S(2)}) collective-permute-start(bf16[64,512]{1,0:T(8,128)(2,1)S(1)} %slice.38), channel_id=1, source_target_pairs={{0,4},{4,8},{8,12},{12,16},{16,20},{20,24},{24,28},{28,32},{32,36}... | collective-permute-start | bytes 196616 | tf_op jit(solution)/shard_map/ppermute | solution.py:23
  22.8 0.7 copy-start.14
  22.9 0.8 copy-start.12
  22.9 0.8 copy-start.13
  24.2 0.9 copy-start.10
  101.3 18.6 %copy-start.1 = (f32[16,1,49152]{2,1,0:T(1,128)S(1)}, f32[16,1,49152]{2,1,0:T(1,128)}, u32[]{:S(2)}) copy-start(f32[16,1,49152]{2,1,0:T(1,128)} %all-gather.6.cloned.1.call-done) | copy-start | bytes 9437188
  122.2 2.3 %copy-start.5 = (f32[98304]{0:T(1024)S(1)}, f32[98304]{0:T(1024)}, u32[]{:S(2)}) copy-start(f32[98304]{0:T(1024)} %get-tuple-element.5) | copy-start | bytes 1179652
  124.5 1.1 copy-start.3
  124.5 1.5 %copy-start.8 = (f32[4,256,128]{1,2,0:T(8,128)S(1)}, f32[4,256,128]{1,2,0:T(8,128)}, u32[]{:S(2)}) copy-start(f32[4,256,128]{1,2,0:T(8,128)} %fusion.32) | copy-start | bytes 1572868
  126.1 1.3 copy-start.2
  126.1 1.3 copy-start.4
  126.1 1.3 copy-start.15
  127.7 5.5 %collective-permute-start.2 = (f32[256]{0:T(256)S(1)}, f32[256]{0:T(256)S(1)}, u32[]{:S(2)}, u32[]{:S(2)}) collective-permute-start(f32[256]{0:T(256)S(1)} %get-tuple-element.7), channel_id=1, source_target_pairs={{0,1},{1,0},{2,3},{3,2},{4,5},{5,4},{6,7},{7,6},{8,9},{9,8},{10,11... | collective-permute-start | bytes 3080 | tf_op jit(solution)/shard_map/ppermute | solution.py:132
  133.2 7.0 %collective-permute-start.3 = (f32[256]{0:T(256)S(1)}, f32[256]{0:T(256)S(1)}, u32[]{:S(2)}, u32[]{:S(2)}) collective-permute-start(f32[256]{0:T(256)S(1)} %add.145), channel_id=1, source_target_pairs={{0,2},{1,3},{2,0},{3,1},{4,6},{5,7},{6,4},{7,5},{8,10},{9,11},{10,... | collective-permute-start | bytes 3080 | tf_op jit(solution)/shard_map/ppermute | solution.py:132
Sparse Core Ops, SparseCore 0:
  16.8 79.8 all-gather.5

commit v4 on v3

--- a/solution.py
+++ b/solution.py
@@ -60,15 +60,16 @@
 def exclusive_prefix(flat):
     cores = lax.axis_size("cc")
     core = lax.axis_index("cc")
+    chips = lax.axis_size("cx") * lax.axis_size("cz")
     pair = lax.all_gather(flat, "cc")
     below_core = masked_rows(pair, core)
     chip = jnp.sum(pair, axis=0)
     share = lax.dynamic_index_in_dim(chip.reshape(cores, -1), core, 0, False)
-    along_z = lax.all_gather(share, "cz")
-    below_z = masked_rows(along_z, lax.axis_index("cz"))
-    along_x = lax.all_gather(jnp.sum(along_z, axis=0), "cx")
-    below_x = masked_rows(along_x, lax.axis_index("cx"))
-    shares = lax.all_gather(below_x + below_z, "cc")
+    recv = lax.all_to_all(share.reshape(chips, -1), ("cx", "cz"), 0, 0, tiled=True)
+    lower = jnp.asarray(np.tril(np.ones((chips, chips), np.float32), -1))
+    pref = jnp.dot(lower, recv, precision=HIGH, preferred_element_type=jnp.float32)
+    back = lax.all_to_all(pref, ("cx", "cz"), 0, 0, tiled=True)
+    shares = lax.all_gather(back.reshape(-1), "cc")
     return shares.reshape(-1) + below_core
 
 
@@ -146,7 +147,7 @@
     feat = phi_k.shape[1]
     local_state = jnp.einsum("hft,thv->hfv", phi_k, values32, precision=HIGH)
     local_norm = jnp.sum(phi_k, axis=-1)
-    size = lax.axis_size("cc") * 128
+    size = lax.axis_size("cc") * lax.axis_size("cx") * lax.axis_size("cz")
     packed = jnp.concatenate([local_state.reshape(-1), local_norm.reshape(-1)])
     used = packed.shape[0]
     quantum = size * 128

time: 150 us -> 92.5 us (0.62); the launches traced: 148 us -> 91.9 us
  waiting for transfers between devices: 68.7 us -> 20.9 us
  starting transfers between devices: 14.3 us -> 40.9 us
  blocking collectives: 19.1 us -> 4.3 us
  between operations: 13.9 us -> 0.51 us
  other arithmetic: 15.4 us -> 5.49 us
  matrix products: 8.36 us -> 10.9 us
    all_gather x1 -> x0, waiting for transfers between devices: 61.1 us -> none  [exclusive_prefix(): along_z = lax.all_gather(share, 'cz')]
    all_to_all x0 -> x2, starting transfers between devices: none -> 26.9 us  [the longest x1 18.9 us: exclusive_prefix(): lax.all_to_all(share.reshape(chips, -1), ('cx', 'cz'), 0, 0, tiled=True)]
    all_to_all x0 -> x2, waiting for transfers between devices: none -> 17 us  [the longest x1 10.8 us: exclusive_prefix(): back = lax.all_to_all(pref, ('cx', 'cz'), 0, 0, tiled=True)]
    all_gather x2 -> x1, blocking collectives: 16.7 us -> 2.03 us  [exclusive_prefix(): shares = lax.all_gather(back.reshape(-1), 'cc')]
    reduce_sum x1 -> x0, other arithmetic: 4.6 us -> none  [exclusive_prefix(): along_x = lax.all_gather(jnp.sum(along_z, axis=0), 'cx')]
    reduce_sum x3 -> x1, other arithmetic: 6.18 us -> 1.73 us  [masked_rows(): return jnp.sum(jnp.where(keep, rows, jnp.float32(0.0)), axis=0)]
    ppermute x2, waiting for transfers between devices: 3.49 us -> 0.01 us  [passed_along(): return lax.ppermute(shard, axis, pairs)]
    all_gather x1 -> x0, local copies, waits for them, and re-layouts: 2.37 us -> none  [exclusive_prefix(): along_x = lax.all_gather(jnp.sum(along_z, axis=0), 'cx')]
  transfers between devices with their start and end apart: 5 -> 6, of which waited for: 4 -> 4; matrix products, arithmetic and copies ran while one was open for 6% -> 13% of each run, Pallas kernels for 0% -> 0%
where the time goes in v4:
time: 92.5 us; the launch traced here: 91.9 us
  starting transfers between devices  40.9 us (44%)
  waiting for transfers between devices  20.9 us (23%)
  matrix products  10.9 us (12%)
  local copies, waits for them, and re-layouts  8.84 us (10%)
  other arithmetic  5.49 us (6%)
  blocking collectives  4.3 us (5%)
    all_to_all x1, starting transfers between devices, exclusive_prefix(): lax.all_to_all(share.reshape(chips, -1), ('cx', 'cz'), 0, 0, tiled=True)  18.9 us
    all_to_all x1, waiting for transfers between devices, exclusive_prefix(): back = lax.all_to_all(pref, ('cx', 'cz'), 0, 0, tiled=True)  10.8 us
    ppermute x2, starting transfers between devices, head_sum(): total = total + lax.ppermute(total, axis, pairs)  8.58 us
    all_to_all x1, starting transfers between devices, exclusive_prefix(): back = lax.all_to_all(pref, ('cx', 'cz'), 0, 0, tiled=True)  8.03 us
    all_to_all x1, waiting for transfers between devices, exclusive_prefix(): lax.all_to_all(share.reshape(chips, -1), ('cx', 'cz'), 0, 0, tiled=True)  6.22 us
    ppermute x2, starting transfers between devices, passed_along(): return lax.ppermute(shard, axis, pairs)  5.39 us
    ppermute x2, waiting for transfers between devices, head_sum(): total = total + lax.ppermute(total, axis, pairs)  3.83 us
    dot_general x2, matrix products, compact_features(): return jnp.einsum('cf,hft->hct', fold, full, precision=HIGH)  3.08 us
  transfers between devices with their start and end apart: 6, of which 4 were waited for; matrix products, arithmetic and copies ran while one was open for 13% of the time, Pallas kernels for 0%

profile of v4, /device:TPU:6, one launch (start us, length us, event | category | flops | bytes accessed | tf_op | source)
XLA Modules:
  0.0 91.9 jit_solution(10829855906075680623)
XLA Ops:
  0.0 0.8 convert_bitcast_fusion
  0.8 0.8 broadcast_multiply_fusion
  1.6 0.1 multiply_multiply_fusion
  1.8 1.6 %fusion.61 = (f32[4,153]{1,0:T(4,128)S(1)}, f32[4,256,153]{1,2,0:T(8,128)S(1)}) fusion(f32[153,273,1]{1,0,2:T(8,128)S(1)} %copy-done.8, f32[4,256,256]{2,1,0:T(8,128)S(1)} %bitcast.81, f32[4,16,256]{2,1,0:T(8,128)S(1)} %broadcast_multiply_fusion, f32[273]{0:T(512)S(1)} %pad.16.clone), kind=kOutput, calls=%fused_computation.90 | convolution fusion | flops 513972640 | bytes 1911416 | tf_op jit(solution)/shard_map/cf,hft->hct/dot_general | solution.py:52
  3.4 0.4 fusion.34
  3.9 0.1 reshape.170
  4.0 2.3 %all-gather = f32[163840]{0:T(1024)S(1)} all-gather(f32[81920]{0:T(1024)S(1)} %select_maximum_fusion), channel_id=2, replica_groups=mesh['cx'=4,'cz'=16,'cc'=2,'head'=4] {'cc'}, dimensions={0}, use_global_device_ids=true | all-gather | bytes 983040 | tf_op jit(solution)/shard_map/all_gather | solution.py:64
  6.3 0.4 reshape.182
  6.7 1.7 %select_reduce_fusion.1 = (f32[81920]{0:T(1024)S(1)}, f32[81920]{0:T(1024)S(1)}) fusion(f32[2,81920]{1,0:T(2,128)S(1)} %reshape.182, pred[2]{0:T(512)(128)(4,1)S(1)} %iota_compare_fusion.4), kind=kLoop, calls=%fused_computation.27 | loop fusion | flops 327680 | bytes 1310722 | tf_op jit(solution)/shard_map/reduce_sum | solution.py:57
  8.5 0.2 reshape.171
  8.7 0.8 constant_dynamic-slice_fusion
  9.5 18.9 %all-to-all-start = ((f32[64,1,640]{2,1,0:T(1,128)}), f32[64,1,640]{2,1,0:T(1,128)S(1)}, u32[]{:S(2)}, u32[]{:S(2)}) async-start(f32[64,1,640]{2,1,0:T(1,128)} %bitcast.8), calls=%async_computation | async-start | bytes 327680 | tf_op jit(solution)/shard_map/all_to_all | solution.py:68
  28.4 1.9 %collective-permute-start.1 = (bf16[64,512]{1,0:T(8,128)(2,1)S(1)}, bf16[64,512]{1,0:T(8,128)(2,1)S(1)}, u32[]{:S(2)}, u32[]{:S(2)}) collective-permute-start(bf16[64,512]{1,0:T(8,128)(2,1)S(1)} %slice.40), channel_id=1, source_target_pairs={{0,4},{4,8},{8,12},{12,16},{16,20},{20,24},{24,28},{28,32},{32,36}... | collective-permute-start | bytes 196616 | tf_op jit(solution)/shard_map/ppermute | solution.py:23
  30.4 0.6 slice.38
  31.0 3.5 %collective-permute-start = (bf16[64,512]{1,0:T(8,128)(2,1)}, bf16[64,512]{1,0:T(8,128)(2,1)S(1)}, u32[]{:S(2)}, u32[]{:S(2)}) collective-permute-start(bf16[64,512]{1,0:T(8,128)(2,1)} %slice.38), channel_id=1, source_target_pairs={{0,4},{4,8},{8,12},{12,16},{16,20},{20,24},{24,28},{28,32},{32,36}... | collective-permute-start | bytes 196616 | tf_op jit(solution)/shard_map/ppermute | solution.py:23
  34.6 0.1 multiply_multiply_fusion.1
  34.7 0.5 fusion.62
  35.2 1.1 %fusion.31 = f32[4,256,128]{1,2,0:T(8,128)} fusion(bf16[4,256,256]{1,2,0:T(8,128)(2,1)S(1)} %get-tuple-element.15, bf16[256,512]{1,0:T(8,128)(2,1)S(1)} %copy-done), kind=kOutput, calls=%fused_computation.46 | convolution fusion | flops 67108864 | bytes 1310720 | tf_op jit(solution)/shard_map/hts,shv->htv/dot_general | solution.py:121
  36.3 0.1 add_compare_fusion
  36.4 0.1 fusion.48
  36.5 1.5 %fusion.8 = f32[4,256,153]{1,2,0:T(8,128)S(1)} fusion(f32[153,273,1]{1,0,2:T(8,128)S(1)} %copy-done.7, f32[4,256,256]{2,1,0:T(8,128)S(1)} %bitcast.80, f32[4,16,256]{2,1,0:T(8,128)S(1)} %broadcast_multiply_fusion.1, f32[273]{0:T(512)S(1)} %pad.16.clone), kind=kOutput, calls=%fused_computation.11 | convolution fusion | flops 513816576 | bytes 1908968 | tf_op jit(solution)/shard_map/cf,hft->hct/dot_general | solution.py:52
  38.2 0.8 copy.45
  38.9 0.8 reshape.180
  39.8 6.2 %all-to-all-done = f32[64,1,640]{2,1,0:T(1,128)S(1)} async-done(((f32[64,1,640]{2,1,0:T(1,128)}), f32[64,1,640]{2,1,0:T(1,128)S(1)}, u32[]{:S(2)}, u32[]{:S(2)}) %all-to-all-start) | async-done | bytes 163872 | tf_op jit(solution)/shard_map/all_to_all | solution.py:68
  46.0 0.3 convolution_bitcast_fusion.1
  46.3 0.8 copy.41
  47.1 8.0 %all-to-all-start.1 = ((f32[64,1,640]{2,1,0:T(1,128)}), f32[64,1,640]{2,1,0:T(1,128)S(1)}, u32[]{:S(2)}, u32[]{:S(2)}) async-start(f32[64,1,640]{2,1,0:T(1,128)} %copy.41), calls=%async_computation.1 | async-start | bytes 327680 | tf_op jit(solution)/shard_map/all_to_all | solution.py:71
  55.4 0.8 copy.44
  56.3 0.8 copy-done.6
  57.1 1.4 %fusion.7 = f32[4,4,64,128]{3,2,1,0:T(8,128)S(1)} fusion(bf16[4,64,4,128]{3,1,2,0:T(8,128)(2,1)S(1)} %copy-done.5, bf16[4,64,4,128]{3,1,2,0:T(8,128)(2,1)} %copy.44, bf16[4,64,4,128]{3,2,1,0:T(4,128)(2,1)S(1)} %copy-done.6), kind=kOutput, calls=%fused_computation.10 | convolution fusion | flops 34734080 | bytes 1310720 | tf_op jit(solution)/shard_map/bihe,bjhe->bhij/dot_general | solution.py:95
  58.5 0.4 fusion.63
  58.9 0.4 copy-done.14
  59.3 1.6 %fusion.6 = f32[4,64,4,128]{3,1,2,0:T(8,128)S(1)} fusion(bf16[4,64,4,128]{3,1,2,0:T(8,128)(2,1)S(1)} %copy.43, bf16[4,64,4,128]{3,1,2,0:T(8,128)(2,1)S(1)} %copy.42, f32[4,64,4]{1,2,0:T(4,128)S(1)} %bitcast.91, f32[4,4,64,128]{3,2,1,0:T(8,128)} %copy-done.14, pred[4,64,128]{2,1,0:T(8,128)(4,1)S(1)} %broadcast_and_fusion), kind=kOutput, calls=%fused_computation.8 | convolution fusion | flops 35259520 | bytes 1609728 | tf_op jit(solution)/shard_map/bhij,bjhe->bihe/dot_general | solution.py:107
  60.9 0.3 copy.47
  61.3 10.8 %all-to-all-done.1 = f32[64,1,640]{2,1,0:T(1,128)S(1)} async-done(((f32[64,1,640]{2,1,0:T(1,128)}), f32[64,1,640]{2,1,0:T(1,128)S(1)}, u32[]{:S(2)}, u32[]{:S(2)}) %all-to-all-start.1) | async-done | bytes 163872 | tf_op jit(solution)/shard_map/all_to_all | solution.py:71
  72.1 2.0 %all-gather.1 = f32[2,1,40960]{2,1,0:T(1,128)S(1)} all-gather(f32[1,1,40960]{2,1,0:T(1,128)S(1)} %bitcast.84), channel_id=1, replica_groups=mesh['cx'=4,'cz'=16,'cc'=2,'head'=4] {'cc'}, dimensions={0}, use_global_device_ids=true | all-gather | bytes 491520 | tf_op jit(solution)/shard_map/all_gather | solution.py:72
  74.2 0.1 reshape.192
  74.3 0.7 reshape.173
  75.1 0.5 fusion.64
  75.6 2.0 %fusion.2 = f32[256,4,128]{0,2,1:T(8,128)S(1)} fusion(f32[4,256,128]{1,2,0:T(8,128)S(1)} %copy-done.3, f32[4,256,153]{1,2,0:T(8,128)S(1)} %fusion.8, f32[4,153,128]{2,1,0:T(8,128)} %reshape.173, f32[256,4]{0,1:T(4,128)S(1)} %fusion.49), kind=kOutput, calls=%fused_computation.4 | convolution fusion | flops 240910336 | bytes 1992704 | tf_op jit(solution)/shard_map/hft,hfv->htv/dot_general | solution.py:171
  77.6 0.2 copy.48
  77.8 0.5 copy-done.13
  78.3 0.3 multiply_reduce_fusion
  78.6 3.5 %collective-permute-start.2 = (f32[256]{0:T(256)S(1)}, f32[256]{0:T(256)S(1)}, u32[]{:S(2)}, u32[]{:S(2)}) collective-permute-start(f32[256]{0:T(256)S(1)} %get-tuple-element.7), channel_id=1, source_target_pairs={{0,1},{1,0},{2,3},{3,2},{4,5},{5,4},{6,7},{7,6},{8,9},{9,8},{10,11... | collective-permute-start | bytes 3080 | tf_op jit(solution)/shard_map/ppermute | solution.py:133
  82.1 2.0 %collective-permute-done.2 = f32[256]{0:T(256)S(1)} collective-permute-done((f32[256]{0:T(256)S(1)}, f32[256]{0:T(256)S(1)}, u32[]{:S(2)}, u32[]{:S(2)}) %collective-permute-start.2) | collective-permute-done | bytes 1056 | tf_op jit(solution)/shard_map/ppermute | solution.py:133
  84.1 5.1 %collective-permute-start.3 = (f32[256]{0:T(256)S(1)}, f32[256]{0:T(256)S(1)}, u32[]{:S(2)}, u32[]{:S(2)}) collective-permute-start(f32[256]{0:T(256)S(1)} %add.130), channel_id=1, source_target_pairs={{0,2},{1,3},{2,0},{3,1},{4,6},{5,7},{6,4},{7,5},{8,10},{9,11},{10,... | collective-permute-start | bytes 3080 | tf_op jit(solution)/shard_map/ppermute | solution.py:133
  89.2 1.9 %collective-permute-done.3 = f32[256]{0:T(256)S(1)} collective-permute-done((f32[256]{0:T(256)S(1)}, f32[256]{0:T(256)S(1)}, u32[]{:S(2)}, u32[]{:S(2)}) %collective-permute-start.3) | collective-permute-done | bytes 1056 | tf_op jit(solution)/shard_map/ppermute | solution.py:133
  91.1 0.8 multiply_convert_fusion
  (58 shorter events, 0.8 us)
Async XLA Ops:
  0.0 3.4 %copy-start = (bf16[256,512]{1,0:T(8,128)(2,1)S(1)}, bf16[256,512]{1,0:T(8,128)(2,1)}, u32[]{:S(2)}) copy-start(bf16[256,512]{1,0:T(8,128)(2,1)} %param.13) | copy-start | bytes 786436
  0.0 1.8 %copy-start.8 = (f32[153,273,1]{1,0,2:T(8,128)S(1)}, f32[153,273,1]{1,0,2:T(8,128)}, u32[]{:S(2)}) copy-start(f32[153,273,1]{1,0,2:T(8,128)} %constant.73) | copy-start | bytes 501232
  6.7 21.7 %copy-start.2 = (bf16[256,512]{1,0:T(8,128)(2,1)S(1)}, bf16[256,512]{1,0:T(8,128)(2,1)}, u32[]{:S(2)}) copy-start(bf16[256,512]{1,0:T(8,128)(2,1)} %param.15) | copy-start | bytes 786436
  8.4 21.9 %copy-start.1 = (bf16[256,512]{1,0:T(8,128)(2,1)S(1)}, bf16[256,512]{1,0:T(8,128)(2,1)}, u32[]{:S(2)}) copy-start(bf16[256,512]{1,0:T(8,128)(2,1)} %param.16) | copy-start | bytes 786436
  8.4 26.0 %copy-start.9 = (bf16[256,64]{0,1:T(8,128)(2,1)S(1)}, bf16[256,64]{0,1:T(8,128)(2,1)}, u32[]{:S(2)}) copy-start(bf16[256,64]{0,1:T(8,128)(2,1)} %param.11) | copy-start | bytes 98308
  9.5 25.2 %copy-start.10 = (bf16[256,64]{0,1:T(8,128)(2,1)S(1)}, bf16[256,64]{0,1:T(8,128)(2,1)}, u32[]{:S(2)}) copy-start(bf16[256,64]{0,1:T(8,128)(2,1)} %param.12) | copy-start | bytes 98308
  9.5 36.5 %all-to-all-start = ((f32[64,1,640]{2,1,0:T(1,128)}), f32[64,1,640]{2,1,0:T(1,128)S(1)}, u32[]{:S(2)}, u32[]{:S(2)}) async-start(f32[64,1,640]{2,1,0:T(1,128)} %bitcast.8), calls=%async_computation | async-start | bytes 327680 | tf_op jit(solution)/shard_map/all_to_all | solution.py:68
  28.4 26.7 %collective-permute-start.1 = (bf16[64,512]{1,0:T(8,128)(2,1)S(1)}, bf16[64,512]{1,0:T(8,128)(2,1)S(1)}, u32[]{:S(2)}, u32[]{:S(2)}) collective-permute-start(bf16[64,512]{1,0:T(8,128)(2,1)S(1)} %slice.40), channel_id=1, source_target_pairs={{0,4},{4,8},{8,12},{12,16},{16,20},{20,24},{24,28},{28,32},{32,36}... | collective-permute-start | bytes 196616 | tf_op jit(solution)/shard_map/ppermute | solution.py:23
  31.0 8.7 %collective-permute-start = (bf16[64,512]{1,0:T(8,128)(2,1)}, bf16[64,512]{1,0:T(8,128)(2,1)S(1)}, u32[]{:S(2)}, u32[]{:S(2)}) collective-permute-start(bf16[64,512]{1,0:T(8,128)(2,1)} %slice.38), channel_id=1, source_target_pairs={{0,4},{4,8},{8,12},{12,16},{16,20},{20,24},{24,28},{28,32},{32,36}... | collective-permute-start | bytes 196616 | tf_op jit(solution)/shard_map/ppermute | solution.py:23
  35.2 1.3 %copy-start.7 = (f32[153,273,1]{1,0,2:T(8,128)S(1)}, f32[153,273,1]{1,0,2:T(8,128)}, u32[]{:S(2)}) copy-start(f32[153,273,1]{1,0,2:T(8,128)} %constant.72) | copy-start | bytes 501232
  36.3 1.7 %copy-start.12 = (bf16[3,512]{1,0:T(4,128)(2,1)S(1)}, bf16[3,512]{1,0:T(4,128)(2,1)}, u32[]{:S(2)}) copy-start(bf16[3,512]{1,0:T(4,128)(2,1)} %param.17) | copy-start | bytes 9220
  38.0 1.0 %copy-start.4 = (bf16[256,512]{1,0:T(8,128)(2,1)S(1)}, bf16[256,512]{1,0:T(8,128)(2,1)}, u32[]{:S(2)}) copy-start(bf16[256,512]{1,0:T(8,128)(2,1)} %param.14) | copy-start | bytes 786436
  38.2 7.9 %copy-start.11 = (f32[64,64]{1,0:T(8,128)S(1)}, f32[64,64]{1,0:T(8,128)}, u32[]{:S(2)}) copy-start(f32[64,64]{1,0:T(8,128)} %constant.69.clone) | copy-start | bytes 49156
  47.1 25.0 %all-to-all-start.1 = ((f32[64,1,640]{2,1,0:T(1,128)}), f32[64,1,640]{2,1,0:T(1,128)S(1)}, u32[]{:S(2)}, u32[]{:S(2)}) async-start(f32[64,1,640]{2,1,0:T(1,128)} %copy.41), calls=%async_computation.1 | async-start | bytes 327680 | tf_op jit(solution)/shard_map/all_to_all | solution.py:71
  55.3 1.0 %copy-start.5 = (bf16[4,64,4,128]{3,1,2,0:T(8,128)(2,1)S(1)}, bf16[4,64,4,128]{3,1,2,0:T(8,128)(2,1)}, u32[]{:S(2)}) copy-start(bf16[4,64,4,128]{3,1,2,0:T(8,128)(2,1)} %copy.45) | copy-start | bytes 786436
  56.2 1.0 %copy-start.6 = (bf16[4,64,4,128]{3,2,1,0:T(4,128)(2,1)S(1)}, bf16[4,64,4,128]{3,2,1,0:T(4,128)(2,1)}, u32[]{:S(2)}) copy-start(bf16[4,64,4,128]{3,2,1,0:T(4,128)(2,1)} %reshape.180) | copy-start | bytes 786436
  58.5 0.8 copy-start.14
  74.2 1.4 %copy-start.3 = (f32[4,256,128]{1,2,0:T(8,128)S(1)}, f32[4,256,128]{1,2,0:T(8,128)}, u32[]{:S(2)}) copy-start(f32[4,256,128]{1,2,0:T(8,128)} %fusion.31) | copy-start | bytes 1572868
  77.6 0.7 copy-start.13
  78.6 5.5 %collective-permute-start.2 = (f32[256]{0:T(256)S(1)}, f32[256]{0:T(256)S(1)}, u32[]{:S(2)}, u32[]{:S(2)}) collective-permute-start(f32[256]{0:T(256)S(1)} %get-tuple-element.7), channel_id=1, source_target_pairs={{0,1},{1,0},{2,3},{3,2},{4,5},{5,4},{6,7},{7,6},{8,9},{9,8},{10,11... | collective-permute-start | bytes 3080 | tf_op jit(solution)/shard_map/ppermute | solution.py:133
  84.1 7.0 %collective-permute-start.3 = (f32[256]{0:T(256)S(1)}, f32[256]{0:T(256)S(1)}, u32[]{:S(2)}, u32[]{:S(2)}) collective-permute-start(f32[256]{0:T(256)S(1)} %add.130), channel_id=1, source_target_pairs={{0,2},{1,3},{2,0},{3,1},{4,6},{5,7},{6,4},{7,5},{8,10},{9,11},{10,... | collective-permute-start | bytes 3080 | tf_op jit(solution)/shard_map/ppermute | solution.py:133

commit v5 on v4

--- a/solution.py
+++ b/solution.py
@@ -127,11 +127,9 @@
 def head_sum(part, axis):
     size = lax.axis_size(axis)
     total = part
-    step = 1
-    while step < size:
-        pairs = [(i, i ^ step) for i in range(size)]
-        total = total + lax.ppermute(total, axis, pairs)
-        step *= 2
+    for step in range(1, size):
+        pairs = [(i, (i + step) % size) for i in range(size)]
+        total = total + lax.ppermute(part, axis, pairs)
     return total
 
 

time: 92.5 us -> 93.8 us (1.014)
  starting transfers between devices: 40.9 us -> 43.9 us
  waiting for transfers between devices: 20.9 us -> 19.2 us
    ppermute x2 -> x3, starting transfers between devices: 8.58 us -> 11.6 us  [head_sum(): total = total + lax.ppermute(part, axis, pairs)]
    ppermute x2 -> x3, waiting for transfers between devices: 3.83 us -> 2.19 us  [head_sum(): total = total + lax.ppermute(part, axis, pairs)]
  transfers between devices with their start and end apart: 6 -> 7, of which waited for: 4 -> 3; matrix products, arithmetic and copies ran while one was open for 13% -> 12% of each run, Pallas kernels for 0% -> 0%
where the time goes in v5:
time: 93.8 us; the launch traced here: 93.2 us
  starting transfers between devices  43.9 us (47%)
  waiting for transfers between devices  19.2 us (20%)
  matrix products  10.9 us (12%)
  local copies, waits for them, and re-layouts  8.83 us (9%)
  other arithmetic  5.49 us (6%)
  blocking collectives  4.3 us (5%)
    all_to_all x1, starting transfers between devices, exclusive_prefix(): lax.all_to_all(share.reshape(chips, -1), ('cx', 'cz'), 0, 0, tiled=True)  18.9 us
    ppermute x3, starting transfers between devices, head_sum(): total = total + lax.ppermute(part, axis, pairs)  11.6 us
    all_to_all x1, waiting for transfers between devices, exclusive_prefix(): back = lax.all_to_all(pref, ('cx', 'cz'), 0, 0, tiled=True)  10.8 us
    all_to_all x1, starting transfers between devices, exclusive_prefix(): back = lax.all_to_all(pref, ('cx', 'cz'), 0, 0, tiled=True)  8.02 us
    all_to_all x1, waiting for transfers between devices, exclusive_prefix(): lax.all_to_all(share.reshape(chips, -1), ('cx', 'cz'), 0, 0, tiled=True)  6.24 us
    ppermute x2, starting transfers between devices, passed_along(): return lax.ppermute(shard, axis, pairs)  5.39 us
    dot_general x2, matrix products, compact_features(): return jnp.einsum('cf,hft->hct', fold, full, precision=HIGH)  3.08 us
    all_gather x1, blocking collectives, exclusive_prefix(): pair = lax.all_gather(flat, 'cc')  2.28 us
  transfers between devices with their start and end apart: 7, of which 3 were waited for; matrix products, arithmetic and copies ran while one was open for 12% of the time, Pallas kernels for 0%

profile of v5, /device:TPU:6, one launch (start us, length us, event | category | flops | bytes accessed | tf_op | source)
XLA Modules:
  0.0 93.2 jit_solution(16972717305750217902)
XLA Ops:
  0.0 0.8 convert_bitcast_fusion
  0.8 0.8 broadcast_multiply_fusion
  1.6 0.1 multiply_multiply_fusion
  1.8 1.6 %fusion.61 = (f32[4,153]{1,0:T(4,128)S(1)}, f32[4,256,153]{1,2,0:T(8,128)S(1)}) fusion(f32[153,273,1]{1,0,2:T(8,128)S(1)} %copy-done.8, f32[4,256,256]{2,1,0:T(8,128)S(1)} %bitcast.81, f32[4,16,256]{2,1,0:T(8,128)S(1)} %broadcast_multiply_fusion, f32[273]{0:T(512)S(1)} %pad.16.clone), kind=kOutput, calls=%fused_computation.90 | convolution fusion | flops 513972640 | bytes 1911416 | tf_op jit(solution)/shard_map/cf,hft->hct/dot_general | solution.py:52
  3.4 0.4 fusion.34
  3.9 0.1 reshape.170
  4.0 2.3 %all-gather = f32[163840]{0:T(1024)S(1)} all-gather(f32[81920]{0:T(1024)S(1)} %select_maximum_fusion), channel_id=2, replica_groups=mesh['cx'=4,'cz'=16,'cc'=2,'head'=4] {'cc'}, dimensions={0}, use_global_device_ids=true | all-gather | bytes 983040 | tf_op jit(solution)/shard_map/all_gather | solution.py:64
  6.3 0.4 reshape.182
  6.7 1.7 %select_reduce_fusion.1 = (f32[81920]{0:T(1024)S(1)}, f32[81920]{0:T(1024)S(1)}) fusion(f32[2,81920]{1,0:T(2,128)S(1)} %reshape.182, pred[2]{0:T(512)(128)(4,1)S(1)} %iota_compare_fusion.4), kind=kLoop, calls=%fused_computation.27 | loop fusion | flops 327680 | bytes 1310722 | tf_op jit(solution)/shard_map/reduce_sum | solution.py:57
  8.5 0.2 reshape.171
  8.7 0.8 constant_dynamic-slice_fusion
  9.5 18.9 %all-to-all-start = ((f32[64,1,640]{2,1,0:T(1,128)}), f32[64,1,640]{2,1,0:T(1,128)S(1)}, u32[]{:S(2)}, u32[]{:S(2)}) async-start(f32[64,1,640]{2,1,0:T(1,128)} %bitcast.8), calls=%async_computation | async-start | bytes 327680 | tf_op jit(solution)/shard_map/all_to_all | solution.py:68
  28.4 1.9 %collective-permute-start.1 = (bf16[64,512]{1,0:T(8,128)(2,1)S(1)}, bf16[64,512]{1,0:T(8,128)(2,1)S(1)}, u32[]{:S(2)}, u32[]{:S(2)}) collective-permute-start(bf16[64,512]{1,0:T(8,128)(2,1)S(1)} %slice.40), channel_id=1, source_target_pairs={{0,4},{4,8},{8,12},{12,16},{16,20},{20,24},{24,28},{28,32},{32,36}... | collective-permute-start | bytes 196616 | tf_op jit(solution)/shard_map/ppermute | solution.py:23
  30.4 0.6 slice.38
  31.0 3.5 %collective-permute-start = (bf16[64,512]{1,0:T(8,128)(2,1)}, bf16[64,512]{1,0:T(8,128)(2,1)S(1)}, u32[]{:S(2)}, u32[]{:S(2)}) collective-permute-start(bf16[64,512]{1,0:T(8,128)(2,1)} %slice.38), channel_id=1, source_target_pairs={{0,4},{4,8},{8,12},{12,16},{16,20},{20,24},{24,28},{28,32},{32,36}... | collective-permute-start | bytes 196616 | tf_op jit(solution)/shard_map/ppermute | solution.py:23
  34.6 0.1 multiply_multiply_fusion.1
  34.7 0.5 fusion.62
  35.2 1.1 %fusion.31 = f32[4,256,128]{1,2,0:T(8,128)} fusion(bf16[4,256,256]{1,2,0:T(8,128)(2,1)S(1)} %get-tuple-element.15, bf16[256,512]{1,0:T(8,128)(2,1)S(1)} %copy-done), kind=kOutput, calls=%fused_computation.46 | convolution fusion | flops 67108864 | bytes 1310720 | tf_op jit(solution)/shard_map/hts,shv->htv/dot_general | solution.py:121
  36.3 0.1 add_compare_fusion
  36.4 0.1 fusion.48
  36.5 1.5 %fusion.8 = f32[4,256,153]{1,2,0:T(8,128)S(1)} fusion(f32[153,273,1]{1,0,2:T(8,128)S(1)} %copy-done.7, f32[4,256,256]{2,1,0:T(8,128)S(1)} %bitcast.80, f32[4,16,256]{2,1,0:T(8,128)S(1)} %broadcast_multiply_fusion.1, f32[273]{0:T(512)S(1)} %pad.16.clone), kind=kOutput, calls=%fused_computation.11 | convolution fusion | flops 513816576 | bytes 1908968 | tf_op jit(solution)/shard_map/cf,hft->hct/dot_general | solution.py:52
  38.2 0.8 copy.45
  38.9 0.8 reshape.180
  39.8 6.2 %all-to-all-done = f32[64,1,640]{2,1,0:T(1,128)S(1)} async-done(((f32[64,1,640]{2,1,0:T(1,128)}), f32[64,1,640]{2,1,0:T(1,128)S(1)}, u32[]{:S(2)}, u32[]{:S(2)}) %all-to-all-start) | async-done | bytes 163872 | tf_op jit(solution)/shard_map/all_to_all | solution.py:68
  46.0 0.3 convolution_bitcast_fusion.1
  46.3 0.8 copy.41
  47.1 8.0 %all-to-all-start.1 = ((f32[64,1,640]{2,1,0:T(1,128)}), f32[64,1,640]{2,1,0:T(1,128)S(1)}, u32[]{:S(2)}, u32[]{:S(2)}) async-start(f32[64,1,640]{2,1,0:T(1,128)} %copy.41), calls=%async_computation.1 | async-start | bytes 327680 | tf_op jit(solution)/shard_map/all_to_all | solution.py:71
  55.4 0.8 copy.44
  56.3 0.8 copy-done.6
  57.1 1.4 %fusion.7 = f32[4,4,64,128]{3,2,1,0:T(8,128)S(1)} fusion(bf16[4,64,4,128]{3,1,2,0:T(8,128)(2,1)S(1)} %copy-done.5, bf16[4,64,4,128]{3,1,2,0:T(8,128)(2,1)} %copy.44, bf16[4,64,4,128]{3,2,1,0:T(4,128)(2,1)S(1)} %copy-done.6), kind=kOutput, calls=%fused_computation.10 | convolution fusion | flops 34734080 | bytes 1310720 | tf_op jit(solution)/shard_map/bihe,bjhe->bhij/dot_general | solution.py:95
  58.5 0.4 fusion.63
  58.9 0.4 copy-done.14
  59.3 1.6 %fusion.6 = f32[4,64,4,128]{3,1,2,0:T(8,128)S(1)} fusion(bf16[4,64,4,128]{3,1,2,0:T(8,128)(2,1)S(1)} %copy.43, bf16[4,64,4,128]{3,1,2,0:T(8,128)(2,1)S(1)} %copy.42, f32[4,64,4]{1,2,0:T(4,128)S(1)} %bitcast.91, f32[4,4,64,128]{3,2,1,0:T(8,128)} %copy-done.14, pred[4,64,128]{2,1,0:T(8,128)(4,1)S(1)} %broadcast_and_fusion), kind=kOutput, calls=%fused_computation.8 | convolution fusion | flops 35259520 | bytes 1609728 | tf_op jit(solution)/shard_map/bhij,bjhe->bihe/dot_general | solution.py:107
  60.9 0.3 copy.47
  61.3 10.8 %all-to-all-done.1 = f32[64,1,640]{2,1,0:T(1,128)S(1)} async-done(((f32[64,1,640]{2,1,0:T(1,128)}), f32[64,1,640]{2,1,0:T(1,128)S(1)}, u32[]{:S(2)}, u32[]{:S(2)}) %all-to-all-start.1) | async-done | bytes 163872 | tf_op jit(solution)/shard_map/all_to_all | solution.py:71
  72.1 2.0 %all-gather.1 = f32[2,1,40960]{2,1,0:T(1,128)S(1)} all-gather(f32[1,1,40960]{2,1,0:T(1,128)S(1)} %bitcast.84), channel_id=1, replica_groups=mesh['cx'=4,'cz'=16,'cc'=2,'head'=4] {'cc'}, dimensions={0}, use_global_device_ids=true | all-gather | bytes 491520 | tf_op jit(solution)/shard_map/all_gather | solution.py:72
  74.2 0.1 reshape.192
  74.3 0.7 reshape.173
  75.0 0.5 fusion.64
  75.5 2.0 %fusion.2 = f32[256,4,128]{0,2,1:T(8,128)S(1)} fusion(f32[4,256,128]{1,2,0:T(8,128)S(1)} %copy-done.3, f32[4,256,153]{1,2,0:T(8,128)S(1)} %fusion.8, f32[4,153,128]{2,1,0:T(8,128)} %reshape.173, f32[256,4]{0,1:T(4,128)S(1)} %fusion.49), kind=kOutput, calls=%fused_computation.4 | convolution fusion | flops 240910336 | bytes 1992704 | tf_op jit(solution)/shard_map/hft,hfv->htv/dot_general | solution.py:169
  77.6 0.2 copy.48
  77.8 0.5 copy-done.13
  78.3 0.3 multiply_reduce_fusion
  78.6 3.5 %collective-permute-start.2 = (f32[256]{0:T(256)S(1)}, f32[256]{0:T(256)S(1)}, u32[]{:S(2)}, u32[]{:S(2)}) collective-permute-start(f32[256]{0:T(256)S(1)} %get-tuple-element.7), channel_id=1, source_target_pairs={{0,1},{1,2},{2,3},{3,0},{4,5},{5,6},{6,7},{7,4},{8,9},{9,10},{10,1... | collective-permute-start | bytes 3080 | tf_op jit(solution)/shard_map/ppermute | solution.py:132
  82.1 4.8 %collective-permute-start.3 = (f32[256]{0:T(256)S(1)}, f32[256]{0:T(256)S(1)}, u32[]{:S(2)}, u32[]{:S(2)}) collective-permute-start(f32[256]{0:T(256)S(1)} %get-tuple-element.7), channel_id=1, source_target_pairs={{0,2},{1,3},{2,0},{3,1},{4,6},{5,7},{6,4},{7,5},{8,10},{9,11},{10,... | collective-permute-start | bytes 3080 | tf_op jit(solution)/shard_map/ppermute | solution.py:132
  86.9 3.3 %collective-permute-start.4 = (f32[256]{0:T(256)S(1)}, f32[256]{0:T(256)S(1)}, u32[]{:S(2)}, u32[]{:S(2)}) collective-permute-start(f32[256]{0:T(256)S(1)} %get-tuple-element.7), channel_id=1, source_target_pairs={{0,3},{1,0},{2,1},{3,2},{4,7},{5,4},{6,5},{7,6},{8,11},{9,8},{10,9... | collective-permute-start | bytes 3080 | tf_op jit(solution)/shard_map/ppermute | solution.py:132
  90.2 2.2 %collective-permute-done.4 = f32[256]{0:T(256)S(1)} collective-permute-done((f32[256]{0:T(256)S(1)}, f32[256]{0:T(256)S(1)}, u32[]{:S(2)}, u32[]{:S(2)}) %collective-permute-start.4) | collective-permute-done | bytes 1056 | tf_op jit(solution)/shard_map/ppermute | solution.py:132
  92.4 0.8 multiply_convert_fusion
  (59 shorter events, 0.8 us)
Async XLA Ops:
  0.0 3.4 %copy-start = (bf16[256,512]{1,0:T(8,128)(2,1)S(1)}, bf16[256,512]{1,0:T(8,128)(2,1)}, u32[]{:S(2)}) copy-start(bf16[256,512]{1,0:T(8,128)(2,1)} %param.13) | copy-start | bytes 786436
  0.0 1.8 %copy-start.8 = (f32[153,273,1]{1,0,2:T(8,128)S(1)}, f32[153,273,1]{1,0,2:T(8,128)}, u32[]{:S(2)}) copy-start(f32[153,273,1]{1,0,2:T(8,128)} %constant.73) | copy-start | bytes 501232
  6.7 21.7 %copy-start.2 = (bf16[256,512]{1,0:T(8,128)(2,1)S(1)}, bf16[256,512]{1,0:T(8,128)(2,1)}, u32[]{:S(2)}) copy-start(bf16[256,512]{1,0:T(8,128)(2,1)} %param.15) | copy-start | bytes 786436
  8.4 21.9 %copy-start.1 = (bf16[256,512]{1,0:T(8,128)(2,1)S(1)}, bf16[256,512]{1,0:T(8,128)(2,1)}, u32[]{:S(2)}) copy-start(bf16[256,512]{1,0:T(8,128)(2,1)} %param.16) | copy-start | bytes 786436
  8.4 26.0 %copy-start.9 = (bf16[256,64]{0,1:T(8,128)(2,1)S(1)}, bf16[256,64]{0,1:T(8,128)(2,1)}, u32[]{:S(2)}) copy-start(bf16[256,64]{0,1:T(8,128)(2,1)} %param.11) | copy-start | bytes 98308
  9.5 25.2 %copy-start.10 = (bf16[256,64]{0,1:T(8,128)(2,1)S(1)}, bf16[256,64]{0,1:T(8,128)(2,1)}, u32[]{:S(2)}) copy-start(bf16[256,64]{0,1:T(8,128)(2,1)} %param.12) | copy-start | bytes 98308
  9.5 36.5 %all-to-all-start = ((f32[64,1,640]{2,1,0:T(1,128)}), f32[64,1,640]{2,1,0:T(1,128)S(1)}, u32[]{:S(2)}, u32[]{:S(2)}) async-start(f32[64,1,640]{2,1,0:T(1,128)} %bitcast.8), calls=%async_computation | async-start | bytes 327680 | tf_op jit(solution)/shard_map/all_to_all | solution.py:68
  28.4 26.7 %collective-permute-start.1 = (bf16[64,512]{1,0:T(8,128)(2,1)S(1)}, bf16[64,512]{1,0:T(8,128)(2,1)S(1)}, u32[]{:S(2)}, u32[]{:S(2)}) collective-permute-start(bf16[64,512]{1,0:T(8,128)(2,1)S(1)} %slice.40), channel_id=1, source_target_pairs={{0,4},{4,8},{8,12},{12,16},{16,20},{20,24},{24,28},{28,32},{32,36}... | collective-permute-start | bytes 196616 | tf_op jit(solution)/shard_map/ppermute | solution.py:23
  31.0 8.7 %collective-permute-start = (bf16[64,512]{1,0:T(8,128)(2,1)}, bf16[64,512]{1,0:T(8,128)(2,1)S(1)}, u32[]{:S(2)}, u32[]{:S(2)}) collective-permute-start(bf16[64,512]{1,0:T(8,128)(2,1)} %slice.38), channel_id=1, source_target_pairs={{0,4},{4,8},{8,12},{12,16},{16,20},{20,24},{24,28},{28,32},{32,36}... | collective-permute-start | bytes 196616 | tf_op jit(solution)/shard_map/ppermute | solution.py:23
  35.2 1.2 %copy-start.7 = (f32[153,273,1]{1,0,2:T(8,128)S(1)}, f32[153,273,1]{1,0,2:T(8,128)}, u32[]{:S(2)}) copy-start(f32[153,273,1]{1,0,2:T(8,128)} %constant.72) | copy-start | bytes 501232
  36.3 1.7 %copy-start.12 = (bf16[3,512]{1,0:T(4,128)(2,1)S(1)}, bf16[3,512]{1,0:T(4,128)(2,1)}, u32[]{:S(2)}) copy-start(bf16[3,512]{1,0:T(4,128)(2,1)} %param.17) | copy-start | bytes 9220
  37.9 1.0 %copy-start.4 = (bf16[256,512]{1,0:T(8,128)(2,1)S(1)}, bf16[256,512]{1,0:T(8,128)(2,1)}, u32[]{:S(2)}) copy-start(bf16[256,512]{1,0:T(8,128)(2,1)} %param.14) | copy-start | bytes 786436
  38.2 7.9 %copy-start.11 = (f32[64,64]{1,0:T(8,128)S(1)}, f32[64,64]{1,0:T(8,128)}, u32[]{:S(2)}) copy-start(f32[64,64]{1,0:T(8,128)} %constant.69.clone) | copy-start | bytes 49156
  47.1 25.0 %all-to-all-start.1 = ((f32[64,1,640]{2,1,0:T(1,128)}), f32[64,1,640]{2,1,0:T(1,128)S(1)}, u32[]{:S(2)}, u32[]{:S(2)}) async-start(f32[64,1,640]{2,1,0:T(1,128)} %copy.41), calls=%async_computation.1 | async-start | bytes 327680 | tf_op jit(solution)/shard_map/all_to_all | solution.py:71
  55.3 1.0 %copy-start.5 = (bf16[4,64,4,128]{3,1,2,0:T(8,128)(2,1)S(1)}, bf16[4,64,4,128]{3,1,2,0:T(8,128)(2,1)}, u32[]{:S(2)}) copy-start(bf16[4,64,4,128]{3,1,2,0:T(8,128)(2,1)} %copy.45) | copy-start | bytes 786436
  56.1 1.0 %copy-start.6 = (bf16[4,64,4,128]{3,2,1,0:T(4,128)(2,1)S(1)}, bf16[4,64,4,128]{3,2,1,0:T(4,128)(2,1)}, u32[]{:S(2)}) copy-start(bf16[4,64,4,128]{3,2,1,0:T(4,128)(2,1)} %reshape.180) | copy-start | bytes 786436
  58.5 0.8 copy-start.14
  74.2 1.4 %copy-start.3 = (f32[4,256,128]{1,2,0:T(8,128)S(1)}, f32[4,256,128]{1,2,0:T(8,128)}, u32[]{:S(2)}) copy-start(f32[4,256,128]{1,2,0:T(8,128)} %fusion.31) | copy-start | bytes 1572868
  77.6 0.7 copy-start.13
  78.6 11.6 %collective-permute-start.2 = (f32[256]{0:T(256)S(1)}, f32[256]{0:T(256)S(1)}, u32[]{:S(2)}, u32[]{:S(2)}) collective-permute-start(f32[256]{0:T(256)S(1)} %get-tuple-element.7), channel_id=1, source_target_pairs={{0,1},{1,2},{2,3},{3,0},{4,5},{5,6},{6,7},{7,4},{8,9},{9,10},{10,1... | collective-permute-start | bytes 3080 | tf_op jit(solution)/shard_map/ppermute | solution.py:132
  82.1 8.1 %collective-permute-start.3 = (f32[256]{0:T(256)S(1)}, f32[256]{0:T(256)S(1)}, u32[]{:S(2)}, u32[]{:S(2)}) collective-permute-start(f32[256]{0:T(256)S(1)} %get-tuple-element.7), channel_id=1, source_target_pairs={{0,2},{1,3},{2,0},{3,1},{4,6},{5,7},{6,4},{7,5},{8,10},{9,11},{10,... | collective-permute-start | bytes 3080 | tf_op jit(solution)/shard_map/ppermute | solution.py:132
  86.9 5.5 %collective-permute-start.4 = (f32[256]{0:T(256)S(1)}, f32[256]{0:T(256)S(1)}, u32[]{:S(2)}, u32[]{:S(2)}) collective-permute-start(f32[256]{0:T(256)S(1)} %get-tuple-element.7), channel_id=1, source_target_pairs={{0,3},{1,0},{2,1},{3,2},{4,7},{5,4},{6,5},{7,6},{8,11},{9,8},{10,9... | collective-permute-start | bytes 3080 | tf_op jit(solution)/shard_map/ppermute | solution.py:132

commit v6 on v4

--- a/solution.py
+++ b/solution.py
@@ -172,7 +172,7 @@
     denom = inner_den + jnp.einsum("hft,hf->ht", phi_q, prior_norm, precision=HIGH)
     lin_out = jnp.transpose(numer / denom[..., None], (1, 0, 2)).reshape(count, heads * VDIM)
     mixed = head_gain[None, :] * (lin_out + window_out + conv_out)
-    squares = head_sum(jnp.sum(mixed * mixed, axis=-1), "head")
+    squares = jnp.sum(lax.all_gather(jnp.sum(mixed * mixed, axis=-1), "head"), axis=0)
     msq = squares / D
     return (mixed * lax.rsqrt(msq + 1e-06)[:, None]).astype(jnp.bfloat16)
 

time: 92.5 us -> 90 us (0.973)
  blocking collectives: 4.3 us -> 14.3 us
  starting transfers between devices: 40.9 us -> 32.4 us
  waiting for transfers between devices: 20.9 us -> 17 us
    all_gather x0 -> x1, blocking collectives: none -> 9.99 us  [body(): lax.all_gather(jnp.sum(mixed * mixed, axis=-1), 'head')]
    ppermute x2 -> x0, starting transfers between devices: 8.58 us -> none  [head_sum(): total = total + lax.ppermute(total, axis, pairs)]
    ppermute x2 -> x0, waiting for transfers between devices: 3.83 us -> none  [head_sum(): total = total + lax.ppermute(total, axis, pairs)]
  transfers between devices with their start and end apart: 6 -> 4, of which waited for: 4 -> 2; matrix products, arithmetic and copies ran while one was open for 13% -> 13% of each run, Pallas kernels for 0% -> 0%
where the time goes in v6:
time: 90 us; the launch traced here: 89.5 us
  starting transfers between devices  32.4 us (36%)
  waiting for transfers between devices  17 us (19%)
  blocking collectives  14.3 us (16%)
  matrix products  10.9 us (12%)
  local copies, waits for them, and re-layouts  8.89 us (10%)
  other arithmetic  5.51 us (6%)
    all_to_all x1, starting transfers between devices, exclusive_prefix(): lax.all_to_all(share.reshape(chips, -1), ('cx', 'cz'), 0, 0, tiled=True)  18.9 us
    all_to_all x1, waiting for transfers between devices, exclusive_prefix(): back = lax.all_to_all(pref, ('cx', 'cz'), 0, 0, tiled=True)  10.8 us
    all_gather x1, blocking collectives, body(): lax.all_gather(jnp.sum(mixed * mixed, axis=-1), 'head')  9.99 us
    all_to_all x1, starting transfers between devices, exclusive_prefix(): back = lax.all_to_all(pref, ('cx', 'cz'), 0, 0, tiled=True)  8.06 us
    all_to_all x1, waiting for transfers between devices, exclusive_prefix(): lax.all_to_all(share.reshape(chips, -1), ('cx', 'cz'), 0, 0, tiled=True)  6.19 us
    ppermute x2, starting transfers between devices, passed_along(): return lax.ppermute(shard, axis, pairs)  5.39 us
    dot_general x2, matrix products, compact_features(): return jnp.einsum('cf,hft->hct', fold, full, precision=HIGH)  3.08 us
    all_gather x1, blocking collectives, exclusive_prefix(): pair = lax.all_gather(flat, 'cc')  2.28 us
  transfers between devices with their start and end apart: 4, of which 2 were waited for; matrix products, arithmetic and copies ran while one was open for 13% of the time, Pallas kernels for 0%

profile of v6, /device:TPU:6, one launch (start us, length us, event | category | flops | bytes accessed | tf_op | source)
XLA Modules:
  0.0 89.5 jit_solution(1847472132033697599)
XLA Ops:
  0.0 0.8 convert_bitcast_fusion
  0.8 0.8 broadcast_multiply_fusion
  1.6 0.1 multiply_multiply_fusion
  1.8 1.6 %fusion.61 = (f32[4,153]{1,0:T(4,128)S(1)}, f32[4,256,153]{1,2,0:T(8,128)S(1)}) fusion(f32[153,273,1]{1,0,2:T(8,128)S(1)} %copy-done.8, f32[4,256,256]{2,1,0:T(8,128)S(1)} %bitcast.82, f32[4,16,256]{2,1,0:T(8,128)S(1)} %broadcast_multiply_fusion, f32[273]{0:T(512)S(1)} %pad.16.clone), kind=kOutput, calls=%fused_computation.90 | convolution fusion | flops 513972640 | bytes 1911416 | tf_op jit(solution)/shard_map/cf,hft->hct/dot_general | solution.py:52
  3.4 0.4 fusion.34
  3.9 0.1 reshape.174
  4.0 2.3 %all-gather = f32[163840]{0:T(1024)S(1)} all-gather(f32[81920]{0:T(1024)S(1)} %select_maximum_fusion), channel_id=2, replica_groups=mesh['cx'=4,'cz'=16,'cc'=2,'head'=4] {'cc'}, dimensions={0}, use_global_device_ids=true | all-gather | bytes 983040 | tf_op jit(solution)/shard_map/all_gather | solution.py:64
  6.3 0.4 reshape.186
  6.7 1.7 %select_reduce_fusion.1 = (f32[81920]{0:T(1024)S(1)}, f32[81920]{0:T(1024)S(1)}) fusion(f32[2,81920]{1,0:T(2,128)S(1)} %reshape.186, pred[2]{0:T(512)(128)(4,1)S(1)} %iota_compare_fusion.4), kind=kLoop, calls=%fused_computation.27 | loop fusion | flops 327680 | bytes 1310722 | tf_op jit(solution)/shard_map/reduce_sum | solution.py:57
  8.5 0.2 reshape.175
  8.7 0.8 constant_dynamic-slice_fusion
  9.5 18.9 %all-to-all-start = ((f32[64,1,640]{2,1,0:T(1,128)}), f32[64,1,640]{2,1,0:T(1,128)S(1)}, u32[]{:S(2)}, u32[]{:S(2)}) async-start(f32[64,1,640]{2,1,0:T(1,128)} %bitcast.8), calls=%async_computation | async-start | bytes 327680 | tf_op jit(solution)/shard_map/all_to_all | solution.py:68
  28.4 1.9 %collective-permute-start.1 = (bf16[64,512]{1,0:T(8,128)(2,1)S(1)}, bf16[64,512]{1,0:T(8,128)(2,1)S(1)}, u32[]{:S(2)}, u32[]{:S(2)}) collective-permute-start(bf16[64,512]{1,0:T(8,128)(2,1)S(1)} %slice.40), channel_id=1, source_target_pairs={{0,4},{4,8},{8,12},{12,16},{16,20},{20,24},{24,28},{28,32},{32,36}... | collective-permute-start | bytes 196616 | tf_op jit(solution)/shard_map/ppermute | solution.py:23
  30.4 0.6 slice.38
  31.0 3.5 %collective-permute-start = (bf16[64,512]{1,0:T(8,128)(2,1)}, bf16[64,512]{1,0:T(8,128)(2,1)S(1)}, u32[]{:S(2)}, u32[]{:S(2)}) collective-permute-start(bf16[64,512]{1,0:T(8,128)(2,1)} %slice.38), channel_id=1, source_target_pairs={{0,4},{4,8},{8,12},{12,16},{16,20},{20,24},{24,28},{28,32},{32,36}... | collective-permute-start | bytes 196616 | tf_op jit(solution)/shard_map/ppermute | solution.py:23
  34.6 0.1 multiply_multiply_fusion.1
  34.7 0.5 fusion.62
  35.3 1.1 %fusion.31 = f32[4,256,128]{1,2,0:T(8,128)} fusion(bf16[4,256,256]{1,2,0:T(8,128)(2,1)S(1)} %get-tuple-element.15, bf16[256,512]{1,0:T(8,128)(2,1)S(1)} %copy-done), kind=kOutput, calls=%fused_computation.46 | convolution fusion | flops 67108864 | bytes 1310720 | tf_op jit(solution)/shard_map/hts,shv->htv/dot_general | solution.py:121
  36.3 0.1 add_compare_fusion
  36.4 0.1 fusion.48
  36.5 1.5 %fusion.8 = f32[4,256,153]{1,2,0:T(8,128)S(1)} fusion(f32[153,273,1]{1,0,2:T(8,128)S(1)} %copy-done.7, f32[4,256,256]{2,1,0:T(8,128)S(1)} %bitcast.81, f32[4,16,256]{2,1,0:T(8,128)S(1)} %broadcast_multiply_fusion.1, f32[273]{0:T(512)S(1)} %pad.16.clone), kind=kOutput, calls=%fused_computation.11 | convolution fusion | flops 513816576 | bytes 1908968 | tf_op jit(solution)/shard_map/cf,hft->hct/dot_general | solution.py:52
  38.1 0.1 reshape.181
  38.2 0.8 copy.45
  38.9 0.8 reshape.184
  39.8 6.2 %all-to-all-done = f32[64,1,640]{2,1,0:T(1,128)S(1)} async-done(((f32[64,1,640]{2,1,0:T(1,128)}), f32[64,1,640]{2,1,0:T(1,128)S(1)}, u32[]{:S(2)}, u32[]{:S(2)}) %all-to-all-start) | async-done | bytes 163872 | tf_op jit(solution)/shard_map/all_to_all | solution.py:68
  46.0 0.3 convolution_bitcast_fusion.1
  46.3 0.8 copy.41
  47.1 8.1 %all-to-all-start.1 = ((f32[64,1,640]{2,1,0:T(1,128)}), f32[64,1,640]{2,1,0:T(1,128)S(1)}, u32[]{:S(2)}, u32[]{:S(2)}) async-start(f32[64,1,640]{2,1,0:T(1,128)} %copy.41), calls=%async_computation.1 | async-start | bytes 327680 | tf_op jit(solution)/shard_map/all_to_all | solution.py:71
  55.3 0.1 convert_element_type.23
  55.3 0.1 reshape.182
  55.4 0.8 copy.44
  56.3 0.8 copy-done.6
  57.2 1.4 %fusion.7 = f32[4,4,64,128]{3,2,1,0:T(8,128)S(1)} fusion(bf16[4,64,4,128]{3,1,2,0:T(8,128)(2,1)S(1)} %copy-done.5, bf16[4,64,4,128]{3,1,2,0:T(8,128)(2,1)} %copy.44, bf16[4,64,4,128]{3,2,1,0:T(4,128)(2,1)S(1)} %copy-done.6), kind=kOutput, calls=%fused_computation.10 | convolution fusion | flops 34734080 | bytes 1310720 | tf_op jit(solution)/shard_map/bihe,bjhe->bhij/dot_general | solution.py:95
  58.6 0.4 fusion.63
  58.9 0.4 copy-done.14
  59.4 1.6 %fusion.6 = f32[4,64,4,128]{3,1,2,0:T(8,128)S(1)} fusion(bf16[4,64,4,128]{3,1,2,0:T(8,128)(2,1)S(1)} %copy.43, bf16[4,64,4,128]{3,1,2,0:T(8,128)(2,1)S(1)} %copy.42, f32[4,64,4]{1,2,0:T(4,128)S(1)} %bitcast.93, f32[4,4,64,128]{3,2,1,0:T(8,128)} %copy-done.14, pred[4,64,128]{2,1,0:T(8,128)(4,1)S(1)} %broadcast_and_fusion), kind=kOutput, calls=%fused_computation.8 | convolution fusion | flops 35259520 | bytes 1609728 | tf_op jit(solution)/shard_map/bhij,bjhe->bihe/dot_general | solution.py:107
  60.9 0.3 copy.47
  61.3 10.8 %all-to-all-done.1 = f32[64,1,640]{2,1,0:T(1,128)S(1)} async-done(((f32[64,1,640]{2,1,0:T(1,128)}), f32[64,1,640]{2,1,0:T(1,128)S(1)}, u32[]{:S(2)}, u32[]{:S(2)}) %all-to-all-start.1) | async-done | bytes 163872 | tf_op jit(solution)/shard_map/all_to_all | solution.py:71
  72.1 2.0 %all-gather.2 = f32[2,1,40960]{2,1,0:T(1,128)S(1)} all-gather(f32[1,1,40960]{2,1,0:T(1,128)S(1)} %bitcast.85), channel_id=1, replica_groups=mesh['cx'=4,'cz'=16,'cc'=2,'head'=4] {'cc'}, dimensions={0}, use_global_device_ids=true | all-gather | bytes 491520 | tf_op jit(solution)/shard_map/all_gather | solution.py:72
  74.3 0.1 reshape.200
  74.3 0.7 reshape.177
  75.1 0.5 fusion.64
  75.6 2.0 %fusion.2 = f32[256,4,128]{0,2,1:T(8,128)S(1)} fusion(f32[4,256,128]{1,2,0:T(8,128)S(1)} %copy-done.3, f32[4,256,153]{1,2,0:T(8,128)S(1)} %fusion.8, f32[4,153,128]{2,1,0:T(8,128)} %reshape.177, f32[256,4]{0,1:T(4,128)S(1)} %fusion.49), kind=kOutput, calls=%fused_computation.4 | convolution fusion | flops 240910336 | bytes 1992704 | tf_op jit(solution)/shard_map/hft,hfv->htv/dot_general | solution.py:171
  77.6 0.2 copy.48
  77.8 0.5 copy-done.13
  78.3 0.3 multiply_reduce_fusion
  78.6 10.0 %all-gather.3 = f32[4,1,256]{2,1,0:T(1,128)S(1)} all-gather(f32[1,1,256]{2,1,0:T(1,128)S(1)} %bitcast.92), channel_id=3, replica_groups=mesh['cx'=4,'cz'=16,'cc'=2,'head'=4] {'head'}, dimensions={0}, use_global_device_ids=true | all-gather | bytes 5120 | tf_op jit(solution)/shard_map/all_gather | solution.py:175
  88.7 0.8 multiply_convert_fusion
  (55 shorter events, 0.6 us)
Async XLA Ops:
  0.0 3.4 %copy-start = (bf16[256,512]{1,0:T(8,128)(2,1)S(1)}, bf16[256,512]{1,0:T(8,128)(2,1)}, u32[]{:S(2)}) copy-start(bf16[256,512]{1,0:T(8,128)(2,1)} %param.13) | copy-start | bytes 786436
  0.0 1.8 %copy-start.8 = (f32[153,273,1]{1,0,2:T(8,128)S(1)}, f32[153,273,1]{1,0,2:T(8,128)}, u32[]{:S(2)}) copy-start(f32[153,273,1]{1,0,2:T(8,128)} %constant.73) | copy-start | bytes 501232
  6.7 21.7 %copy-start.2 = (bf16[256,512]{1,0:T(8,128)(2,1)S(1)}, bf16[256,512]{1,0:T(8,128)(2,1)}, u32[]{:S(2)}) copy-start(bf16[256,512]{1,0:T(8,128)(2,1)} %param.15) | copy-start | bytes 786436
  8.4 21.9 %copy-start.1 = (bf16[256,512]{1,0:T(8,128)(2,1)S(1)}, bf16[256,512]{1,0:T(8,128)(2,1)}, u32[]{:S(2)}) copy-start(bf16[256,512]{1,0:T(8,128)(2,1)} %param.16) | copy-start | bytes 786436
  8.4 26.0 %copy-start.9 = (bf16[256,64]{0,1:T(8,128)(2,1)S(1)}, bf16[256,64]{0,1:T(8,128)(2,1)}, u32[]{:S(2)}) copy-start(bf16[256,64]{0,1:T(8,128)(2,1)} %param.11) | copy-start | bytes 98308
  9.5 25.2 %copy-start.10 = (bf16[256,64]{0,1:T(8,128)(2,1)S(1)}, bf16[256,64]{0,1:T(8,128)(2,1)}, u32[]{:S(2)}) copy-start(bf16[256,64]{0,1:T(8,128)(2,1)} %param.12) | copy-start | bytes 98308
  9.5 36.5 %all-to-all-start = ((f32[64,1,640]{2,1,0:T(1,128)}), f32[64,1,640]{2,1,0:T(1,128)S(1)}, u32[]{:S(2)}, u32[]{:S(2)}) async-start(f32[64,1,640]{2,1,0:T(1,128)} %bitcast.8), calls=%async_computation | async-start | bytes 327680 | tf_op jit(solution)/shard_map/all_to_all | solution.py:68
  28.4 26.8 %collective-permute-start.1 = (bf16[64,512]{1,0:T(8,128)(2,1)S(1)}, bf16[64,512]{1,0:T(8,128)(2,1)S(1)}, u32[]{:S(2)}, u32[]{:S(2)}) collective-permute-start(bf16[64,512]{1,0:T(8,128)(2,1)S(1)} %slice.40), channel_id=1, source_target_pairs={{0,4},{4,8},{8,12},{12,16},{16,20},{20,24},{24,28},{28,32},{32,36}... | collective-permute-start | bytes 196616 | tf_op jit(solution)/shard_map/ppermute | solution.py:23
  31.0 8.8 %collective-permute-start = (bf16[64,512]{1,0:T(8,128)(2,1)}, bf16[64,512]{1,0:T(8,128)(2,1)S(1)}, u32[]{:S(2)}, u32[]{:S(2)}) collective-permute-start(bf16[64,512]{1,0:T(8,128)(2,1)} %slice.38), channel_id=1, source_target_pairs={{0,4},{4,8},{8,12},{12,16},{16,20},{20,24},{24,28},{28,32},{32,36}... | collective-permute-start | bytes 196616 | tf_op jit(solution)/shard_map/ppermute | solution.py:23
  35.2 1.2 %copy-start.7 = (f32[153,273,1]{1,0,2:T(8,128)S(1)}, f32[153,273,1]{1,0,2:T(8,128)}, u32[]{:S(2)}) copy-start(f32[153,273,1]{1,0,2:T(8,128)} %constant.72) | copy-start | bytes 501232
  36.3 1.7 %copy-start.12 = (bf16[3,512]{1,0:T(4,128)(2,1)S(1)}, bf16[3,512]{1,0:T(4,128)(2,1)}, u32[]{:S(2)}) copy-start(bf16[3,512]{1,0:T(4,128)(2,1)} %param.17) | copy-start | bytes 9220
  38.0 1.0 %copy-start.4 = (bf16[256,512]{1,0:T(8,128)(2,1)S(1)}, bf16[256,512]{1,0:T(8,128)(2,1)}, u32[]{:S(2)}) copy-start(bf16[256,512]{1,0:T(8,128)(2,1)} %param.14) | copy-start | bytes 786436
  38.2 7.8 %copy-start.11 = (f32[64,64]{1,0:T(8,128)S(1)}, f32[64,64]{1,0:T(8,128)}, u32[]{:S(2)}) copy-start(f32[64,64]{1,0:T(8,128)} %constant.69.clone) | copy-start | bytes 49156
  47.1 25.0 %all-to-all-start.1 = ((f32[64,1,640]{2,1,0:T(1,128)}), f32[64,1,640]{2,1,0:T(1,128)S(1)}, u32[]{:S(2)}, u32[]{:S(2)}) async-start(f32[64,1,640]{2,1,0:T(1,128)} %copy.41), calls=%async_computation.1 | async-start | bytes 327680 | tf_op jit(solution)/shard_map/all_to_all | solution.py:71
  55.3 1.0 %copy-start.5 = (bf16[4,64,4,128]{3,1,2,0:T(8,128)(2,1)S(1)}, bf16[4,64,4,128]{3,1,2,0:T(8,128)(2,1)}, u32[]{:S(2)}) copy-start(bf16[4,64,4,128]{3,1,2,0:T(8,128)(2,1)} %copy.45) | copy-start | bytes 786436
  56.2 1.0 %copy-start.6 = (bf16[4,64,4,128]{3,2,1,0:T(4,128)(2,1)S(1)}, bf16[4,64,4,128]{3,2,1,0:T(4,128)(2,1)}, u32[]{:S(2)}) copy-start(bf16[4,64,4,128]{3,2,1,0:T(4,128)(2,1)} %reshape.184) | copy-start | bytes 786436
  58.6 0.8 copy-start.14
  74.2 1.4 %copy-start.3 = (f32[4,256,128]{1,2,0:T(8,128)S(1)}, f32[4,256,128]{1,2,0:T(8,128)}, u32[]{:S(2)}) copy-start(f32[4,256,128]{1,2,0:T(8,128)} %fusion.31) | copy-start | bytes 1572868
  77.6 0.7 copy-start.13

commit v7 on v6

--- a/solution.py
+++ b/solution.py
@@ -12,6 +12,7 @@
 TAPS = 3
 D = 2048
 HIGH = lax.Precision.HIGHEST
+THREE = lax.Precision.HIGH
 
 
 CTX = ("cx", "cz", "cc")
@@ -49,7 +50,7 @@
 def compact_features(x_tok, doubled):
     full = features_outer(x_tok)
     fold = fold_matrix(x_tok.shape[-1], doubled)
-    return jnp.einsum("cf,hft->hct", fold, full, precision=HIGH)
+    return jnp.einsum("cf,hft->hct", fold, full, precision=THREE)
 
 
 def masked_rows(rows, upto):
@@ -145,7 +146,7 @@
     phi_q = compact_features(queries, True)
     phi_k = compact_features(keys, False)
     feat = phi_k.shape[1]
-    local_state = jnp.einsum("hft,thv->hfv", phi_k, values32, precision=HIGH)
+    local_state = jnp.einsum("hft,thv->hfv", phi_k, values32, precision=THREE)
     local_norm = jnp.sum(phi_k, axis=-1)
     size = lax.axis_size("cc") * lax.axis_size("cx") * lax.axis_size("cz")
     packed = jnp.concatenate([local_state.reshape(-1), local_norm.reshape(-1)])
@@ -168,8 +169,8 @@
     for tap in range(TAPS):
         conv_out = conv_out + taps[tap][None, :] * value_f32[WIN - tap : WIN - tap + count]
     inner_num, inner_den = inner_causal(queries, keys, values)
-    numer = inner_num + jnp.einsum("hft,hfv->htv", phi_q, prior_state, precision=HIGH)
-    denom = inner_den + jnp.einsum("hft,hf->ht", phi_q, prior_norm, precision=HIGH)
+    numer = inner_num + jnp.einsum("hft,hfv->htv", phi_q, prior_state, precision=THREE)
+    denom = inner_den + jnp.einsum("hft,hf->ht", phi_q, prior_norm, precision=THREE)
     lin_out = jnp.transpose(numer / denom[..., None], (1, 0, 2)).reshape(count, heads * VDIM)
     mixed = head_gain[None, :] * (lin_out + window_out + conv_out)
     squares = jnp.sum(lax.all_gather(jnp.sum(mixed * mixed, axis=-1), "head"), axis=0)

time: 90 us -> 88.1 us (0.979)
  matrix products: 10.9 us -> 8.93 us
    dot_general x5, matrix products: 6.06 us -> 4.1 us  [the longest x2 1.85 us: compact_features(): return jnp.einsum('cf,hft->hct', fold, full, precision=THREE)]
  transfers between devices with their start and end apart: 4 -> 4, of which waited for: 2 -> 3; matrix products, arithmetic and copies ran while one was open for 13% -> 13% of each run, Pallas kernels for 0% -> 0%
where the time goes in v7:
time: 88.1 us; the launch traced here: 87.5 us
  starting transfers between devices  31.8 us (36%)
  waiting for transfers between devices  17.7 us (20%)
  blocking collectives  14.3 us (16%)
  matrix products  8.93 us (10%)
  local copies, waits for them, and re-layouts  8.89 us (10%)
  other arithmetic  5.51 us (6%)
    all_to_all x1, starting transfers between devices, exclusive_prefix(): lax.all_to_all(share.reshape(chips, -1), ('cx', 'cz'), 0, 0, tiled=True)  18.9 us
    all_to_all x1, waiting for transfers between devices, exclusive_prefix(): back = lax.all_to_all(pref, ('cx', 'cz'), 0, 0, tiled=True)  10.8 us
    all_gather x1, blocking collectives, body(): lax.all_gather(jnp.sum(mixed * mixed, axis=-1), 'head')  9.99 us
    all_to_all x1, starting transfers between devices, exclusive_prefix(): back = lax.all_to_all(pref, ('cx', 'cz'), 0, 0, tiled=True)  7.45 us
    all_to_all x1, waiting for transfers between devices, exclusive_prefix(): lax.all_to_all(share.reshape(chips, -1), ('cx', 'cz'), 0, 0, tiled=True)  6.45 us
    ppermute x2, starting transfers between devices, passed_along(): return lax.ppermute(shard, axis, pairs)  5.39 us
    all_gather x1, blocking collectives, exclusive_prefix(): pair = lax.all_gather(flat, 'cc')  2.28 us
    all_gather x1, blocking collectives, exclusive_prefix(): shares = lax.all_gather(back.reshape(-1), 'cc')  2.03 us
  transfers between devices with their start and end apart: 4, of which 3 were waited for; matrix products, arithmetic and copies ran while one was open for 13% of the time, Pallas kernels for 0%

profile of v7, /device:TPU:6, one launch (start us, length us, event | category | flops | bytes accessed | tf_op | source)
XLA Modules:
  0.0 87.5 jit_solution(3722249081622962182)
XLA Ops:
  0.0 0.8 convert_bitcast_fusion
  0.8 0.8 broadcast_multiply_fusion
  1.6 0.1 multiply_multiply_fusion
  1.8 1.0 %fusion.61 = (f32[4,153]{1,0:T(4,128)S(1)}, f32[4,256,153]{1,2,0:T(8,128)S(1)}) fusion(f32[153,273,1]{1,0,2:T(8,128)S(1)} %copy-done.8, f32[4,256,256]{2,1,0:T(8,128)S(1)} %bitcast.82, f32[4,16,256]{2,1,0:T(8,128)S(1)} %broadcast_multiply_fusion, f32[273]{0:T(512)S(1)} %pad.16.clone), kind=kOutput, calls=%fused_computation.90 | convolution fusion | flops 257343904 | bytes 1911416 | tf_op jit(solution)/shard_map/cf,hft->hct/dot_general | solution.py:53
  2.8 0.3 fusion.34
  3.2 0.1 reshape.174
  3.3 2.3 %all-gather = f32[163840]{0:T(1024)S(1)} all-gather(f32[81920]{0:T(1024)S(1)} %select_maximum_fusion), channel_id=2, replica_groups=mesh['cx'=4,'cz'=16,'cc'=2,'head'=4] {'cc'}, dimensions={0}, use_global_device_ids=true | all-gather | bytes 983040 | tf_op jit(solution)/shard_map/all_gather | solution.py:65
  5.6 0.4 reshape.186
  6.0 1.7 %select_reduce_fusion.1 = (f32[81920]{0:T(1024)S(1)}, f32[81920]{0:T(1024)S(1)}) fusion(f32[2,81920]{1,0:T(2,128)S(1)} %reshape.186, pred[2]{0:T(512)(128)(4,1)S(1)} %iota_compare_fusion.4), kind=kLoop, calls=%fused_computation.27 | loop fusion | flops 327680 | bytes 1310722 | tf_op jit(solution)/shard_map/reduce_sum | solution.py:58
  7.7 0.2 reshape.175
  7.9 0.8 constant_dynamic-slice_fusion
  8.8 18.9 %all-to-all-start = ((f32[64,1,640]{2,1,0:T(1,128)}), f32[64,1,640]{2,1,0:T(1,128)S(1)}, u32[]{:S(2)}, u32[]{:S(2)}) async-start(f32[64,1,640]{2,1,0:T(1,128)} %bitcast.8), calls=%async_computation | async-start | bytes 327680 | tf_op jit(solution)/shard_map/all_to_all | solution.py:69
  27.7 1.9 %collective-permute-start.1 = (bf16[64,512]{1,0:T(8,128)(2,1)S(1)}, bf16[64,512]{1,0:T(8,128)(2,1)S(1)}, u32[]{:S(2)}, u32[]{:S(2)}) collective-permute-start(bf16[64,512]{1,0:T(8,128)(2,1)S(1)} %slice.40), channel_id=1, source_target_pairs={{0,4},{4,8},{8,12},{12,16},{16,20},{20,24},{24,28},{28,32},{32,36}... | collective-permute-start | bytes 196616 | tf_op jit(solution)/shard_map/ppermute | solution.py:24
  29.7 0.6 slice.38
  30.3 3.5 %collective-permute-start = (bf16[64,512]{1,0:T(8,128)(2,1)}, bf16[64,512]{1,0:T(8,128)(2,1)S(1)}, u32[]{:S(2)}, u32[]{:S(2)}) collective-permute-start(bf16[64,512]{1,0:T(8,128)(2,1)} %slice.38), channel_id=1, source_target_pairs={{0,4},{4,8},{8,12},{12,16},{16,20},{20,24},{24,28},{28,32},{32,36}... | collective-permute-start | bytes 196616 | tf_op jit(solution)/shard_map/ppermute | solution.py:24
  33.9 0.1 multiply_multiply_fusion.1
  34.0 0.5 fusion.62
  34.5 1.1 %fusion.31 = f32[4,256,128]{1,2,0:T(8,128)} fusion(bf16[4,256,256]{1,2,0:T(8,128)(2,1)S(1)} %get-tuple-element.15, bf16[256,512]{1,0:T(8,128)(2,1)S(1)} %copy-done), kind=kOutput, calls=%fused_computation.46 | convolution fusion | flops 67108864 | bytes 1310720 | tf_op jit(solution)/shard_map/hts,shv->htv/dot_general | solution.py:122
  35.6 0.1 add_compare_fusion
  35.7 0.1 fusion.48
  35.8 0.8 fusion.8
  36.8 0.1 reshape.181
  36.9 0.8 copy.45
  37.6 0.8 reshape.184
  38.4 0.4 collective-permute-done
  38.8 6.4 %all-to-all-done = f32[64,1,640]{2,1,0:T(1,128)S(1)} async-done(((f32[64,1,640]{2,1,0:T(1,128)}), f32[64,1,640]{2,1,0:T(1,128)S(1)}, u32[]{:S(2)}, u32[]{:S(2)}) %all-to-all-start) | async-done | bytes 163872 | tf_op jit(solution)/shard_map/all_to_all | solution.py:69
  45.3 0.3 convolution_bitcast_fusion.1
  45.6 0.8 copy.41
  46.4 7.4 %all-to-all-start.1 = ((f32[64,1,640]{2,1,0:T(1,128)}), f32[64,1,640]{2,1,0:T(1,128)S(1)}, u32[]{:S(2)}, u32[]{:S(2)}) async-start(f32[64,1,640]{2,1,0:T(1,128)} %copy.41), calls=%async_computation.1 | async-start | bytes 327680 | tf_op jit(solution)/shard_map/all_to_all | solution.py:72
  53.9 0.1 convert_element_type.23
  54.1 0.8 copy.44
  55.0 0.8 copy-done.6
  55.8 1.4 %fusion.7 = f32[4,4,64,128]{3,2,1,0:T(8,128)S(1)} fusion(bf16[4,64,4,128]{3,1,2,0:T(8,128)(2,1)S(1)} %copy-done.5, bf16[4,64,4,128]{3,1,2,0:T(8,128)(2,1)} %copy.44, bf16[4,64,4,128]{3,2,1,0:T(4,128)(2,1)S(1)} %copy-done.6), kind=kOutput, calls=%fused_computation.10 | convolution fusion | flops 34734080 | bytes 1310720 | tf_op jit(solution)/shard_map/bihe,bjhe->bhij/dot_general | solution.py:96
  57.2 0.4 fusion.63
  57.6 0.4 copy-done.14
  58.1 1.6 %fusion.6 = f32[4,64,4,128]{3,1,2,0:T(8,128)S(1)} fusion(bf16[4,64,4,128]{3,1,2,0:T(8,128)(2,1)S(1)} %copy.43, bf16[4,64,4,128]{3,1,2,0:T(8,128)(2,1)S(1)} %copy.42, f32[4,64,4]{1,2,0:T(4,128)S(1)} %bitcast.93, f32[4,4,64,128]{3,2,1,0:T(8,128)} %copy-done.14, pred[4,64,128]{2,1,0:T(8,128)(4,1)S(1)} %broadcast_and_fusion), kind=kOutput, calls=%fused_computation.8 | convolution fusion | flops 35259520 | bytes 1609728 | tf_op jit(solution)/shard_map/bhij,bjhe->bihe/dot_general | solution.py:108
  59.6 0.3 copy.47
  60.0 10.8 %all-to-all-done.1 = f32[64,1,640]{2,1,0:T(1,128)S(1)} async-done(((f32[64,1,640]{2,1,0:T(1,128)}), f32[64,1,640]{2,1,0:T(1,128)S(1)}, u32[]{:S(2)}, u32[]{:S(2)}) %all-to-all-start.1) | async-done | bytes 163872 | tf_op jit(solution)/shard_map/all_to_all | solution.py:72
  70.8 2.0 %all-gather.2 = f32[2,1,40960]{2,1,0:T(1,128)S(1)} all-gather(f32[1,1,40960]{2,1,0:T(1,128)S(1)} %bitcast.85), channel_id=1, replica_groups=mesh['cx'=4,'cz'=16,'cc'=2,'head'=4] {'cc'}, dimensions={0}, use_global_device_ids=true | all-gather | bytes 491520 | tf_op jit(solution)/shard_map/all_gather | solution.py:73
  72.9 0.1 reshape.200
  73.0 0.7 reshape.177
  73.7 0.3 fusion.64
  74.0 1.6 %fusion.2 = f32[256,4,128]{0,2,1:T(8,128)S(1)} fusion(f32[4,256,128]{1,2,0:T(8,128)S(1)} %copy-done.3, f32[4,256,153]{1,2,0:T(8,128)S(1)} %fusion.8, f32[4,153,128]{2,1,0:T(8,128)} %reshape.177, f32[256,4]{0,1:T(4,128)S(1)} %fusion.49), kind=kOutput, calls=%fused_computation.4 | convolution fusion | flops 120586240 | bytes 1992704 | tf_op jit(solution)/shard_map/hft,hfv->htv/dot_general | solution.py:172
  75.7 0.2 copy.48
  75.9 0.5 copy-done.13
  76.4 0.3 multiply_reduce_fusion
  76.7 10.0 %all-gather.3 = f32[4,1,256]{2,1,0:T(1,128)S(1)} all-gather(f32[1,1,256]{2,1,0:T(1,128)S(1)} %bitcast.92), channel_id=3, replica_groups=mesh['cx'=4,'cz'=16,'cc'=2,'head'=4] {'head'}, dimensions={0}, use_global_device_ids=true | all-gather | bytes 5120 | tf_op jit(solution)/shard_map/all_gather | solution.py:176
  86.7 0.8 multiply_convert_fusion
  (55 shorter events, 0.7 us)
Async XLA Ops:
  0.0 2.8 %copy-start = (bf16[256,512]{1,0:T(8,128)(2,1)S(1)}, bf16[256,512]{1,0:T(8,128)(2,1)}, u32[]{:S(2)}) copy-start(bf16[256,512]{1,0:T(8,128)(2,1)} %param.13) | copy-start | bytes 786436
  0.0 1.8 %copy-start.8 = (f32[153,273,1]{1,0,2:T(8,128)S(1)}, f32[153,273,1]{1,0,2:T(8,128)}, u32[]{:S(2)}) copy-start(f32[153,273,1]{1,0,2:T(8,128)} %constant.73) | copy-start | bytes 501232
  6.0 21.7 %copy-start.2 = (bf16[256,512]{1,0:T(8,128)(2,1)S(1)}, bf16[256,512]{1,0:T(8,128)(2,1)}, u32[]{:S(2)}) copy-start(bf16[256,512]{1,0:T(8,128)(2,1)} %param.15) | copy-start | bytes 786436
  7.7 21.9 %copy-start.1 = (bf16[256,512]{1,0:T(8,128)(2,1)S(1)}, bf16[256,512]{1,0:T(8,128)(2,1)}, u32[]{:S(2)}) copy-start(bf16[256,512]{1,0:T(8,128)(2,1)} %param.16) | copy-start | bytes 786436
  7.7 26.0 %copy-start.9 = (bf16[256,64]{0,1:T(8,128)(2,1)S(1)}, bf16[256,64]{0,1:T(8,128)(2,1)}, u32[]{:S(2)}) copy-start(bf16[256,64]{0,1:T(8,128)(2,1)} %param.11) | copy-start | bytes 98308
  8.8 25.2 %copy-start.10 = (bf16[256,64]{0,1:T(8,128)(2,1)S(1)}, bf16[256,64]{0,1:T(8,128)(2,1)}, u32[]{:S(2)}) copy-start(bf16[256,64]{0,1:T(8,128)(2,1)} %param.12) | copy-start | bytes 98308
  8.8 36.5 %all-to-all-start = ((f32[64,1,640]{2,1,0:T(1,128)}), f32[64,1,640]{2,1,0:T(1,128)S(1)}, u32[]{:S(2)}, u32[]{:S(2)}) async-start(f32[64,1,640]{2,1,0:T(1,128)} %bitcast.8), calls=%async_computation | async-start | bytes 327680 | tf_op jit(solution)/shard_map/all_to_all | solution.py:69
  27.7 26.2 %collective-permute-start.1 = (bf16[64,512]{1,0:T(8,128)(2,1)S(1)}, bf16[64,512]{1,0:T(8,128)(2,1)S(1)}, u32[]{:S(2)}, u32[]{:S(2)}) collective-permute-start(bf16[64,512]{1,0:T(8,128)(2,1)S(1)} %slice.40), channel_id=1, source_target_pairs={{0,4},{4,8},{8,12},{12,16},{16,20},{20,24},{24,28},{28,32},{32,36}... | collective-permute-start | bytes 196616 | tf_op jit(solution)/shard_map/ppermute | solution.py:24
  30.3 8.5 %collective-permute-start = (bf16[64,512]{1,0:T(8,128)(2,1)}, bf16[64,512]{1,0:T(8,128)(2,1)S(1)}, u32[]{:S(2)}, u32[]{:S(2)}) collective-permute-start(bf16[64,512]{1,0:T(8,128)(2,1)} %slice.38), channel_id=1, source_target_pairs={{0,4},{4,8},{8,12},{12,16},{16,20},{20,24},{24,28},{28,32},{32,36}... | collective-permute-start | bytes 196616 | tf_op jit(solution)/shard_map/ppermute | solution.py:24
  34.5 1.3 %copy-start.7 = (f32[153,273,1]{1,0,2:T(8,128)S(1)}, f32[153,273,1]{1,0,2:T(8,128)}, u32[]{:S(2)}) copy-start(f32[153,273,1]{1,0,2:T(8,128)} %constant.72) | copy-start | bytes 501232
  35.6 1.1 %copy-start.12 = (bf16[3,512]{1,0:T(4,128)(2,1)S(1)}, bf16[3,512]{1,0:T(4,128)(2,1)}, u32[]{:S(2)}) copy-start(bf16[3,512]{1,0:T(4,128)(2,1)} %param.17) | copy-start | bytes 9220
  36.6 1.0 %copy-start.4 = (bf16[256,512]{1,0:T(8,128)(2,1)S(1)}, bf16[256,512]{1,0:T(8,128)(2,1)}, u32[]{:S(2)}) copy-start(bf16[256,512]{1,0:T(8,128)(2,1)} %param.14) | copy-start | bytes 786436
  36.8 8.4 %copy-start.11 = (f32[64,64]{1,0:T(8,128)S(1)}, f32[64,64]{1,0:T(8,128)}, u32[]{:S(2)}) copy-start(f32[64,64]{1,0:T(8,128)} %constant.69.clone) | copy-start | bytes 49156
  46.4 24.4 %all-to-all-start.1 = ((f32[64,1,640]{2,1,0:T(1,128)}), f32[64,1,640]{2,1,0:T(1,128)S(1)}, u32[]{:S(2)}, u32[]{:S(2)}) async-start(f32[64,1,640]{2,1,0:T(1,128)} %copy.41), calls=%async_computation.1 | async-start | bytes 327680 | tf_op jit(solution)/shard_map/all_to_all | solution.py:72
  54.0 1.0 %copy-start.5 = (bf16[4,64,4,128]{3,1,2,0:T(8,128)(2,1)S(1)}, bf16[4,64,4,128]{3,1,2,0:T(8,128)(2,1)}, u32[]{:S(2)}) copy-start(bf16[4,64,4,128]{3,1,2,0:T(8,128)(2,1)} %copy.45) | copy-start | bytes 786436
  54.9 1.0 %copy-start.6 = (bf16[4,64,4,128]{3,2,1,0:T(4,128)(2,1)S(1)}, bf16[4,64,4,128]{3,2,1,0:T(4,128)(2,1)}, u32[]{:S(2)}) copy-start(bf16[4,64,4,128]{3,2,1,0:T(4,128)(2,1)} %reshape.184) | copy-start | bytes 786436
  57.2 0.8 copy-start.14
  72.9 1.2 %copy-start.3 = (f32[4,256,128]{1,2,0:T(8,128)S(1)}, f32[4,256,128]{1,2,0:T(8,128)}, u32[]{:S(2)}) copy-start(f32[4,256,128]{1,2,0:T(8,128)} %fusion.31) | copy-start | bytes 1572868
  75.7 0.7 copy-start.13

commit v8 on v7

--- a/solution.py
+++ b/solution.py
@@ -64,8 +64,8 @@
     chips = lax.axis_size("cx") * lax.axis_size("cz")
     pair = lax.all_gather(flat, "cc")
     below_core = masked_rows(pair, core)
-    chip = jnp.sum(pair, axis=0)
-    share = lax.dynamic_index_in_dim(chip.reshape(cores, -1), core, 0, False)
+    halves = pair.reshape(cores, cores, -1)
+    share = jnp.sum(lax.dynamic_index_in_dim(halves, core, 1, False), axis=0)
     recv = lax.all_to_all(share.reshape(chips, -1), ("cx", "cz"), 0, 0, tiled=True)
     lower = jnp.asarray(np.tril(np.ones((chips, chips), np.float32), -1))
     pref = jnp.dot(lower, recv, precision=HIGH, preferred_element_type=jnp.float32)

time: 88.1 us -> 92.9 us (1.054)
  starting transfers between devices: 31.8 us -> 37.9 us
  waiting for transfers between devices: 17.7 us -> 12.2 us
  other arithmetic: 5.51 us -> 7.25 us
  matrix products: 8.93 us -> 10.5 us
    all_to_all x1, starting transfers between devices: 7.45 us -> 13.6 us  [exclusive_prefix(): back = lax.all_to_all(pref, ('cx', 'cz'), 0, 0, tiled=True)]
    all_to_all x1, waiting for transfers between devices: 6.45 us -> 0.64 us  [exclusive_prefix(): lax.all_to_all(share.reshape(chips, -1), ('cx', 'cz'), 0, 0, tiled=True)]
    reduce_sum x0 -> x1, other arithmetic: none -> 1.29 us  [exclusive_prefix(): share = jnp.sum(lax.dynamic_index_in_dim(halves, core, 1, False), axis=0)]
    dot_general x2, matrix products: 1.85 us -> 2.8 us  [compact_features(): return jnp.einsum('cf,hft->hct', fold, full, precision=THREE)]
    unnamed x31 -> x33, local copies, waits for them, and re-layouts: 1.82 us -> 2.44 us
  transfers between devices with their start and end apart: 4 -> 4, of which waited for: 3 -> 2; matrix products, arithmetic and copies ran while one was open for 13% -> 18% of each run, Pallas kernels for 0% -> 0%
where the time goes in v8:
time: 92.9 us; the launch traced here: 92.2 us
  starting transfers between devices  37.9 us (41%)
  blocking collectives  14.3 us (15%)
  waiting for transfers between devices  12.2 us (13%)
  matrix products  10.5 us (11%)
  local copies, waits for them, and re-layouts  9.6 us (10%)
  other arithmetic  7.25 us (8%)
    all_to_all x1, starting transfers between devices, exclusive_prefix(): lax.all_to_all(share.reshape(chips, -1), ('cx', 'cz'), 0, 0, tiled=True)  18.9 us
    all_to_all x1, starting transfers between devices, exclusive_prefix(): back = lax.all_to_all(pref, ('cx', 'cz'), 0, 0, tiled=True)  13.6 us
    all_to_all x1, waiting for transfers between devices, exclusive_prefix(): back = lax.all_to_all(pref, ('cx', 'cz'), 0, 0, tiled=True)  11.6 us
    all_gather x1, blocking collectives, body(): lax.all_gather(jnp.sum(mixed * mixed, axis=-1), 'head')  9.99 us
    ppermute x2, starting transfers between devices, passed_along(): return lax.ppermute(shard, axis, pairs)  5.39 us
    dot_general x2, matrix products, compact_features(): return jnp.einsum('cf,hft->hct', fold, full, precision=THREE)  2.8 us
    unnamed x33, local copies, waits for them, and re-layouts  2.44 us
    all_gather x1, blocking collectives, exclusive_prefix(): pair = lax.all_gather(flat, 'cc')  2.28 us
  transfers between devices with their start and end apart: 4, of which 2 were waited for; matrix products, arithmetic and copies ran while one was open for 18% of the time, Pallas kernels for 0%

profile of v8, /device:TPU:6, one launch (start us, length us, event | category | flops | bytes accessed | tf_op | source)
XLA Modules:
  0.0 92.2 jit_solution(8467697027104167730)
XLA Ops:
  0.0 0.8 convert_bitcast_fusion
  0.8 0.8 broadcast_multiply_fusion
  1.6 0.1 multiply_multiply_fusion
  1.8 1.0 %fusion.61 = (f32[4,153]{1,0:T(4,128)S(1)}, f32[4,256,153]{1,2,0:T(8,128)S(1)}) fusion(f32[153,273,1]{1,0,2:T(8,128)S(1)} %copy-done.8, f32[4,256,256]{2,1,0:T(8,128)S(1)} %bitcast.82, f32[4,16,256]{2,1,0:T(8,128)S(1)} %broadcast_multiply_fusion, f32[273]{0:T(512)S(1)} %pad.16.clone), kind=kOutput, calls=%fused_computation.90 | convolution fusion | flops 257343904 | bytes 1911416 | tf_op jit(solution)/shard_map/cf,hft->hct/dot_general | solution.py:53
  2.8 0.3 fusion.34
  3.2 0.1 reshape.173
  3.3 2.3 %all-gather = f32[163840]{0:T(1024)S(1)} all-gather(f32[81920]{0:T(1024)S(1)} %select_maximum_fusion), channel_id=2, replica_groups=mesh['cx'=4,'cz'=16,'cc'=2,'head'=4] {'cc'}, dimensions={0}, use_global_device_ids=true | all-gather | bytes 983040 | tf_op jit(solution)/shard_map/all_gather | solution.py:65
  5.6 0.4 reshape.174
  6.0 1.3 %dynamic-slice_reduce_fusion = f32[40960]{0:T(1024)} fusion(f32[2,2,40960]{2,1,0:T(2,128)S(1)} %reshape.174, s32[]{:T(128)S(6)} %select_n.20), kind=kLoop, calls=%fused_computation.50 | loop fusion | flops 40960 | bytes 491524 | tf_op jit(solution)/shard_map/reduce_sum | solution.py:68
  7.2 18.9 %all-to-all-start = ((f32[64,1,640]{2,1,0:T(1,128)}), f32[64,1,640]{2,1,0:T(1,128)S(1)}, u32[]{:S(2)}, u32[]{:S(2)}) async-start(f32[64,1,640]{2,1,0:T(1,128)} %bitcast.8), calls=%async_computation | async-start | bytes 327680 | tf_op jit(solution)/shard_map/all_to_all | solution.py:69
  26.2 1.9 %collective-permute-start.1 = (bf16[64,512]{1,0:T(8,128)(2,1)S(1)}, bf16[64,512]{1,0:T(8,128)(2,1)S(1)}, u32[]{:S(2)}, u32[]{:S(2)}) collective-permute-start(bf16[64,512]{1,0:T(8,128)(2,1)S(1)} %slice.40), channel_id=1, source_target_pairs={{0,4},{4,8},{8,12},{12,16},{16,20},{20,24},{24,28},{28,32},{32,36}... | collective-permute-start | bytes 196616 | tf_op jit(solution)/shard_map/ppermute | solution.py:24
  28.1 0.6 slice.38
  28.8 3.5 %collective-permute-start = (bf16[64,512]{1,0:T(8,128)(2,1)}, bf16[64,512]{1,0:T(8,128)(2,1)}, u32[]{:S(2)}, u32[]{:S(2)}) collective-permute-start(bf16[64,512]{1,0:T(8,128)(2,1)} %slice.38), channel_id=1, source_target_pairs={{0,4},{4,8},{8,12},{12,16},{16,20},{20,24},{24,28},{28,32},{32,36}... | collective-permute-start | bytes 196616 | tf_op jit(solution)/shard_map/ppermute | solution.py:24
  32.2 0.5 iota_compare_fusion.4
  32.8 0.4 reshape.185
  33.3 0.1 multiply_multiply_fusion.1
  33.4 0.5 copy-done.10
  33.9 1.1 %fusion.62 = (f32[4,256]{1,0:T(4,128)}, bf16[4,256,256]{1,2,0:T(8,128)(2,1)S(1)}) fusion(bf16[256,4,16]{0,2,1:T(8,128)(2,1)S(1)} %bitcast.87, bf16[256,4,16]{0,2,1:T(8,128)(2,1)S(1)} %bitcast.88, pred[256,256]{0,1:T(8,128)(4,1)S(1)} %iota_compare_fusion.1), kind=kOutput, calls=%fused_computation.91 | convolution fusion | flops 10484736 | bytes 659456 | tf_op jit(solution)/shard_map/thf,shf->hts/dot_general | solution.py:117
  35.1 1.1 %fusion.31 = f32[4,256,128]{1,2,0:T(8,128)} fusion(bf16[4,256,256]{1,2,0:T(8,128)(2,1)S(1)} %get-tuple-element.13, bf16[256,512]{1,0:T(8,128)(2,1)S(1)} %copy-done), kind=kOutput, calls=%fused_computation.46 | convolution fusion | flops 67108864 | bytes 1310720 | tf_op jit(solution)/shard_map/hts,shv->htv/dot_general | solution.py:122
  36.1 0.1 add_compare_fusion
  36.2 0.1 fusion.48
  36.3 1.8 %fusion.8 = f32[4,256,153]{1,2,0:T(8,128)S(1)} fusion(f32[153,273,1]{1,0,2:T(8,128)} %constant.72, f32[4,256,256]{2,1,0:T(8,128)S(1)} %bitcast.81, f32[4,16,256]{2,1,0:T(8,128)S(1)} %broadcast_multiply_fusion.1, f32[273]{0:T(512)S(1)} %pad.16.clone), kind=kOutput, calls=%fused_computation.11 | convolution fusion | flops 257187840 | bytes 1908968 | tf_op jit(solution)/shard_map/cf,hft->hct/dot_general | solution.py:53
  38.1 1.7 %select_reduce_fusion.1 = f32[81920]{0:T(1024)S(1)} fusion(f32[2,81920]{1,0:T(2,128)S(1)} %reshape.185, pred[2]{0:T(512)(128)(4,1)} %iota_compare_fusion.4), kind=kLoop, calls=%fused_computation.27 | loop fusion | flops 245760 | bytes 983042 | tf_op jit(solution)/shard_map/reduce_sum | solution.py:58
  40.0 0.8 copy.57
  40.7 0.8 reshape.183
  41.5 0.8 copy.55
  42.3 0.8 constant_dynamic-update-slice_fusion.1
  43.1 0.6 all-to-all-done
  43.8 0.3 convolution_bitcast_fusion.1
  44.1 0.8 copy.53
  44.9 13.6 %all-to-all-start.1 = ((f32[64,1,640]{2,1,0:T(1,128)}), f32[64,1,640]{2,1,0:T(1,128)S(1)}, u32[]{:S(2)}, u32[]{:S(2)}) async-start(f32[64,1,640]{2,1,0:T(1,128)} %copy.53), calls=%async_computation.1 | async-start | bytes 327680 | tf_op jit(solution)/shard_map/all_to_all | solution.py:72
  58.8 0.8 copy.56
  59.7 1.4 %fusion.7 = f32[4,4,64,128]{3,2,1,0:T(8,128)S(1)} fusion(bf16[4,64,4,128]{3,1,2,0:T(8,128)(2,1)S(1)} %copy-done.6, bf16[4,64,4,128]{3,1,2,0:T(8,128)(2,1)} %copy.56, bf16[4,64,4,128]{3,2,1,0:T(4,128)(2,1)S(1)} %copy-done.7), kind=kOutput, calls=%fused_computation.10 | convolution fusion | flops 34734080 | bytes 1310720 | tf_op jit(solution)/shard_map/bihe,bjhe->bhij/dot_general | solution.py:96
  61.2 0.4 fusion.63
  61.6 0.4 copy-done.15
  62.0 1.6 %fusion.6 = f32[4,64,4,128]{3,1,2,0:T(8,128)S(1)} fusion(bf16[4,64,4,128]{3,1,2,0:T(8,128)(2,1)S(1)} %copy-done.5, bf16[4,64,4,128]{3,1,2,0:T(8,128)(2,1)S(1)} %copy.54, f32[4,64,4]{1,2,0:T(4,128)S(1)} %bitcast.93, f32[4,4,64,128]{3,2,1,0:T(8,128)} %copy-done.15, pred[4,64,128]{2,1,0:T(8,128)(4,1)S(1)} %broadcast_and_fusion), kind=kOutput, calls=%fused_computation.8 | convolution fusion | flops 35259520 | bytes 1609728 | tf_op jit(solution)/shard_map/bhij,bjhe->bihe/dot_general | solution.py:108
  63.6 0.3 copy.59
  63.9 11.6 %all-to-all-done.1 = f32[64,1,640]{2,1,0:T(1,128)S(1)} async-done(((f32[64,1,640]{2,1,0:T(1,128)}), f32[64,1,640]{2,1,0:T(1,128)S(1)}, u32[]{:S(2)}, u32[]{:S(2)}) %all-to-all-start.1) | async-done | bytes 163872 | tf_op jit(solution)/shard_map/all_to_all | solution.py:72
  75.5 2.0 %all-gather.2 = f32[2,1,40960]{2,1,0:T(1,128)S(1)} all-gather(f32[1,1,40960]{2,1,0:T(1,128)S(1)} %bitcast.85), channel_id=1, replica_groups=mesh['cx'=4,'cz'=16,'cc'=2,'head'=4] {'cc'}, dimensions={0}, use_global_device_ids=true | all-gather | bytes 491520 | tf_op jit(solution)/shard_map/all_gather | solution.py:73
  77.6 0.1 reshape.200
  77.7 0.7 reshape.176
  78.4 0.3 fusion.64
  78.7 1.6 %fusion.2 = f32[256,4,128]{0,2,1:T(8,128)S(1)} fusion(f32[4,256,128]{1,2,0:T(8,128)S(1)} %copy-done.3, f32[4,256,153]{1,2,0:T(8,128)S(1)} %fusion.8, f32[4,153,128]{2,1,0:T(8,128)} %reshape.176, f32[256,4]{0,1:T(4,128)S(1)} %fusion.49), kind=kOutput, calls=%fused_computation.4 | convolution fusion | flops 120586240 | bytes 1992704 | tf_op jit(solution)/shard_map/hft,hfv->htv/dot_general | solution.py:172
  80.4 0.2 copy.60
  80.6 0.5 copy-done.14
  81.0 0.3 multiply_reduce_fusion
  81.4 10.0 %all-gather.3 = f32[4,1,256]{2,1,0:T(1,128)S(1)} all-gather(f32[1,1,256]{2,1,0:T(1,128)S(1)} %bitcast.92), channel_id=3, replica_groups=mesh['cx'=4,'cz'=16,'cc'=2,'head'=4] {'head'}, dimensions={0}, use_global_device_ids=true | all-gather | bytes 5120 | tf_op jit(solution)/shard_map/all_gather | solution.py:176
  91.4 0.8 multiply_convert_fusion
  (57 shorter events, 0.8 us)
Async XLA Ops:
  0.0 2.8 %copy-start = (bf16[256,512]{1,0:T(8,128)(2,1)S(1)}, bf16[256,512]{1,0:T(8,128)(2,1)}, u32[]{:S(2)}) copy-start(bf16[256,512]{1,0:T(8,128)(2,1)} %param.13) | copy-start | bytes 786436
  0.0 1.7 %copy-start.8 = (f32[153,273,1]{1,0,2:T(8,128)S(1)}, f32[153,273,1]{1,0,2:T(8,128)}, u32[]{:S(2)}) copy-start(f32[153,273,1]{1,0,2:T(8,128)} %constant.73) | copy-start | bytes 501232
  5.6 20.6 %copy-start.2 = (bf16[256,512]{1,0:T(8,128)(2,1)S(1)}, bf16[256,512]{1,0:T(8,128)(2,1)}, u32[]{:S(2)}) copy-start(bf16[256,512]{1,0:T(8,128)(2,1)} %param.15) | copy-start | bytes 786436
  5.6 22.6 %copy-start.1 = (bf16[256,512]{1,0:T(8,128)(2,1)S(1)}, bf16[256,512]{1,0:T(8,128)(2,1)}, u32[]{:S(2)}) copy-start(bf16[256,512]{1,0:T(8,128)(2,1)} %param.16) | copy-start | bytes 786436
  7.2 25.9 %copy-start.9 = (bf16[256,64]{0,1:T(8,128)(2,1)S(1)}, bf16[256,64]{0,1:T(8,128)(2,1)}, u32[]{:S(2)}) copy-start(bf16[256,64]{0,1:T(8,128)(2,1)} %param.11) | copy-start | bytes 98308
  7.2 36.5 %all-to-all-start = ((f32[64,1,640]{2,1,0:T(1,128)}), f32[64,1,640]{2,1,0:T(1,128)S(1)}, u32[]{:S(2)}, u32[]{:S(2)}) async-start(f32[64,1,640]{2,1,0:T(1,128)} %bitcast.8), calls=%async_computation | async-start | bytes 327680 | tf_op jit(solution)/shard_map/all_to_all | solution.py:69
  26.2 32.3 %collective-permute-start.1 = (bf16[64,512]{1,0:T(8,128)(2,1)S(1)}, bf16[64,512]{1,0:T(8,128)(2,1)S(1)}, u32[]{:S(2)}, u32[]{:S(2)}) collective-permute-start(bf16[64,512]{1,0:T(8,128)(2,1)S(1)} %slice.40), channel_id=1, source_target_pairs={{0,4},{4,8},{8,12},{12,16},{16,20},{20,24},{24,28},{28,32},{32,36}... | collective-permute-start | bytes 196616 | tf_op jit(solution)/shard_map/ppermute | solution.py:24
  28.8 13.5 %collective-permute-start = (bf16[64,512]{1,0:T(8,128)(2,1)}, bf16[64,512]{1,0:T(8,128)(2,1)}, u32[]{:S(2)}, u32[]{:S(2)}) collective-permute-start(bf16[64,512]{1,0:T(8,128)(2,1)} %slice.38), channel_id=1, source_target_pairs={{0,4},{4,8},{8,12},{12,16},{16,20},{20,24},{24,28},{28,32},{32,36}... | collective-permute-start | bytes 196616 | tf_op jit(solution)/shard_map/ppermute | solution.py:24
  33.2 0.8 copy-start.10
  35.1 1.2 %copy-start.12 = (bf16[3,512]{1,0:T(4,128)(2,1)S(1)}, bf16[3,512]{1,0:T(4,128)(2,1)}, u32[]{:S(2)}) copy-start(bf16[3,512]{1,0:T(4,128)(2,1)} %param.17) | copy-start | bytes 9220
  39.8 1.0 %copy-start.4 = (bf16[256,512]{1,0:T(8,128)(2,1)S(1)}, bf16[256,512]{1,0:T(8,128)(2,1)}, u32[]{:S(2)}) copy-start(bf16[256,512]{1,0:T(8,128)(2,1)} %param.14) | copy-start | bytes 786436
  39.9 3.8 %copy-start.11 = (f32[64,64]{1,0:T(8,128)S(1)}, f32[64,64]{1,0:T(8,128)}, u32[]{:S(2)}) copy-start(f32[64,64]{1,0:T(8,128)} %constant.69.clone) | copy-start | bytes 49156
  44.9 30.5 %all-to-all-start.1 = ((f32[64,1,640]{2,1,0:T(1,128)}), f32[64,1,640]{2,1,0:T(1,128)S(1)}, u32[]{:S(2)}, u32[]{:S(2)}) async-start(f32[64,1,640]{2,1,0:T(1,128)} %copy.53), calls=%async_computation.1 | async-start | bytes 327680 | tf_op jit(solution)/shard_map/all_to_all | solution.py:72
  58.7 1.0 %copy-start.6 = (bf16[4,64,4,128]{3,1,2,0:T(8,128)(2,1)S(1)}, bf16[4,64,4,128]{3,1,2,0:T(8,128)(2,1)}, u32[]{:S(2)}) copy-start(bf16[4,64,4,128]{3,1,2,0:T(8,128)(2,1)} %copy.57) | copy-start | bytes 786436
  58.7 1.0 %copy-start.7 = (bf16[4,64,4,128]{3,2,1,0:T(4,128)(2,1)S(1)}, bf16[4,64,4,128]{3,2,1,0:T(4,128)(2,1)}, u32[]{:S(2)}) copy-start(bf16[4,64,4,128]{3,2,1,0:T(4,128)(2,1)} %reshape.183) | copy-start | bytes 786436
  59.7 2.3 %copy-start.5 = (bf16[4,64,4,128]{3,1,2,0:T(8,128)(2,1)S(1)}, bf16[4,64,4,128]{3,1,2,0:T(8,128)(2,1)}, u32[]{:S(2)}) copy-start(bf16[4,64,4,128]{3,1,2,0:T(8,128)(2,1)} %copy.55) | copy-start | bytes 786436
  61.2 0.8 copy-start.15
  77.5 1.2 %copy-start.13 = (f32[4,256]{1,0:T(4,128)S(1)}, f32[4,256]{1,0:T(4,128)}, u32[]{:S(2)}) copy-start(f32[4,256]{1,0:T(4,128)} %get-tuple-element.12) | copy-start | bytes 12292
  77.5 1.2 %copy-start.3 = (f32[4,256,128]{1,2,0:T(8,128)S(1)}, f32[4,256,128]{1,2,0:T(8,128)}, u32[]{:S(2)}) copy-start(f32[4,256,128]{1,2,0:T(8,128)} %fusion.31) | copy-start | bytes 1572868
  80.3 0.7 copy-start.14

commit v9 on v8

--- a/solution.py
+++ b/solution.py
@@ -24,33 +24,34 @@
     return lax.ppermute(shard, axis, pairs)
 
 
-def features_outer(x_tok):
-    xt = jnp.transpose(x_tok.astype(jnp.float32), (1, 2, 0))
-    heads, fdim, count = xt.shape
+def pair_selectors(fdim, doubled):
+    pairs = [(i, j) for i in range(fdim) for j in range(i, fdim)]
+    left = np.zeros((len(pairs), fdim), np.float32)
+    right = np.zeros((len(pairs), fdim), np.float32)
+    for r, (i, j) in enumerate(pairs):
+        left[r, i] = 2.0 if (doubled and i != j) else 1.0
+        right[r, j] = 1.0
+    return jnp.asarray(left, jnp.bfloat16), jnp.asarray(right, jnp.bfloat16)
+
+
+def compact_features(x_tok, doubled):
+    count, heads, fdim = x_tok.shape
+    left, right = pair_selectors(fdim, doubled)
+    xb = jnp.transpose(x_tok, (1, 2, 0))
+    a = jnp.einsum("rf,hft->hrt", left, xb, preferred_element_type=jnp.float32)
+    b = jnp.einsum("rf,hft->hrt", right, xb, preferred_element_type=jnp.float32)
+    xt = xb.astype(jnp.float32)
     ones = jnp.ones((heads, 1, count), jnp.float32)
-    outer = (xt[:, :, None, :] * xt[:, None, :, :]).reshape(heads, fdim * fdim, count) * (
-        1.0 / math.sqrt(32.0)
-    )
+    outer = (a * b) * (1.0 / math.sqrt(32.0))
     return jnp.concatenate([ones, xt * 0.5, outer], axis=1)
 
 
-def fold_matrix(fdim, doubled):
-    full = 1 + fdim + fdim * fdim
-    pairs = [(i, j) for i in range(fdim) for j in range(i, fdim)]
-    fold = np.zeros((1 + fdim + len(pairs), full), np.float32)
-    for r in range(1 + fdim):
-        fold[r, r] = 1.0
-    for r, (i, j) in enumerate(pairs):
-        fold[1 + fdim + r, 1 + fdim + i * fdim + j] = 1.0
-        if doubled and i != j:
-            fold[1 + fdim + r, 1 + fdim + j * fdim + i] = 1.0
-    return jnp.asarray(fold)
-
-
-def compact_features(x_tok, doubled):
-    full = features_outer(x_tok)
-    fold = fold_matrix(x_tok.shape[-1], doubled)
-    return jnp.einsum("cf,hft->hct", fold, full, precision=THREE)
+def split_dot(feats, values):
+    hi = feats.astype(jnp.bfloat16)
+    lo = (feats - hi.astype(jnp.float32)).astype(jnp.bfloat16)
+    first = jnp.einsum("hft,thv->hfv", hi, values, preferred_element_type=jnp.float32)
+    second = jnp.einsum("hft,thv->hfv", lo, values, preferred_element_type=jnp.float32)
+    return first + second
 
 
 def masked_rows(rows, upto):
@@ -142,11 +143,10 @@
     queries = lin_query.reshape(count, heads, FDIM)
     keys = lin_key.reshape(count, heads, FDIM)
     values = lin_values.reshape(count, heads, VDIM)
-    values32 = values.astype(jnp.float32)
     phi_q = compact_features(queries, True)
     phi_k = compact_features(keys, False)
     feat = phi_k.shape[1]
-    local_state = jnp.einsum("hft,thv->hfv", phi_k, values32, precision=THREE)
+    local_state = split_dot(phi_k, values)
     local_norm = jnp.sum(phi_k, axis=-1)
     size = lax.axis_size("cc") * lax.axis_size("cx") * lax.axis_size("cz")
     packed = jnp.concatenate([local_state.reshape(-1), local_norm.reshape(-1)])

time: 92.9 us -> 92.3 us (level)
  matrix products: 10.5 us -> 7.17 us
  local copies, waits for them, and re-layouts: 9.6 us -> 11.8 us
  waiting for transfers between devices: 12.2 us -> 13.8 us
    unnamed x33 -> x39, local copies, waits for them, and re-layouts: 2.44 us -> 6.22 us
    dot_general x3 -> x6, matrix products: 3.14 us -> 1.61 us  [the longest x2 0.51 us: compact_features(): b = jnp.einsum('rf,hft->hrt', right, xb, preferred_element_type=jnp.float32)]
    all_to_all x1, waiting for transfers between devices: 0.64 us -> 1.92 us  [exclusive_prefix(): lax.all_to_all(share.reshape(chips, -1), ('cx', 'cz'), 0, 0, tiled=True)]
    dot_general x1, matrix products: 1.44 us -> 0.45 us  [window_slab(): jnp.einsum('bihe,bjhe->bhij', qb, keys, preferred_element_type=jnp.float32)]
  transfers between devices with their start and end apart: 4 -> 4, of which waited for: 2 -> 2; matrix products, arithmetic and copies ran while one was open for 18% -> 15% of each run, Pallas kernels for 0% -> 0%
where the time goes in v9:
time: 92.3 us; the launch traced here: 91.5 us
  starting transfers between devices  37.5 us (41%)
  blocking collectives  14.3 us (15%)
  waiting for transfers between devices  13.8 us (15%)
  local copies, waits for them, and re-layouts  11.8 us (13%)
  matrix products  7.17 us (8%)
  other arithmetic  6.56 us (7%)
    all_to_all x1, starting transfers between devices, exclusive_prefix(): lax.all_to_all(share.reshape(chips, -1), ('cx', 'cz'), 0, 0, tiled=True)  18.9 us
    all_to_all x1, starting transfers between devices, exclusive_prefix(): back = lax.all_to_all(pref, ('cx', 'cz'), 0, 0, tiled=True)  13 us
    all_to_all x1, waiting for transfers between devices, exclusive_prefix(): back = lax.all_to_all(pref, ('cx', 'cz'), 0, 0, tiled=True)  11.8 us
    all_gather x1, blocking collectives, body(): lax.all_gather(jnp.sum(mixed * mixed, axis=-1), 'head')  9.99 us
    unnamed x39, local copies, waits for them, and re-layouts  6.22 us
    ppermute x2, starting transfers between devices, passed_along(): return lax.ppermute(shard, axis, pairs)  5.51 us
    all_gather x1, blocking collectives, exclusive_prefix(): pair = lax.all_gather(flat, 'cc')  2.28 us
    all_gather x1, blocking collectives, exclusive_prefix(): shares = lax.all_gather(back.reshape(-1), 'cc')  2.03 us
  transfers between devices with their start and end apart: 4, of which 2 were waited for; matrix products, arithmetic and copies ran while one was open for 15% of the time, Pallas kernels for 0%

profile of v9, /device:TPU:6, one launch (start us, length us, event | category | flops | bytes accessed | tf_op | source)
XLA Modules:
  0.0 91.5 jit_solution(1322908995425907408)
XLA Ops:
  0.0 0.8 convert_multiply_fusion
  1.1 0.4 copy-done.10
  1.6 0.3 fusion.4
  1.8 0.3 fusion.26
  2.2 0.3 fusion.28
  2.5 0.3 convolution_add_fusion.1
  2.9 2.3 %all-gather = f32[163840]{0:T(1024)S(1)} all-gather(f32[81920]{0:T(1024)S(1)} %select_maximum_fusion), channel_id=2, replica_groups=mesh['cx'=4,'cz'=16,'cc'=2,'head'=4] {'cc'}, dimensions={0}, use_global_device_ids=true | all-gather | bytes 983040 | tf_op jit(solution)/shard_map/all_gather | solution.py:66
  5.2 0.4 reshape.158
  5.6 1.3 %dynamic-slice_reduce_fusion = f32[40960]{0:T(1024)} fusion(f32[2,2,40960]{2,1,0:T(2,128)S(1)} %reshape.158, s32[]{:T(128)S(6)} %select_n.20), kind=kLoop, calls=%fused_computation.54 | loop fusion | flops 40960 | bytes 491524 | tf_op jit(solution)/shard_map/reduce_sum | solution.py:69
  6.9 18.9 %all-to-all-start = ((f32[64,1,640]{2,1,0:T(1,128)}), f32[64,1,640]{2,1,0:T(1,128)S(1)}, u32[]{:S(2)}, u32[]{:S(2)}) async-start(f32[64,1,640]{2,1,0:T(1,128)} %bitcast.11), calls=%async_computation | async-start | bytes 327680 | tf_op jit(solution)/shard_map/all_to_all | solution.py:70
  25.9 0.6 slice.40
  26.5 1.9 %collective-permute-start.1 = (bf16[64,512]{1,0:T(8,128)(2,1)}, bf16[64,512]{1,0:T(8,128)(2,1)S(1)}, u32[]{:S(2)}, u32[]{:S(2)}) collective-permute-start(bf16[64,512]{1,0:T(8,128)(2,1)} %slice.40), channel_id=1, source_target_pairs={{0,4},{4,8},{8,12},{12,16},{16,20},{20,24},{24,28},{28,32},{32,36}... | collective-permute-start | bytes 196616 | tf_op jit(solution)/shard_map/ppermute | solution.py:24
  28.4 0.6 slice.38
  29.0 3.6 %collective-permute-start = (bf16[64,512]{1,0:T(8,128)(2,1)}, bf16[64,512]{1,0:T(8,128)(2,1)}, u32[]{:S(2)}, u32[]{:S(2)}) collective-permute-start(bf16[64,512]{1,0:T(8,128)(2,1)} %slice.38), channel_id=1, source_target_pairs={{0,4},{4,8},{8,12},{12,16},{16,20},{20,24},{24,28},{28,32},{32,36}... | collective-permute-start | bytes 196616 | tf_op jit(solution)/shard_map/ppermute | solution.py:24
  33.0 0.3 fusion.2
  33.2 1.1 %fusion.65 = (f32[4,256]{1,0:T(4,128)}, bf16[4,256,256]{1,2,0:T(8,128)(2,1)S(1)}) fusion(bf16[256,4,16]{0,2,1:T(8,128)(2,1)S(1)} %bitcast.94, bf16[256,4,16]{0,2,1:T(8,128)(2,1)S(1)} %bitcast.91, pred[256,256]{0,1:T(8,128)(4,1)S(1)} %iota_compare_fusion.1), kind=kOutput, calls=%fused_computation.95 | convolution fusion | flops 10484736 | bytes 659456 | tf_op jit(solution)/shard_map/thf,shf->hts/dot_general | solution.py:118
  34.3 1.1 %fusion.23 = f32[4,256,128]{1,2,0:T(8,128)} fusion(bf16[4,256,256]{1,2,0:T(8,128)(2,1)S(1)} %get-tuple-element.11, bf16[256,512]{1,0:T(8,128)(2,1)S(1)} %copy-done), kind=kOutput, calls=%fused_computation.42 | convolution fusion | flops 67108864 | bytes 1310720 | tf_op jit(solution)/shard_map/hts,shv->htv/dot_general | solution.py:123
  35.6 0.6 copy-done.13
  36.2 0.6 broadcast_and_fusion
  36.8 0.4 reshape.169
  37.2 0.6 convert_multiply_fusion.1
  37.8 1.0 %select_reduce_fusion.1 = f32[81920]{0:T(1024)S(1)} fusion(f32[2,81920]{1,0:T(2,128)S(1)} %reshape.169, pred[2]{0:T(512)(128)(4,1)S(1)} %iota_compare_fusion.4), kind=kLoop, calls=%fused_computation.24 | loop fusion | flops 245760 | bytes 983042 | tf_op jit(solution)/shard_map/reduce_sum | solution.py:59
  39.0 0.9 copy-done.6
  39.9 0.8 reshape.167
  40.7 0.8 constant_dynamic-update-slice_fusion.1
  41.6 1.9 %all-to-all-done = f32[64,1,640]{2,1,0:T(1,128)S(1)} async-done(((f32[64,1,640]{2,1,0:T(1,128)}), f32[64,1,640]{2,1,0:T(1,128)S(1)}, u32[]{:S(2)}, u32[]{:S(2)}) %all-to-all-start) | async-done | bytes 163872 | tf_op jit(solution)/shard_map/all_to_all | solution.py:70
  43.5 0.3 convolution_bitcast_fusion.1
  43.8 0.8 copy.60
  44.7 13.0 %all-to-all-start.1 = ((f32[64,1,640]{2,1,0:T(1,128)}), f32[64,1,640]{2,1,0:T(1,128)S(1)}, u32[]{:S(2)}, u32[]{:S(2)}) async-start(f32[64,1,640]{2,1,0:T(1,128)} %copy.60), calls=%async_computation.1 | async-start | bytes 327680 | tf_op jit(solution)/shard_map/all_to_all | solution.py:73
  58.1 0.8 copy.61
  59.0 0.5 fusion.11
  59.5 0.3 copy-done.11
  59.8 0.4 fusion.66
  60.1 0.4 copy-done.18
  60.5 0.3 copy-done.8
  60.9 1.6 %fusion.10 = f32[4,64,4,128]{3,1,2,0:T(8,128)S(1)} fusion(bf16[4,64,4,128]{3,1,2,0:T(8,128)(2,1)S(1)} %copy.62, bf16[4,64,4,128]{3,1,2,0:T(8,128)(2,1)S(1)} %copy-done.8, f32[4,64,4]{1,2,0:T(4,128)S(1)} %bitcast.100, f32[4,4,64,128]{3,2,1,0:T(8,128)} %copy-done.18, pred[4,64,128]{2,1,0:T(8,128)(4,1)S(1)} %copy-done.11), kind=kOutput, calls=%fused_computation.14 | convolution fusion | flops 35259520 | bytes 1609728 | tf_op jit(solution)/shard_map/bhij,bjhe->bihe/dot_general | solution.py:109
  62.4 0.3 copy.66
  62.8 11.8 %all-to-all-done.1 = f32[64,1,640]{2,1,0:T(1,128)S(1)} async-done(((f32[64,1,640]{2,1,0:T(1,128)}), f32[64,1,640]{2,1,0:T(1,128)S(1)}, u32[]{:S(2)}, u32[]{:S(2)}) %all-to-all-start.1) | async-done | bytes 163872 | tf_op jit(solution)/shard_map/all_to_all | solution.py:73
  74.6 2.0 %all-gather.2 = f32[2,1,40960]{2,1,0:T(1,128)S(1)} all-gather(f32[1,1,40960]{2,1,0:T(1,128)S(1)} %bitcast.86), channel_id=1, replica_groups=mesh['cx'=4,'cz'=16,'cc'=2,'head'=4] {'cc'}, dimensions={0}, use_global_device_ids=true | all-gather | bytes 491520 | tf_op jit(solution)/shard_map/all_gather | solution.py:74
  76.9 0.8 copy-done.9
  77.7 0.4 fusion.25
  78.0 0.3 copy-done.16
  78.3 0.4 copy-done.3
  78.7 0.7 fusion.6
  79.7 0.7 copy-done.17
  80.3 0.3 multiply_reduce_fusion
  80.7 10.0 %all-gather.3 = f32[4,1,256]{2,1,0:T(1,128)S(1)} all-gather(f32[1,1,256]{2,1,0:T(1,128)S(1)} %bitcast.99), channel_id=3, replica_groups=mesh['cx'=4,'cz'=16,'cc'=2,'head'=4] {'head'}, dimensions={0}, use_global_device_ids=true | all-gather | bytes 5120 | tf_op jit(solution)/shard_map/all_gather | solution.py:176
  90.7 0.8 multiply_convert_fusion
  (63 shorter events, 2.0 us)
Async XLA Ops:
  0.0 2.2 %copy-start = (bf16[256,512]{1,0:T(8,128)(2,1)S(1)}, bf16[256,512]{1,0:T(8,128)(2,1)}, u32[]{:S(2)}) copy-start(bf16[256,512]{1,0:T(8,128)(2,1)} %param.15) | copy-start | bytes 786436
  0.0 0.8 copy-start.4
  0.0 0.8 copy-start.15
  0.9 0.7 copy-start.10
  5.6 20.2 %copy-start.2 = (bf16[256,512]{1,0:T(8,128)(2,1)S(1)}, bf16[256,512]{1,0:T(8,128)(2,1)}, u32[]{:S(2)}) copy-start(bf16[256,512]{1,0:T(8,128)(2,1)} %param.17) | copy-start | bytes 786436
  6.9 21.5 %copy-start.1 = (bf16[256,512]{1,0:T(8,128)(2,1)S(1)}, bf16[256,512]{1,0:T(8,128)(2,1)}, u32[]{:S(2)}) copy-start(bf16[256,512]{1,0:T(8,128)(2,1)} %param.18) | copy-start | bytes 786436
  6.9 36.6 %all-to-all-start = ((f32[64,1,640]{2,1,0:T(1,128)}), f32[64,1,640]{2,1,0:T(1,128)S(1)}, u32[]{:S(2)}, u32[]{:S(2)}) async-start(f32[64,1,640]{2,1,0:T(1,128)} %bitcast.11), calls=%async_computation | async-start | bytes 327680 | tf_op jit(solution)/shard_map/all_to_all | solution.py:70
  26.5 31.2 %collective-permute-start.1 = (bf16[64,512]{1,0:T(8,128)(2,1)}, bf16[64,512]{1,0:T(8,128)(2,1)S(1)}, u32[]{:S(2)}, u32[]{:S(2)}) collective-permute-start(bf16[64,512]{1,0:T(8,128)(2,1)} %slice.40), channel_id=1, source_target_pairs={{0,4},{4,8},{8,12},{12,16},{16,20},{20,24},{24,28},{28,32},{32,36}... | collective-permute-start | bytes 196616 | tf_op jit(solution)/shard_map/ppermute | solution.py:24
  28.4 4.3 %copy-start.14 = (bf16[136,16,1]{0,1,2:T(8,128)(2,1)S(1)}, bf16[136,16,1]{0,1,2:T(8,128)(2,1)}, u32[]{:S(2)}) copy-start(bf16[136,16,1]{0,1,2:T(8,128)(2,1)} %constant.75) | copy-start | bytes 13060
  29.0 3.7 %copy-start.5 = (bf16[256,64]{0,1:T(8,128)(2,1)S(1)}, bf16[256,64]{0,1:T(8,128)(2,1)}, u32[]{:S(2)}) copy-start(bf16[256,64]{0,1:T(8,128)(2,1)} %param.13) | copy-start | bytes 98308
  29.0 11.7 %collective-permute-start = (bf16[64,512]{1,0:T(8,128)(2,1)}, bf16[64,512]{1,0:T(8,128)(2,1)}, u32[]{:S(2)}, u32[]{:S(2)}) collective-permute-start(bf16[64,512]{1,0:T(8,128)(2,1)} %slice.38), channel_id=1, source_target_pairs={{0,4},{4,8},{8,12},{12,16},{16,20},{20,24},{24,28},{28,32},{32,36}... | collective-permute-start | bytes 196616 | tf_op jit(solution)/shard_map/ppermute | solution.py:24
  35.5 0.7 copy-start.13
  39.0 1.0 %copy-start.6 = (bf16[256,512]{1,0:T(8,128)(2,1)S(1)}, bf16[256,512]{1,0:T(8,128)(2,1)}, u32[]{:S(2)}) copy-start(bf16[256,512]{1,0:T(8,128)(2,1)} %param.16) | copy-start | bytes 786436
  41.6 1.9 %copy-start.12 = (f32[64,64]{1,0:T(8,128)S(1)}, f32[64,64]{1,0:T(8,128)}, u32[]{:S(2)}) copy-start(f32[64,64]{1,0:T(8,128)} %constant.72.clone) | copy-start | bytes 49156
  44.7 30.0 %all-to-all-start.1 = ((f32[64,1,640]{2,1,0:T(1,128)}), f32[64,1,640]{2,1,0:T(1,128)S(1)}, u32[]{:S(2)}, u32[]{:S(2)}) async-start(f32[64,1,640]{2,1,0:T(1,128)} %copy.60), calls=%async_computation.1 | async-start | bytes 327680 | tf_op jit(solution)/shard_map/all_to_all | solution.py:73
  58.0 1.0 %copy-start.7 = (bf16[4,64,4,128]{3,2,1,0:T(4,128)(2,1)S(1)}, bf16[4,64,4,128]{3,2,1,0:T(4,128)(2,1)}, u32[]{:S(2)}) copy-start(bf16[4,64,4,128]{3,2,1,0:T(4,128)(2,1)} %reshape.167) | copy-start | bytes 786436
  59.0 0.8 copy-start.11
  59.8 0.8 copy-start.18
  59.8 1.1 %copy-start.8 = (bf16[4,64,4,128]{3,1,2,0:T(8,128)(2,1)S(1)}, bf16[4,64,4,128]{3,1,2,0:T(8,128)(2,1)}, u32[]{:S(2)}) copy-start(bf16[4,64,4,128]{3,1,2,0:T(8,128)(2,1)} %copy.61) | copy-start | bytes 786436
  76.8 0.8 copy-start.9
  77.7 0.7 copy-start.16
  77.7 1.0 %copy-start.3 = (f32[4,256,128]{1,2,0:T(8,128)S(1)}, f32[4,256,128]{1,2,0:T(8,128)}, u32[]{:S(2)}) copy-start(f32[4,256,128]{1,2,0:T(8,128)} %fusion.23) | copy-start | bytes 1572868
  79.7 0.7 copy-start.17

commit v10 on v7

--- a/solution.py
+++ b/solution.py
@@ -159,7 +159,7 @@
     prior_state = prior[:split].reshape(heads, feat, VDIM)
     prior_norm = prior[split:used].reshape(heads, feat)
     start = lax.axis_index(CTX) * count
-    rims = passed_along((win_key[count - WIN :], win_value[count - WIN :]), CTX, 1)
+    rims = passed_along(jnp.stack([win_key[count - WIN :], win_value[count - WIN :]]), CTX, 1)
     key_ext = jnp.concatenate([rims[0], win_key], axis=0)
     value_ext = jnp.concatenate([rims[1], win_value], axis=0)
     window_out = window_slab(win_query, key_ext, value_ext, start)

time: 88.1 us -> 90.8 us (1.031)
  waiting for transfers between devices: 17.7 us -> 20.5 us
  starting transfers between devices: 31.8 us -> 30.2 us
  other arithmetic: 5.51 us -> 6.8 us
    all_to_all x1, waiting for transfers between devices: 10.8 us -> 14.3 us  [exclusive_prefix(): back = lax.all_to_all(pref, ('cx', 'cz'), 0, 0, tiled=True)]
    ppermute x2 -> x1, starting transfers between devices: 5.39 us -> 1.91 us  [passed_along(): return lax.ppermute(shard, axis, pairs)]
    all_to_all x1, starting transfers between devices: 7.45 us -> 9.45 us  [exclusive_prefix(): back = lax.all_to_all(pref, ('cx', 'cz'), 0, 0, tiled=True)]
    all_to_all x1, waiting for transfers between devices: 6.45 us -> 5.23 us  [exclusive_prefix(): lax.all_to_all(share.reshape(chips, -1), ('cx', 'cz'), 0, 0, tiled=True)]
    dot_general x1, matrix products: 1.4 us -> 0.45 us  [window_slab(): jnp.einsum('bihe,bjhe->bhij', qb, keys, preferred_element_type=jnp.float32)]
    unnamed x31 -> x38, local copies, waits for them, and re-layouts: 1.82 us -> 1.44 us
  transfers between devices with their start and end apart: 4 -> 3, of which waited for: 3 -> 3; matrix products, arithmetic and copies ran while one was open for 13% -> 13% of each run, Pallas kernels for 0% -> 0%
where the time goes in v10:
time: 90.8 us; the launch traced here: 90.2 us
  starting transfers between devices  30.2 us (33%)
  waiting for transfers between devices  20.5 us (23%)
  blocking collectives  14.3 us (16%)
  matrix products  9.28 us (10%)
  local copies, waits for them, and re-layouts  8.7 us (10%)
  other arithmetic  6.8 us (7%)
    all_to_all x1, starting transfers between devices, exclusive_prefix(): lax.all_to_all(share.reshape(chips, -1), ('cx', 'cz'), 0, 0, tiled=True)  18.8 us
    all_to_all x1, waiting for transfers between devices, exclusive_prefix(): back = lax.all_to_all(pref, ('cx', 'cz'), 0, 0, tiled=True)  14.3 us
    all_gather x1, blocking collectives, body(): lax.all_gather(jnp.sum(mixed * mixed, axis=-1), 'head')  9.98 us
    all_to_all x1, starting transfers between devices, exclusive_prefix(): back = lax.all_to_all(pref, ('cx', 'cz'), 0, 0, tiled=True)  9.45 us
    all_to_all x1, waiting for transfers between devices, exclusive_prefix(): lax.all_to_all(share.reshape(chips, -1), ('cx', 'cz'), 0, 0, tiled=True)  5.23 us
    dot_general x2, matrix products, compact_features(): return jnp.einsum('cf,hft->hct', fold, full, precision=THREE)  2.5 us
    all_gather x1, blocking collectives, exclusive_prefix(): pair = lax.all_gather(flat, 'cc')  2.28 us
    all_gather x1, blocking collectives, exclusive_prefix(): shares = lax.all_gather(back.reshape(-1), 'cc')  2.03 us
  transfers between devices with their start and end apart: 3, of which 3 were waited for; matrix products, arithmetic and copies ran while one was open for 13% of the time, Pallas kernels for 0%

profile of v10, /device:TPU:6, one launch (start us, length us, event | category | flops | bytes accessed | tf_op | source)
XLA Modules:
  0.0 90.2 jit_solution(11356086694719164807)
XLA Ops:
  0.0 0.8 convert_bitcast_fusion
  0.8 0.8 broadcast_multiply_fusion
  1.6 0.1 multiply_multiply_fusion
  1.8 1.0 %fusion.63 = (f32[4,153]{1,0:T(4,128)S(1)}, f32[4,256,153]{1,2,0:T(8,128)S(1)}) fusion(f32[153,273,1]{1,0,2:T(8,128)S(1)} %copy-done.9, f32[4,256,256]{2,1,0:T(8,128)S(1)} %bitcast.90, f32[4,16,256]{2,1,0:T(8,128)S(1)} %broadcast_multiply_fusion, f32[273]{0:T(512)S(1)} %pad.20.clone), kind=kOutput, calls=%fused_computation.98 | convolution fusion | flops 257343904 | bytes 1911416 | tf_op jit(solution)/shard_map/cf,hft->hct/dot_general | solution.py:53
  2.8 0.3 fusion.36
  3.2 0.1 reshape.174
  3.3 2.3 %all-gather = f32[163840]{0:T(1024)S(1)} all-gather(f32[81920]{0:T(1024)S(1)} %select_maximum_fusion), channel_id=2, replica_groups=mesh['cx'=4,'cz'=16,'cc'=2,'head'=4] {'cc'}, dimensions={0}, use_global_device_ids=true | all-gather | bytes 983040 | tf_op jit(solution)/shard_map/all_gather | solution.py:65
  5.6 0.4 reshape.186
  6.0 1.7 %select_reduce_fusion.1 = (f32[81920]{0:T(1024)S(1)}, f32[81920]{0:T(1024)S(1)}) fusion(f32[2,81920]{1,0:T(2,128)S(1)} %reshape.186, pred[2]{0:T(512)(128)(4,1)S(1)} %iota_compare_fusion.4), kind=kLoop, calls=%fused_computation.27 | loop fusion | flops 327680 | bytes 1310722 | tf_op jit(solution)/shard_map/reduce_sum | solution.py:58
  7.8 0.2 reshape.175
  8.0 0.8 constant_dynamic-slice_fusion
  8.8 18.8 %all-to-all-start = ((f32[64,1,640]{2,1,0:T(1,128)}), f32[64,1,640]{2,1,0:T(1,128)S(1)}, u32[]{:S(2)}, u32[]{:S(2)}) async-start(f32[64,1,640]{2,1,0:T(1,128)} %bitcast.8), calls=%async_computation | async-start | bytes 327680 | tf_op jit(solution)/shard_map/all_to_all | solution.py:69
  27.6 0.7 pad_maximum_fusion.2
  28.3 1.9 %collective-permute-start = (bf16[2,64,512]{2,1,0:T(8,128)(2,1)}, bf16[2,64,512]{2,1,0:T(8,128)(2,1)}, u32[]{:S(2)}, u32[]{:S(2)}) collective-permute-start(bf16[2,64,512]{2,1,0:T(8,128)(2,1)} %pad_maximum_fusion.2), channel_id=1, source_target_pairs={{0,4},{4,8},{8,12},{12,16},{16,20},{20,24},{24,28},{28,32},{32,36}... | collective-permute-start | bytes 393224 | tf_op jit(solution)/shard_map/ppermute | solution.py:24
  30.4 0.1 multiply_multiply_fusion.1
  30.6 0.5 copy-done.11
  31.0 1.1 %fusion.64 = (f32[4,256]{1,0:T(4,128)}, bf16[4,256,256]{1,2,0:T(8,128)(2,1)S(1)}) fusion(bf16[256,4,16]{0,2,1:T(8,128)(2,1)S(1)} %bitcast.95, bf16[256,4,16]{0,2,1:T(8,128)(2,1)S(1)} %bitcast.96, pred[256,256]{0,1:T(8,128)(4,1)S(1)} %iota_compare_fusion.1), kind=kOutput, calls=%fused_computation.99 | convolution fusion | flops 10484736 | bytes 659456 | tf_op jit(solution)/shard_map/thf,shf->hts/dot_general | solution.py:117
  32.2 1.1 %fusion.31 = f32[4,256,128]{1,2,0:T(8,128)} fusion(bf16[4,256,256]{1,2,0:T(8,128)(2,1)S(1)} %get-tuple-element.17, bf16[256,512]{1,0:T(8,128)(2,1)S(1)} %copy-done), kind=kOutput, calls=%fused_computation.46 | convolution fusion | flops 67108864 | bytes 1310720 | tf_op jit(solution)/shard_map/hts,shv->htv/dot_general | solution.py:122
  33.2 0.1 add_compare_fusion
  33.3 0.1 fusion.50
  33.4 0.7 copy.45
  34.2 0.8 reshape.184
  34.9 0.8 copy.43
  35.7 0.6 broadcast_and_fusion
  36.3 1.5 %fusion.8 = f32[4,256,153]{1,2,0:T(8,128)S(1)} fusion(f32[153,273,1]{1,0,2:T(8,128)S(1)} %copy-done.8, f32[4,256,256]{2,1,0:T(8,128)S(1)} %bitcast.89, f32[4,16,256]{2,1,0:T(8,128)S(1)} %broadcast_multiply_fusion.1, f32[273]{0:T(512)} %copy-done.14), kind=kOutput, calls=%fused_computation.11 | convolution fusion | flops 257187840 | bytes 1908968 | tf_op jit(solution)/shard_map/cf,hft->hct/dot_general | solution.py:53
  37.8 1.0 %collective-permute-done = bf16[2,64,512]{2,1,0:T(8,128)(2,1)} collective-permute-done((bf16[2,64,512]{2,1,0:T(8,128)(2,1)}, bf16[2,64,512]{2,1,0:T(8,128)(2,1)}, u32[]{:S(2)}, u32[]{:S(2)}) %collective-permute-start) | collective-permute-done | bytes 131104 | tf_op jit(solution)/shard_map/ppermute | solution.py:24
  38.8 0.9 slice_bitcast_fusion.1
  40.0 5.2 %all-to-all-done = f32[64,1,640]{2,1,0:T(1,128)S(1)} async-done(((f32[64,1,640]{2,1,0:T(1,128)}), f32[64,1,640]{2,1,0:T(1,128)S(1)}, u32[]{:S(2)}, u32[]{:S(2)}) %all-to-all-start) | async-done | bytes 163872 | tf_op jit(solution)/shard_map/all_to_all | solution.py:69
  45.2 0.3 convolution_bitcast_fusion.1
  45.6 0.8 copy.41
  46.4 9.4 %all-to-all-start.1 = ((f32[64,1,640]{2,1,0:T(1,128)}), f32[64,1,640]{2,1,0:T(1,128)S(1)}, u32[]{:S(2)}, u32[]{:S(2)}) async-start(f32[64,1,640]{2,1,0:T(1,128)} %copy.41), calls=%async_computation.1 | async-start | bytes 327680 | tf_op jit(solution)/shard_map/all_to_all | solution.py:72
  55.9 0.5 fusion.7
  56.4 0.4 fusion.65
  56.7 0.4 copy-done.18
  57.1 1.6 %fusion.6 = f32[4,64,4,128]{3,1,2,0:T(8,128)S(1)} fusion(bf16[4,64,4,128]{3,1,2,0:T(8,128)(2,1)S(1)} %copy-done.5, bf16[4,64,4,128]{3,1,2,0:T(8,128)(2,1)S(1)} %copy.42, f32[4,64,4]{1,2,0:T(4,128)S(1)} %bitcast.101, f32[4,4,64,128]{3,2,1,0:T(8,128)} %copy-done.18, pred[4,64,128]{2,1,0:T(8,128)(4,1)S(1)} %copy-done.12), kind=kOutput, calls=%fused_computation.8 | convolution fusion | flops 35259520 | bytes 1609728 | tf_op jit(solution)/shard_map/bhij,bjhe->bihe/dot_general | solution.py:108
  58.8 0.3 copy.47
  59.1 0.1 fusion.33
  59.2 14.3 %all-to-all-done.1 = f32[64,1,640]{2,1,0:T(1,128)S(1)} async-done(((f32[64,1,640]{2,1,0:T(1,128)}), f32[64,1,640]{2,1,0:T(1,128)S(1)}, u32[]{:S(2)}, u32[]{:S(2)}) %all-to-all-start.1) | async-done | bytes 163872 | tf_op jit(solution)/shard_map/all_to_all | solution.py:72
  73.5 2.0 %all-gather.2 = f32[2,1,40960]{2,1,0:T(1,128)S(1)} all-gather(f32[1,1,40960]{2,1,0:T(1,128)S(1)} %bitcast.93), channel_id=1, replica_groups=mesh['cx'=4,'cz'=16,'cc'=2,'head'=4] {'cc'}, dimensions={0}, use_global_device_ids=true | all-gather | bytes 491520 | tf_op jit(solution)/shard_map/all_gather | solution.py:73
  75.6 0.1 reshape.200
  75.7 0.7 reshape.177
  76.5 0.3 fusion.66
  76.8 1.6 %fusion.2 = f32[256,4,128]{0,2,1:T(8,128)S(1)} fusion(f32[4,256,128]{1,2,0:T(8,128)S(1)} %copy-done.3, f32[4,256,153]{1,2,0:T(8,128)S(1)} %fusion.8, f32[4,153,128]{2,1,0:T(8,128)} %reshape.177, f32[256,4]{0,1:T(4,128)S(1)} %fusion.51), kind=kOutput, calls=%fused_computation.4 | convolution fusion | flops 120586240 | bytes 1992704 | tf_op jit(solution)/shard_map/hft,hfv->htv/dot_general | solution.py:172
  78.4 0.2 copy.48
  78.6 0.5 copy-done.17
  79.1 0.3 multiply_reduce_fusion
  79.4 10.0 %all-gather.3 = f32[4,1,256]{2,1,0:T(1,128)S(1)} all-gather(f32[1,1,256]{2,1,0:T(1,128)S(1)} %bitcast.100), channel_id=3, replica_groups=mesh['cx'=4,'cz'=16,'cc'=2,'head'=4] {'head'}, dimensions={0}, use_global_device_ids=true | all-gather | bytes 5120 | tf_op jit(solution)/shard_map/all_gather | solution.py:176
  89.4 0.8 multiply_convert_fusion
  (60 shorter events, 0.7 us)
Async XLA Ops:
  0.0 2.8 %copy-start = (bf16[256,512]{1,0:T(8,128)(2,1)S(1)}, bf16[256,512]{1,0:T(8,128)(2,1)}, u32[]{:S(2)}) copy-start(bf16[256,512]{1,0:T(8,128)(2,1)} %param.13) | copy-start | bytes 786436
  0.0 1.8 %copy-start.9 = (f32[153,273,1]{1,0,2:T(8,128)S(1)}, f32[153,273,1]{1,0,2:T(8,128)}, u32[]{:S(2)}) copy-start(f32[153,273,1]{1,0,2:T(8,128)} %constant.73) | copy-start | bytes 501232
  1.8 1.0 %copy-start.14 = (f32[273]{0:T(512)}, f32[273]{0:T(512)S(1)}, u32[]{:S(2)}) copy-start(f32[273]{0:T(512)S(1)} %pad.20.clone) | copy-start | bytes 3280
  6.0 21.6 %copy-start.1 = (bf16[256,512]{1,0:T(8,128)(2,1)S(1)}, bf16[256,512]{1,0:T(8,128)(2,1)}, u32[]{:S(2)}) copy-start(bf16[256,512]{1,0:T(8,128)(2,1)} %param.16) | copy-start | bytes 786436
  6.0 21.6 %copy-start.2 = (bf16[256,512]{1,0:T(8,128)(2,1)S(1)}, bf16[256,512]{1,0:T(8,128)(2,1)}, u32[]{:S(2)}) copy-start(bf16[256,512]{1,0:T(8,128)(2,1)} %param.15) | copy-start | bytes 786436
  7.7 22.5 %copy-start.10 = (bf16[256,64]{0,1:T(8,128)(2,1)S(1)}, bf16[256,64]{0,1:T(8,128)(2,1)}, u32[]{:S(2)}) copy-start(bf16[256,64]{0,1:T(8,128)(2,1)} %param.11) | copy-start | bytes 98308
  8.8 36.5 %all-to-all-start = ((f32[64,1,640]{2,1,0:T(1,128)}), f32[64,1,640]{2,1,0:T(1,128)S(1)}, u32[]{:S(2)}, u32[]{:S(2)}) async-start(f32[64,1,640]{2,1,0:T(1,128)} %bitcast.8), calls=%async_computation | async-start | bytes 327680 | tf_op jit(solution)/shard_map/all_to_all | solution.py:69
  28.3 10.5 %collective-permute-start = (bf16[2,64,512]{2,1,0:T(8,128)(2,1)}, bf16[2,64,512]{2,1,0:T(8,128)(2,1)}, u32[]{:S(2)}, u32[]{:S(2)}) collective-permute-start(bf16[2,64,512]{2,1,0:T(8,128)(2,1)} %pad_maximum_fusion.2), channel_id=1, source_target_pairs={{0,4},{4,8},{8,12},{12,16},{16,20},{20,24},{24,28},{28,32},{32,36}... | collective-permute-start | bytes 393224 | tf_op jit(solution)/shard_map/ppermute | solution.py:24
  30.3 0.8 copy-start.11
  32.2 2.0 %copy-start.4 = (bf16[256,512]{1,0:T(8,128)(2,1)S(1)}, bf16[256,512]{1,0:T(8,128)(2,1)}, u32[]{:S(2)}) copy-start(bf16[256,512]{1,0:T(8,128)(2,1)} %param.14) | copy-start | bytes 786436
  33.2 3.1 %copy-start.8 = (f32[153,273,1]{1,0,2:T(8,128)S(1)}, f32[153,273,1]{1,0,2:T(8,128)}, u32[]{:S(2)}) copy-start(f32[153,273,1]{1,0,2:T(8,128)} %constant.72) | copy-start | bytes 501232
  35.7 2.1 %copy-start.15 = (bf16[3,512]{1,0:T(4,128)(2,1)S(1)}, bf16[3,512]{1,0:T(4,128)(2,1)}, u32[]{:S(2)}) copy-start(bf16[3,512]{1,0:T(4,128)(2,1)} %param.17) | copy-start | bytes 9220
  39.8 5.5 %copy-start.13 = (f32[64,64]{1,0:T(8,128)S(1)}, f32[64,64]{1,0:T(8,128)}, u32[]{:S(2)}) copy-start(f32[64,64]{1,0:T(8,128)} %constant.69.clone) | copy-start | bytes 49156
  39.9 16.0 %copy-start.6 = (bf16[4,64,4,128]{3,1,2,0:T(8,128)(2,1)S(1)}, bf16[4,64,4,128]{3,1,2,0:T(8,128)(2,1)}, u32[]{:S(2)}) copy-start(bf16[4,64,4,128]{3,1,2,0:T(8,128)(2,1)} %copy.45) | copy-start | bytes 786436
  39.9 16.0 %copy-start.7 = (bf16[4,64,4,128]{3,2,1,0:T(4,128)(2,1)S(1)}, bf16[4,64,4,128]{3,2,1,0:T(4,128)(2,1)}, u32[]{:S(2)}) copy-start(bf16[4,64,4,128]{3,2,1,0:T(4,128)(2,1)} %reshape.184) | copy-start | bytes 786436
  45.5 10.8 %copy-start.12 = (pred[4,64,128]{2,1,0:T(8,128)(4,1)S(1)}, pred[4,64,128]{2,1,0:T(8,128)(4,1)}, u32[]{:S(2)}) copy-start(pred[4,64,128]{2,1,0:T(8,128)(4,1)} %broadcast_and_fusion) | copy-start | bytes 98308
  46.4 27.1 %all-to-all-start.1 = ((f32[64,1,640]{2,1,0:T(1,128)}), f32[64,1,640]{2,1,0:T(1,128)S(1)}, u32[]{:S(2)}, u32[]{:S(2)}) async-start(f32[64,1,640]{2,1,0:T(1,128)} %copy.41), calls=%async_computation.1 | async-start | bytes 327680 | tf_op jit(solution)/shard_map/all_to_all | solution.py:72
  55.9 1.3 %copy-start.5 = (bf16[4,64,4,128]{3,1,2,0:T(8,128)(2,1)S(1)}, bf16[4,64,4,128]{3,1,2,0:T(8,128)(2,1)}, u32[]{:S(2)}) copy-start(bf16[4,64,4,128]{3,1,2,0:T(8,128)(2,1)} %copy.43) | copy-start | bytes 786436
  56.3 0.8 copy-start.18
  75.6 1.2 %copy-start.16 = (f32[4,256]{1,0:T(4,128)S(1)}, f32[4,256]{1,0:T(4,128)}, u32[]{:S(2)}) copy-start(f32[4,256]{1,0:T(4,128)} %get-tuple-element.16) | copy-start | bytes 12292
  75.6 1.2 %copy-start.3 = (f32[4,256,128]{1,2,0:T(8,128)S(1)}, f32[4,256,128]{1,2,0:T(8,128)}, u32[]{:S(2)}) copy-start(f32[4,256,128]{1,2,0:T(8,128)} %fusion.31) | copy-start | bytes 1572868
  78.4 0.7 copy-start.17

commit v11 on v9

--- a/solution.py
+++ b/solution.py
@@ -59,7 +59,7 @@
     return jnp.sum(jnp.where(keep, rows, jnp.float32(0.0)), axis=0)
 
 
-def exclusive_prefix(flat):
+def exclusive_prefix(flat, later):
     cores = lax.axis_size("cc")
     core = lax.axis_index("cc")
     chips = lax.axis_size("cx") * lax.axis_size("cz")
@@ -68,11 +68,12 @@
     halves = pair.reshape(cores, cores, -1)
     share = jnp.sum(lax.dynamic_index_in_dim(halves, core, 1, False), axis=0)
     recv = lax.all_to_all(share.reshape(chips, -1), ("cx", "cz"), 0, 0, tiled=True)
+    recv, later = lax.optimization_barrier((recv, later))
     lower = jnp.asarray(np.tril(np.ones((chips, chips), np.float32), -1))
     pref = jnp.dot(lower, recv, precision=HIGH, preferred_element_type=jnp.float32)
     back = lax.all_to_all(pref, ("cx", "cz"), 0, 0, tiled=True)
     shares = lax.all_gather(back.reshape(-1), "cc")
-    return shares.reshape(-1) + below_core
+    return shares.reshape(-1) + below_core, later
 
 
 def window_slab(query, key_ext, value_ext, start):
@@ -154,7 +155,7 @@
     quantum = size * 128
     padded = -(-used // quantum) * quantum
     packed = jnp.pad(packed, (0, padded - used))
-    prior = exclusive_prefix(packed)
+    prior, win_query = exclusive_prefix(packed, win_query)
     split = heads * feat * VDIM
     prior_state = prior[:split].reshape(heads, feat, VDIM)
     prior_norm = prior[split:used].reshape(heads, feat)

time: 92.3 us -> 90.1 us (0.976)
  starting transfers between devices: 37.5 us -> 34.2 us
  local copies, waits for them, and re-layouts: 11.8 us -> 8.66 us
  waiting for transfers between devices: 13.8 us -> 15.8 us
  matrix products: 7.17 us -> 8.78 us
    unnamed x39 -> x36, local copies, waits for them, and re-layouts: 6.22 us -> 2.59 us
    all_to_all x1, starting transfers between devices: 13 us -> 9.91 us  [exclusive_prefix(): back = lax.all_to_all(pref, ('cx', 'cz'), 0, 0, tiled=True)]
    all_to_all x1, waiting for transfers between devices: 1.92 us -> 5.04 us  [exclusive_prefix(): lax.all_to_all(share.reshape(chips, -1), ('cx', 'cz'), 0, 0, tiled=True)]
    sub x1, other arithmetic: 0.37 us -> 1.61 us  [window_slab(): prob = jnp.where(allowed, jnp.exp(scores - top), jnp.float32(0.0))]
    all_to_all x1, waiting for transfers between devices: 11.8 us -> 10.7 us  [exclusive_prefix(): back = lax.all_to_all(pref, ('cx', 'cz'), 0, 0, tiled=True)]
    reshape x1, local copies, waits for them, and re-layouts: 0.2 us -> 1.24 us  [body(): jnp.transpose(numer / denom[..., None], (1, 0, 2))]
where the time goes in v11:
time: 90.1 us; the launch traced here: 89.4 us
  starting transfers between devices  34.2 us (38%)
  waiting for transfers between devices  15.8 us (18%)
  blocking collectives  14.3 us (16%)
  matrix products  8.78 us (10%)
  local copies, waits for them, and re-layouts  8.66 us (10%)
  other arithmetic  7.19 us (8%)
    all_to_all x1, starting transfers between devices, exclusive_prefix(): lax.all_to_all(share.reshape(chips, -1), ('cx', 'cz'), 0, 0, tiled=True)  18.9 us
    all_to_all x1, waiting for transfers between devices, exclusive_prefix(): back = lax.all_to_all(pref, ('cx', 'cz'), 0, 0, tiled=True)  10.7 us
    all_gather x1, blocking collectives, body(): lax.all_gather(jnp.sum(mixed * mixed, axis=-1), 'head')  9.99 us
    all_to_all x1, starting transfers between devices, exclusive_prefix(): back = lax.all_to_all(pref, ('cx', 'cz'), 0, 0, tiled=True)  9.91 us
    ppermute x2, starting transfers between devices, passed_along(): return lax.ppermute(shard, axis, pairs)  5.39 us
    all_to_all x1, waiting for transfers between devices, exclusive_prefix(): lax.all_to_all(share.reshape(chips, -1), ('cx', 'cz'), 0, 0, tiled=True)  5.04 us
    unnamed x36, local copies, waits for them, and re-layouts  2.59 us
    all_gather x1, blocking collectives, exclusive_prefix(): pair = lax.all_gather(flat, 'cc')  2.28 us
  transfers between devices with their start and end apart: 4, of which 2 were waited for; matrix products, arithmetic and copies ran while one was open for 15% of the time, Pallas kernels for 0%

profile of v11, /device:TPU:6, one launch (start us, length us, event | category | flops | bytes accessed | tf_op | source)
XLA Modules:
  0.0 89.4 jit_solution(8019577137719872911)
XLA Ops:
  0.0 0.8 convert_multiply_fusion
  0.9 0.2 fusion.65
  1.1 0.4 copy-done.9
  1.6 0.3 fusion.4
  1.8 0.3 fusion.25
  2.2 0.3 fusion.27
  2.5 0.3 convolution_add_fusion.1
  2.8 0.1 reshape.157
  2.9 2.3 %all-gather = f32[163840]{0:T(1024)S(1)} all-gather(f32[81920]{0:T(1024)S(1)} %select_maximum_fusion), channel_id=2, replica_groups=mesh['cx'=4,'cz'=16,'cc'=2,'head'=4] {'cc'}, dimensions={0}, use_global_device_ids=true | all-gather | bytes 983040 | tf_op jit(solution)/shard_map/all_gather | solution.py:66
  5.2 0.4 reshape.158
  5.6 1.3 %dynamic-slice_reduce_fusion = f32[40960]{0:T(1024)} fusion(f32[2,2,40960]{2,1,0:T(2,128)S(1)} %reshape.158, s32[]{:T(128)S(6)} %select_n.20), kind=kLoop, calls=%fused_computation.53 | loop fusion | flops 40960 | bytes 491524 | tf_op jit(solution)/shard_map/reduce_sum | solution.py:69
  6.9 18.9 %all-to-all-start = ((f32[64,1,640]{2,1,0:T(1,128)}), f32[64,1,640]{2,1,0:T(1,128)S(1)}, u32[]{:S(2)}, u32[]{:S(2)}) async-start(f32[64,1,640]{2,1,0:T(1,128)} %bitcast.11), calls=%async_computation | async-start | bytes 327680 | tf_op jit(solution)/shard_map/all_to_all | solution.py:70
  25.9 0.6 slice.40
  26.5 1.9 %collective-permute-start.1 = (bf16[64,512]{1,0:T(8,128)(2,1)}, bf16[64,512]{1,0:T(8,128)(2,1)S(1)}, u32[]{:S(2)}, u32[]{:S(2)}) collective-permute-start(bf16[64,512]{1,0:T(8,128)(2,1)} %slice.40), channel_id=1, source_target_pairs={{0,4},{4,8},{8,12},{12,16},{16,20},{20,24},{24,28},{28,32},{32,36}... | collective-permute-start | bytes 196616 | tf_op jit(solution)/shard_map/ppermute | solution.py:24
  28.4 3.5 %collective-permute-start = (bf16[64,512]{1,0:T(8,128)(2,1)S(1)}, bf16[64,512]{1,0:T(8,128)(2,1)S(1)}, u32[]{:S(2)}, u32[]{:S(2)}) collective-permute-start(bf16[64,512]{1,0:T(8,128)(2,1)S(1)} %slice.38), channel_id=1, source_target_pairs={{0,4},{4,8},{8,12},{12,16},{16,20},{20,24},{24,28},{28,32},{32,36}... | collective-permute-start | bytes 196616 | tf_op jit(solution)/shard_map/ppermute | solution.py:24
  32.0 0.1 add_compare_fusion
  32.1 0.1 fusion.47
  32.2 0.6 copy-done.5
  32.7 0.2 fusion.64
  33.0 0.3 fusion.2
  33.2 1.1 %fusion.62 = (f32[4,256]{1,0:T(4,128)}, bf16[4,256,256]{1,2,0:T(8,128)(2,1)S(1)}) fusion(bf16[256,4,16]{0,2,1:T(8,128)(2,1)S(1)} %bitcast.94, bf16[256,4,16]{0,2,1:T(8,128)(2,1)S(1)} %bitcast.91, pred[256,256]{0,1:T(8,128)(4,1)S(1)} %iota_compare_fusion.1), kind=kOutput, calls=%fused_computation.93 | convolution fusion | flops 10484736 | bytes 659456 | tf_op jit(solution)/shard_map/thf,shf->hts/dot_general | solution.py:119
  34.4 1.1 %fusion.22 = f32[4,256,128]{1,2,0:T(8,128)} fusion(bf16[4,256,256]{1,2,0:T(8,128)(2,1)S(1)} %get-tuple-element.15, bf16[256,512]{1,0:T(8,128)(2,1)S(1)} %copy-done), kind=kOutput, calls=%fused_computation.41 | convolution fusion | flops 67108864 | bytes 1310720 | tf_op jit(solution)/shard_map/hts,shv->htv/dot_general | solution.py:124
  35.4 0.6 broadcast_and_fusion
  36.1 0.4 reshape.169
  36.5 1.0 %select_reduce_fusion.1 = f32[81920]{0:T(1024)S(1)} fusion(f32[2,81920]{1,0:T(2,128)S(1)} %reshape.169, pred[2]{0:T(512)(128)(4,1)S(1)} %iota_compare_fusion.4), kind=kLoop, calls=%fused_computation.23 | loop fusion | flops 245760 | bytes 983042 | tf_op jit(solution)/shard_map/reduce_sum | solution.py:59
  37.7 0.8 copy.62
  38.5 5.0 %all-to-all-done = f32[64,1,640]{2,1,0:T(1,128)S(1)} async-done(((f32[64,1,640]{2,1,0:T(1,128)}), f32[64,1,640]{2,1,0:T(1,128)S(1)}, u32[]{:S(2)}, u32[]{:S(2)}) %all-to-all-start) | async-done | bytes 163872 | tf_op jit(solution)/shard_map/all_to_all | solution.py:70
  43.5 0.3 convolution_bitcast_fusion.1
  43.8 0.8 copy.60
  44.7 9.9 %all-to-all-start.1 = ((f32[64,1,640]{2,1,0:T(1,128)}), f32[64,1,640]{2,1,0:T(1,128)S(1)}, u32[]{:S(2)}, u32[]{:S(2)}) async-start(f32[64,1,640]{2,1,0:T(1,128)} %copy.60), calls=%async_computation.1 | async-start | bytes 327680 | tf_op jit(solution)/shard_map/all_to_all | solution.py:74
  54.9 0.8 copy.61
  55.7 0.2 copy-done.6
  56.0 1.3 %convolution_multiply_fusion.2 = f32[4,4,64,128]{3,2,1,0:T(8,128)} fusion(bf16[4,64,4,128]{3,1,2,0:T(8,128)(2,1)S(1)} %copy.64, bf16[4,64,4,128]{3,1,2,0:T(8,128)(2,1)S(1)} %copy.63, bf16[4,64,4,128]{3,2,1,0:T(4,128)(2,1)S(1)} %reshape.165), kind=kOutput, calls=%fused_computation.15 | convolution fusion | flops 34734080 | bytes 1310720 | tf_op jit(solution)/shard_map/bihe,bjhe->bhij/dot_general | solution.py:98
  57.2 1.6 %fusion.63 = f32[4,4,64]{2,1,0:T(4,128)S(1)} fusion(f32[4,4,64,128]{3,2,1,0:T(8,128)} %convolution_multiply_fusion.2, pred[4,64,128]{2,1,0:T(8,128)(4,1)S(1)} %copy-done.10), kind=kOutput, calls=%fused_computation.94 | output fusion | flops 524415 | bytes 561152 | tf_op jit(solution)/shard_map/sub | solution.py:108
  58.9 1.6 %fusion.10 = f32[4,64,4,128]{3,1,2,0:T(8,128)S(1)} fusion(bf16[4,64,4,128]{3,1,2,0:T(8,128)(2,1)S(1)} %copy-done.7, bf16[4,64,4,128]{3,1,2,0:T(8,128)(2,1)S(1)} %copy-done.8, f32[4,64,4]{1,2,0:T(4,128)S(1)} %bitcast.100, f32[4,4,64,128]{3,2,1,0:T(8,128)} %convolution_multiply_fusion.2, pred[4,64,128]{2,1,0:T(8,128)(4,1)S(1)} %copy-done.10), kind=kOutput, calls=%fused_computation.14 | convolution fusion | flops 35259520 | bytes 1609728 | tf_op jit(solution)/shard_map/bhij,bjhe->bihe/dot_general | solution.py:110
  60.4 0.3 copy.66
  60.8 10.7 %all-to-all-done.1 = f32[64,1,640]{2,1,0:T(1,128)S(1)} async-done(((f32[64,1,640]{2,1,0:T(1,128)}), f32[64,1,640]{2,1,0:T(1,128)S(1)}, u32[]{:S(2)}, u32[]{:S(2)}) %all-to-all-start.1) | async-done | bytes 163872 | tf_op jit(solution)/shard_map/all_to_all | solution.py:74
  71.5 2.0 %all-gather.2 = f32[2,1,40960]{2,1,0:T(1,128)S(1)} all-gather(f32[1,1,40960]{2,1,0:T(1,128)S(1)} %bitcast.86), channel_id=1, replica_groups=mesh['cx'=4,'cz'=16,'cc'=2,'head'=4] {'cc'}, dimensions={0}, use_global_device_ids=true | all-gather | bytes 491520 | tf_op jit(solution)/shard_map/all_gather | solution.py:75
  73.6 0.1 reshape.185
  73.8 0.4 fusion.24
  74.1 0.3 copy-done.15
  74.4 0.4 copy-done.3
  74.8 1.5 %fusion.6 = f32[256,4,128]{0,2,1:T(8,128)} fusion(f32[4,256,128]{1,2,0:T(8,128)S(1)} %copy-done.3, f32[4,153,128]{2,1,0:T(8,128)S(1)} %reshape.160, f32[4,136,256]{2,1,0:T(8,128)S(1)} %fusion.2, f32[4,16,256]{2,1,0:T(8,128)S(1)} %convert_multiply_fusion.1, f32[153]{0:T(256)S(1)} %pad.16.clone, f32[256,4]{0,1:T(4,128)S(1)} %fusion.48), kind=kOutput, calls=%fused_computation.10 | convolution fusion | flops 120899584 | bytes 1989220 | tf_op jit(solution)/shard_map/hft,hfv->htv/dot_general | solution.py:173
  76.3 1.2 %copy.67 = f32[256,512]{1,0:T(8,128)S(1)} copy(f32[256,512]{0,1:T(8,128)} %bitcast.87) | data formatting | bytes 1048576 | tf_op jit(solution)/shard_map/reshape | solution.py:175
  77.6 0.7 copy-done.16
  78.2 0.3 multiply_reduce_fusion
  78.6 10.0 %all-gather.3 = f32[4,1,256]{2,1,0:T(1,128)S(1)} all-gather(f32[1,1,256]{2,1,0:T(1,128)S(1)} %bitcast.99), channel_id=3, replica_groups=mesh['cx'=4,'cz'=16,'cc'=2,'head'=4] {'head'}, dimensions={0}, use_global_device_ids=true | all-gather | bytes 5120 | tf_op jit(solution)/shard_map/all_gather | solution.py:177
  88.6 0.8 multiply_convert_fusion
  (60 shorter events, 0.9 us)
Async XLA Ops:
  0.0 2.2 %copy-start = (bf16[256,512]{1,0:T(8,128)(2,1)S(1)}, bf16[256,512]{1,0:T(8,128)(2,1)}, u32[]{:S(2)}) copy-start(bf16[256,512]{1,0:T(8,128)(2,1)} %param.15) | copy-start | bytes 786436
  0.0 0.8 copy-start.4
  0.0 0.8 copy-start.14
  0.9 0.7 copy-start.9
  5.6 20.2 %copy-start.2 = (bf16[256,512]{1,0:T(8,128)(2,1)S(1)}, bf16[256,512]{1,0:T(8,128)(2,1)}, u32[]{:S(2)}) copy-start(bf16[256,512]{1,0:T(8,128)(2,1)} %param.17) | copy-start | bytes 786436
  6.9 21.5 %copy-start.1 = (bf16[256,512]{1,0:T(8,128)(2,1)S(1)}, bf16[256,512]{1,0:T(8,128)(2,1)}, u32[]{:S(2)}) copy-start(bf16[256,512]{1,0:T(8,128)(2,1)} %param.18) | copy-start | bytes 786436
  6.9 36.6 %all-to-all-start = ((f32[64,1,640]{2,1,0:T(1,128)}), f32[64,1,640]{2,1,0:T(1,128)S(1)}, u32[]{:S(2)}, u32[]{:S(2)}) async-start(f32[64,1,640]{2,1,0:T(1,128)} %bitcast.11), calls=%async_computation | async-start | bytes 327680 | tf_op jit(solution)/shard_map/all_to_all | solution.py:70
  26.5 28.1 %collective-permute-start.1 = (bf16[64,512]{1,0:T(8,128)(2,1)}, bf16[64,512]{1,0:T(8,128)(2,1)S(1)}, u32[]{:S(2)}, u32[]{:S(2)}) collective-permute-start(bf16[64,512]{1,0:T(8,128)(2,1)} %slice.40), channel_id=1, source_target_pairs={{0,4},{4,8},{8,12},{12,16},{16,20},{20,24},{24,28},{28,32},{32,36}... | collective-permute-start | bytes 196616 | tf_op jit(solution)/shard_map/ppermute | solution.py:24
  28.4 3.8 %copy-start.13 = (bf16[136,16,1]{0,1,2:T(8,128)(2,1)S(1)}, bf16[136,16,1]{0,1,2:T(8,128)(2,1)}, u32[]{:S(2)}) copy-start(bf16[136,16,1]{0,1,2:T(8,128)(2,1)} %constant.75) | copy-start | bytes 13060
  28.4 10.0 %collective-permute-start = (bf16[64,512]{1,0:T(8,128)(2,1)S(1)}, bf16[64,512]{1,0:T(8,128)(2,1)S(1)}, u32[]{:S(2)}, u32[]{:S(2)}) collective-permute-start(bf16[64,512]{1,0:T(8,128)(2,1)S(1)} %slice.38), channel_id=1, source_target_pairs={{0,4},{4,8},{8,12},{12,16},{16,20},{20,24},{24,28},{28,32},{32,36}... | collective-permute-start | bytes 196616 | tf_op jit(solution)/shard_map/ppermute | solution.py:24
  32.0 0.8 copy-start.5
  34.4 1.1 %copy-start.12 = (bf16[3,512]{1,0:T(4,128)(2,1)S(1)}, bf16[3,512]{1,0:T(4,128)(2,1)}, u32[]{:S(2)}) copy-start(bf16[3,512]{1,0:T(4,128)(2,1)} %param.19) | copy-start | bytes 9220
  38.5 5.1 %copy-start.11 = (f32[64,64]{1,0:T(8,128)S(1)}, f32[64,64]{1,0:T(8,128)}, u32[]{:S(2)}) copy-start(f32[64,64]{1,0:T(8,128)} %constant.72.clone) | copy-start | bytes 49156
  44.7 26.9 %all-to-all-start.1 = ((f32[64,1,640]{2,1,0:T(1,128)}), f32[64,1,640]{2,1,0:T(1,128)S(1)}, u32[]{:S(2)}, u32[]{:S(2)}) async-start(f32[64,1,640]{2,1,0:T(1,128)} %copy.60), calls=%async_computation.1 | async-start | bytes 327680 | tf_op jit(solution)/shard_map/all_to_all | solution.py:74
  54.9 1.0 %copy-start.6 = (bf16[256,512]{1,0:T(8,128)(2,1)S(1)}, bf16[256,512]{1,0:T(8,128)(2,1)}, u32[]{:S(2)}) copy-start(bf16[256,512]{1,0:T(8,128)(2,1)} %param.16) | copy-start | bytes 786436
  56.0 1.3 %copy-start.10 = (pred[4,64,128]{2,1,0:T(8,128)(4,1)S(1)}, pred[4,64,128]{2,1,0:T(8,128)(4,1)}, u32[]{:S(2)}) copy-start(pred[4,64,128]{2,1,0:T(8,128)(4,1)} %broadcast_and_fusion) | copy-start | bytes 98308
  57.2 1.6 %copy-start.7 = (bf16[4,64,4,128]{3,1,2,0:T(8,128)(2,1)S(1)}, bf16[4,64,4,128]{3,1,2,0:T(8,128)(2,1)}, u32[]{:S(2)}) copy-start(bf16[4,64,4,128]{3,1,2,0:T(8,128)(2,1)} %copy.62) | copy-start | bytes 786436
  57.2 1.6 %copy-start.8 = (bf16[4,64,4,128]{3,1,2,0:T(8,128)(2,1)S(1)}, bf16[4,64,4,128]{3,1,2,0:T(8,128)(2,1)}, u32[]{:S(2)}) copy-start(bf16[4,64,4,128]{3,1,2,0:T(8,128)(2,1)} %copy.61) | copy-start | bytes 786436
  73.7 0.7 copy-start.15
  73.7 1.0 %copy-start.3 = (f32[4,256,128]{1,2,0:T(8,128)S(1)}, f32[4,256,128]{1,2,0:T(8,128)}, u32[]{:S(2)}) copy-start(f32[4,256,128]{1,2,0:T(8,128)} %fusion.22) | copy-start | bytes 1572868
  77.6 0.7 copy-start.16

commit v12 on v7

--- a/solution.py
+++ b/solution.py
@@ -58,7 +58,7 @@
     return jnp.sum(jnp.where(keep, rows, jnp.float32(0.0)), axis=0)
 
 
-def exclusive_prefix(flat):
+def exclusive_prefix(flat, later):
     cores = lax.axis_size("cc")
     core = lax.axis_index("cc")
     chips = lax.axis_size("cx") * lax.axis_size("cz")
@@ -67,11 +67,12 @@
     chip = jnp.sum(pair, axis=0)
     share = lax.dynamic_index_in_dim(chip.reshape(cores, -1), core, 0, False)
     recv = lax.all_to_all(share.reshape(chips, -1), ("cx", "cz"), 0, 0, tiled=True)
+    recv, later = lax.optimization_barrier((recv, later))
     lower = jnp.asarray(np.tril(np.ones((chips, chips), np.float32), -1))
     pref = jnp.dot(lower, recv, precision=HIGH, preferred_element_type=jnp.float32)
     back = lax.all_to_all(pref, ("cx", "cz"), 0, 0, tiled=True)
     shares = lax.all_gather(back.reshape(-1), "cc")
-    return shares.reshape(-1) + below_core
+    return shares.reshape(-1) + below_core, later
 
 
 def window_slab(query, key_ext, value_ext, start):
@@ -154,7 +155,7 @@
     quantum = size * 128
     padded = -(-used // quantum) * quantum
     packed = jnp.pad(packed, (0, padded - used))
-    prior = exclusive_prefix(packed)
+    prior, win_query = exclusive_prefix(packed, win_query)
     split = heads * feat * VDIM
     prior_state = prior[:split].reshape(heads, feat, VDIM)
     prior_norm = prior[split:used].reshape(heads, feat)

time: 88.1 us -> 87.3 us (level)
  local copies, waits for them, and re-layouts: 8.89 us -> 8 us
    unnamed x31 -> x26, local copies, waits for them, and re-layouts: 1.82 us -> 0.59 us
    div x1, local copies, waits for them, and re-layouts: 0.34 us -> 1.38 us  [window_slab(): out = out / jnp.transpose(total, (0, 2, 1))[..., None]]
    dot_general x1, matrix products: 1.4 us -> 0.45 us  [window_slab(): jnp.einsum('bihe,bjhe->bhij', qb, keys, preferred_element_type=jnp.float32)]
where the time goes in v12:
time: 87.3 us; the launch traced here: 86.7 us
  starting transfers between devices  31.5 us (36%)
  waiting for transfers between devices  18.4 us (21%)
  blocking collectives  14.3 us (16%)
  matrix products  8.63 us (10%)
  local copies, waits for them, and re-layouts  8 us (9%)
  other arithmetic  5.53 us (6%)
    all_to_all x1, starting transfers between devices, exclusive_prefix(): lax.all_to_all(share.reshape(chips, -1), ('cx', 'cz'), 0, 0, tiled=True)  18.9 us
    all_to_all x1, waiting for transfers between devices, exclusive_prefix(): back = lax.all_to_all(pref, ('cx', 'cz'), 0, 0, tiled=True)  10.7 us
    all_gather x1, blocking collectives, body(): lax.all_gather(jnp.sum(mixed * mixed, axis=-1), 'head')  9.99 us
    all_to_all x1, starting transfers between devices, exclusive_prefix(): back = lax.all_to_all(pref, ('cx', 'cz'), 0, 0, tiled=True)  7.15 us
    all_to_all x1, waiting for transfers between devices, exclusive_prefix(): lax.all_to_all(share.reshape(chips, -1), ('cx', 'cz'), 0, 0, tiled=True)  6.46 us
    ppermute x2, starting transfers between devices, passed_along(): return lax.ppermute(shard, axis, pairs)  5.39 us
    all_gather x1, blocking collectives, exclusive_prefix(): pair = lax.all_gather(flat, 'cc')  2.28 us
    dot_general x1, matrix products, window_slab(): jnp.einsum('bhij,bjhe->bihe', prob.astype(jnp.bfloat16), vals, preferred_...  2.21 us
  transfers between devices with their start and end apart: 4, of which 3 were waited for; matrix products, arithmetic and copies ran while one was open for 13% of the time, Pallas kernels for 0%

profile of v12, /device:TPU:6, one launch (start us, length us, event | category | flops | bytes accessed | tf_op | source)
XLA Modules:
  0.0 86.7 jit_solution(14772459204032301038)
XLA Ops:
  0.0 0.8 convert_bitcast_fusion
  0.8 0.8 broadcast_multiply_fusion
  1.6 0.1 multiply_multiply_fusion
  1.8 1.0 %fusion.58 = (f32[4,153]{1,0:T(4,128)S(1)}, f32[4,256,153]{1,2,0:T(8,128)S(1)}) fusion(f32[153,273,1]{1,0,2:T(8,128)S(1)} %copy-done.6, f32[4,256,256]{2,1,0:T(8,128)S(1)} %bitcast.81, f32[4,16,256]{2,1,0:T(8,128)S(1)} %broadcast_multiply_fusion, f32[273]{0:T(512)S(1)} %pad.16.clone), kind=kOutput, calls=%fused_computation.88 | convolution fusion | flops 257343904 | bytes 1911416 | tf_op jit(solution)/shard_map/cf,hft->hct/dot_general | solution.py:53
  2.8 0.3 fusion.33
  3.2 0.1 reshape.174
  3.3 2.3 %all-gather = f32[163840]{0:T(1024)S(1)} all-gather(f32[81920]{0:T(1024)S(1)} %select_maximum_fusion), channel_id=2, replica_groups=mesh['cx'=4,'cz'=16,'cc'=2,'head'=4] {'cc'}, dimensions={0}, use_global_device_ids=true | all-gather | bytes 983040 | tf_op jit(solution)/shard_map/all_gather | solution.py:65
  5.6 0.4 reshape.186
  6.0 1.7 %select_reduce_fusion.1 = (f32[81920]{0:T(1024)S(1)}, f32[81920]{0:T(1024)S(1)}) fusion(f32[2,81920]{1,0:T(2,128)S(1)} %reshape.186, pred[2]{0:T(512)(128)(4,1)S(1)} %iota_compare_fusion.4), kind=kLoop, calls=%fused_computation.26 | loop fusion | flops 327680 | bytes 1310722 | tf_op jit(solution)/shard_map/reduce_sum | solution.py:58
  7.7 0.2 reshape.175
  7.9 0.8 constant_dynamic-slice_fusion
  8.8 18.9 %all-to-all-start = ((f32[64,1,640]{2,1,0:T(1,128)}), f32[64,1,640]{2,1,0:T(1,128)S(1)}, u32[]{:S(2)}, u32[]{:S(2)}) async-start(f32[64,1,640]{2,1,0:T(1,128)} %bitcast.8), calls=%async_computation | async-start | bytes 327680 | tf_op jit(solution)/shard_map/all_to_all | solution.py:69
  27.7 1.9 %collective-permute-start.1 = (bf16[64,512]{1,0:T(8,128)(2,1)S(1)}, bf16[64,512]{1,0:T(8,128)(2,1)S(1)}, u32[]{:S(2)}, u32[]{:S(2)}) collective-permute-start(bf16[64,512]{1,0:T(8,128)(2,1)S(1)} %slice.40), channel_id=1, source_target_pairs={{0,4},{4,8},{8,12},{12,16},{16,20},{20,24},{24,28},{28,32},{32,36}... | collective-permute-start | bytes 196616 | tf_op jit(solution)/shard_map/ppermute | solution.py:24
  29.7 0.6 slice.38
  30.3 3.5 %collective-permute-start = (bf16[64,512]{1,0:T(8,128)(2,1)}, bf16[64,512]{1,0:T(8,128)(2,1)S(1)}, u32[]{:S(2)}, u32[]{:S(2)}) collective-permute-start(bf16[64,512]{1,0:T(8,128)(2,1)} %slice.38), channel_id=1, source_target_pairs={{0,4},{4,8},{8,12},{12,16},{16,20},{20,24},{24,28},{28,32},{32,36}... | collective-permute-start | bytes 196616 | tf_op jit(solution)/shard_map/ppermute | solution.py:24
  33.9 0.1 multiply_multiply_fusion.1
  34.0 0.5 fusion.59
  34.5 1.1 %fusion.30 = f32[4,256,128]{1,2,0:T(8,128)} fusion(bf16[4,256,256]{1,2,0:T(8,128)(2,1)S(1)} %get-tuple-element.19, bf16[256,512]{1,0:T(8,128)(2,1)S(1)} %copy-done), kind=kOutput, calls=%fused_computation.45 | convolution fusion | flops 67108864 | bytes 1310720 | tf_op jit(solution)/shard_map/hts,shv->htv/dot_general | solution.py:123
  35.6 0.1 add_compare_fusion
  35.7 0.1 fusion.45
  35.8 0.8 fusion.7
  36.7 0.1 reshape.184
  36.7 0.1 reshape.181
  36.9 0.8 copy.43
  37.6 1.2 %collective-permute-done = bf16[64,512]{1,0:T(8,128)(2,1)S(1)} collective-permute-done((bf16[64,512]{1,0:T(8,128)(2,1)}, bf16[64,512]{1,0:T(8,128)(2,1)S(1)}, u32[]{:S(2)}, u32[]{:S(2)}) %collective-permute-start) | collective-permute-done | bytes 65568 | tf_op jit(solution)/shard_map/ppermute | solution.py:24
  38.8 6.5 %all-to-all-done = f32[64,1,640]{2,1,0:T(1,128)S(1)} async-done(((f32[64,1,640]{2,1,0:T(1,128)}), f32[64,1,640]{2,1,0:T(1,128)S(1)}, u32[]{:S(2)}, u32[]{:S(2)}) %all-to-all-start) | async-done | bytes 163872 | tf_op jit(solution)/shard_map/all_to_all | solution.py:69
  45.3 0.3 convolution_bitcast_fusion.1
  45.6 0.8 copy.41
  46.4 7.1 %all-to-all-start.1 = ((f32[64,1,640]{2,1,0:T(1,128)}), f32[64,1,640]{2,1,0:T(1,128)S(1)}, u32[]{:S(2)}, u32[]{:S(2)}) async-start(f32[64,1,640]{2,1,0:T(1,128)} %copy.41), calls=%async_computation.1 | async-start | bytes 327680 | tf_op jit(solution)/shard_map/all_to_all | solution.py:73
  53.7 0.1 convert_element_type.23
  53.7 0.1 reshape.183
  53.9 0.1 reshape.180
  54.0 0.8 copy.42
  54.8 0.4 convolution_multiply_fusion
  55.3 0.4 fusion.60
  55.7 2.2 %fusion.6 = f32[4,64,4,128]{3,1,2,0:T(8,128)} fusion(bf16[4,64,4,128]{3,1,2,0:T(8,128)(2,1)} %copy.43, bf16[4,64,4,128]{3,1,2,0:T(8,128)(2,1)} %copy.42, f32[4,64,4]{1,2,0:T(4,128)S(1)} %bitcast.93, f32[4,4,64,128]{3,2,1,0:T(8,128)S(1)} %convolution_multiply_fusion, pred[4,64,128]{2,1,0:T(8,128)(4,1)S(1)} %broadcast_and_fusion), kind=kOutput, calls=%fused_computation.8 | convolution fusion | flops 35259520 | bytes 1609728 | tf_op jit(solution)/shard_map/bhij,bjhe->bihe/dot_general | solution.py:109
  57.9 1.4 %copy.47 = f32[4,64,4,128]{3,2,1,0:T(4,128)S(1)} copy(f32[4,64,4,128]{3,1,2,0:T(8,128)} %fusion.6) | data formatting | bytes 1048576 | tf_op jit(solution)/shard_map/div | solution.py:112
  59.3 10.7 %all-to-all-done.1 = f32[64,1,640]{2,1,0:T(1,128)S(1)} async-done(((f32[64,1,640]{2,1,0:T(1,128)}), f32[64,1,640]{2,1,0:T(1,128)S(1)}, u32[]{:S(2)}, u32[]{:S(2)}) %all-to-all-start.1) | async-done | bytes 163872 | tf_op jit(solution)/shard_map/all_to_all | solution.py:73
  70.0 2.0 %all-gather.2 = f32[2,1,40960]{2,1,0:T(1,128)S(1)} all-gather(f32[1,1,40960]{2,1,0:T(1,128)S(1)} %bitcast.85), channel_id=1, replica_groups=mesh['cx'=4,'cz'=16,'cc'=2,'head'=4] {'cc'}, dimensions={0}, use_global_device_ids=true | all-gather | bytes 491520 | tf_op jit(solution)/shard_map/all_gather | solution.py:74
  72.1 0.1 reshape.200
  72.2 0.7 reshape.177
  72.9 0.3 fusion.61
  73.2 1.6 %fusion.2 = f32[256,4,128]{0,2,1:T(8,128)S(1)} fusion(f32[4,256,128]{1,2,0:T(8,128)S(1)} %copy-done.3, f32[4,256,153]{1,2,0:T(8,128)S(1)} %fusion.7, f32[4,153,128]{2,1,0:T(8,128)} %reshape.177, f32[256,4]{0,1:T(4,128)S(1)} %fusion.46), kind=kOutput, calls=%fused_computation.4 | convolution fusion | flops 120586240 | bytes 1992704 | tf_op jit(solution)/shard_map/hft,hfv->htv/dot_general | solution.py:173
  74.9 0.2 copy.48
  75.1 0.5 copy-done.11
  75.6 0.3 multiply_reduce_fusion
  75.9 10.0 %all-gather.3 = f32[4,1,256]{2,1,0:T(1,128)S(1)} all-gather(f32[1,1,256]{2,1,0:T(1,128)S(1)} %bitcast.92), channel_id=3, replica_groups=mesh['cx'=4,'cz'=16,'cc'=2,'head'=4] {'head'}, dimensions={0}, use_global_device_ids=true | all-gather | bytes 5120 | tf_op jit(solution)/shard_map/all_gather | solution.py:177
  85.9 0.8 multiply_convert_fusion
  (50 shorter events, 0.6 us)
Async XLA Ops:
  0.0 2.8 %copy-start = (bf16[256,512]{1,0:T(8,128)(2,1)S(1)}, bf16[256,512]{1,0:T(8,128)(2,1)}, u32[]{:S(2)}) copy-start(bf16[256,512]{1,0:T(8,128)(2,1)} %param.13) | copy-start | bytes 786436
  0.0 1.8 %copy-start.6 = (f32[153,273,1]{1,0,2:T(8,128)S(1)}, f32[153,273,1]{1,0,2:T(8,128)}, u32[]{:S(2)}) copy-start(f32[153,273,1]{1,0,2:T(8,128)} %constant.73) | copy-start | bytes 501232
  6.0 21.7 %copy-start.2 = (bf16[256,512]{1,0:T(8,128)(2,1)S(1)}, bf16[256,512]{1,0:T(8,128)(2,1)}, u32[]{:S(2)}) copy-start(bf16[256,512]{1,0:T(8,128)(2,1)} %param.15) | copy-start | bytes 786436
  7.7 21.9 %copy-start.1 = (bf16[256,512]{1,0:T(8,128)(2,1)S(1)}, bf16[256,512]{1,0:T(8,128)(2,1)}, u32[]{:S(2)}) copy-start(bf16[256,512]{1,0:T(8,128)(2,1)} %param.16) | copy-start | bytes 786436
  7.7 26.0 %copy-start.7 = (bf16[256,64]{0,1:T(8,128)(2,1)S(1)}, bf16[256,64]{0,1:T(8,128)(2,1)}, u32[]{:S(2)}) copy-start(bf16[256,64]{0,1:T(8,128)(2,1)} %param.11) | copy-start | bytes 98308
  8.8 25.2 %copy-start.8 = (bf16[256,64]{0,1:T(8,128)(2,1)S(1)}, bf16[256,64]{0,1:T(8,128)(2,1)}, u32[]{:S(2)}) copy-start(bf16[256,64]{0,1:T(8,128)(2,1)} %param.12) | copy-start | bytes 98308
  8.8 36.5 %all-to-all-start = ((f32[64,1,640]{2,1,0:T(1,128)}), f32[64,1,640]{2,1,0:T(1,128)S(1)}, u32[]{:S(2)}, u32[]{:S(2)}) async-start(f32[64,1,640]{2,1,0:T(1,128)} %bitcast.8), calls=%async_computation | async-start | bytes 327680 | tf_op jit(solution)/shard_map/all_to_all | solution.py:69
  27.7 25.9 %collective-permute-start.1 = (bf16[64,512]{1,0:T(8,128)(2,1)S(1)}, bf16[64,512]{1,0:T(8,128)(2,1)S(1)}, u32[]{:S(2)}, u32[]{:S(2)}) collective-permute-start(bf16[64,512]{1,0:T(8,128)(2,1)S(1)} %slice.40), channel_id=1, source_target_pairs={{0,4},{4,8},{8,12},{12,16},{16,20},{20,24},{24,28},{28,32},{32,36}... | collective-permute-start | bytes 196616 | tf_op jit(solution)/shard_map/ppermute | solution.py:24
  30.3 8.5 %collective-permute-start = (bf16[64,512]{1,0:T(8,128)(2,1)}, bf16[64,512]{1,0:T(8,128)(2,1)S(1)}, u32[]{:S(2)}, u32[]{:S(2)}) collective-permute-start(bf16[64,512]{1,0:T(8,128)(2,1)} %slice.38), channel_id=1, source_target_pairs={{0,4},{4,8},{8,12},{12,16},{16,20},{20,24},{24,28},{28,32},{32,36}... | collective-permute-start | bytes 196616 | tf_op jit(solution)/shard_map/ppermute | solution.py:24
  34.5 1.2 %copy-start.5 = (f32[153,273,1]{1,0,2:T(8,128)S(1)}, f32[153,273,1]{1,0,2:T(8,128)}, u32[]{:S(2)}) copy-start(f32[153,273,1]{1,0,2:T(8,128)} %constant.72) | copy-start | bytes 501232
  35.6 1.1 %copy-start.10 = (bf16[3,512]{1,0:T(4,128)(2,1)S(1)}, bf16[3,512]{1,0:T(4,128)(2,1)}, u32[]{:S(2)}) copy-start(bf16[3,512]{1,0:T(4,128)(2,1)} %param.17) | copy-start | bytes 9220
  36.8 8.5 %copy-start.9 = (f32[64,64]{1,0:T(8,128)S(1)}, f32[64,64]{1,0:T(8,128)}, u32[]{:S(2)}) copy-start(f32[64,64]{1,0:T(8,128)} %constant.69.clone) | copy-start | bytes 49156
  46.4 23.6 %all-to-all-start.1 = ((f32[64,1,640]{2,1,0:T(1,128)}), f32[64,1,640]{2,1,0:T(1,128)S(1)}, u32[]{:S(2)}, u32[]{:S(2)}) async-start(f32[64,1,640]{2,1,0:T(1,128)} %copy.41), calls=%async_computation.1 | async-start | bytes 327680 | tf_op jit(solution)/shard_map/all_to_all | solution.py:73
  53.8 1.0 %copy-start.4 = (bf16[256,512]{1,0:T(8,128)(2,1)S(1)}, bf16[256,512]{1,0:T(8,128)(2,1)}, u32[]{:S(2)}) copy-start(bf16[256,512]{1,0:T(8,128)(2,1)} %param.14) | copy-start | bytes 786436
  72.1 1.2 %copy-start.3 = (f32[4,256,128]{1,2,0:T(8,128)S(1)}, f32[4,256,128]{1,2,0:T(8,128)}, u32[]{:S(2)}) copy-start(f32[4,256,128]{1,2,0:T(8,128)} %fusion.30) | copy-start | bytes 1572868
  74.9 0.7 copy-start.11

commit v13 on v12

--- a/solution.py
+++ b/solution.py
@@ -149,16 +149,21 @@
     feat = phi_k.shape[1]
     local_state = jnp.einsum("hft,thv->hfv", phi_k, values32, precision=THREE)
     local_norm = jnp.sum(phi_k, axis=-1)
-    size = lax.axis_size("cc") * lax.axis_size("cx") * lax.axis_size("cz")
-    packed = jnp.concatenate([local_state.reshape(-1), local_norm.reshape(-1)])
-    used = packed.shape[0]
-    quantum = size * 128
-    padded = -(-used // quantum) * quantum
-    packed = jnp.pad(packed, (0, padded - used))
+    norm_rows = -(-feat // VDIM)
+    rows = -(-(feat + norm_rows) // 8) * 8
+    norm_block = jnp.pad(local_norm, ((0, 0), (0, norm_rows * VDIM - feat)))
+    packed = jnp.concatenate(
+        [
+            local_state,
+            norm_block.reshape(heads, norm_rows, VDIM),
+            jnp.zeros((heads, rows - feat - norm_rows, VDIM), jnp.float32),
+        ],
+        axis=1,
+    ).reshape(-1)
     prior, win_query = exclusive_prefix(packed, win_query)
-    split = heads * feat * VDIM
-    prior_state = prior[:split].reshape(heads, feat, VDIM)
-    prior_norm = prior[split:used].reshape(heads, feat)
+    blocks = prior.reshape(heads, rows, VDIM)
+    prior_state = blocks[:, :feat, :]
+    prior_norm = blocks[:, feat : feat + norm_rows, :].reshape(heads, -1)[:, :feat]
     start = lax.axis_index(CTX) * count
     rims = passed_along((win_key[count - WIN :], win_value[count - WIN :]), CTX, 1)
     key_ext = jnp.concatenate([rims[0], win_key], axis=0)

time: 87.3 us -> 91.7 us (1.050)
  waiting for transfers between devices: 18.4 us -> 11.4 us
  starting transfers between devices: 31.5 us -> 37.1 us
  local copies, waits for them, and re-layouts: 8 us -> 10.7 us
  other arithmetic: 5.53 us -> 8.03 us
    all_to_all x1, starting transfers between devices: 7.15 us -> 12.6 us  [exclusive_prefix(): back = lax.all_to_all(pref, ('cx', 'cz'), 0, 0, tiled=True)]
    all_to_all x1, waiting for transfers between devices: 6.46 us -> 1.62 us  [exclusive_prefix(): lax.all_to_all(share.reshape(chips, -1), ('cx', 'cz'), 0, 0, tiled=True)]
    unnamed x26 -> x32, local copies, waits for them, and re-layouts: 0.59 us -> 3.16 us
    ppermute x2, waiting for transfers between devices: 1.17 us -> 0.01 us  [passed_along(): return lax.ppermute(shard, axis, pairs)]
    dot_general x1, matrix products: 1.65 us -> 0.67 us  [body(): jnp.einsum('hft,hfv->htv', phi_q, prior_state, precision=THREE)]
    all_to_all x1, waiting for transfers between devices: 10.7 us -> 9.78 us  [exclusive_prefix(): back = lax.all_to_all(pref, ('cx', 'cz'), 0, 0, tiled=True)]
    reduce_sum x0 -> x1, other arithmetic: none -> 0.92 us  [exclusive_prefix(): chip = jnp.sum(pair, axis=0)]
  transfers between devices with their start and end apart: 4 -> 4, of which waited for: 3 -> 2; matrix products, arithmetic and copies ran while one was open for 13% -> 21% of each run, Pallas kernels for 0% -> 0%
where the time goes in v13:
time: 91.7 us; the launch traced here: 91 us
  starting transfers between devices  37.1 us (40%)
  blocking collectives  14.4 us (16%)
  waiting for transfers between devices  11.4 us (12%)
  local copies, waits for them, and re-layouts  10.7 us (12%)
  matrix products  8.94 us (10%)
  other arithmetic  8.03 us (9%)
    all_to_all x1, starting transfers between devices, exclusive_prefix(): lax.all_to_all(share.reshape(chips, -1), ('cx', 'cz'), 0, 0, tiled=True)  19.1 us
    all_to_all x1, starting transfers between devices, exclusive_prefix(): back = lax.all_to_all(pref, ('cx', 'cz'), 0, 0, tiled=True)  12.6 us
    all_gather x1, blocking collectives, body(): lax.all_gather(jnp.sum(mixed * mixed, axis=-1), 'head')  9.99 us
    all_to_all x1, waiting for transfers between devices, exclusive_prefix(): back = lax.all_to_all(pref, ('cx', 'cz'), 0, 0, tiled=True)  9.78 us
    ppermute x2, starting transfers between devices, passed_along(): return lax.ppermute(shard, axis, pairs)  5.38 us
    unnamed x32, local copies, waits for them, and re-layouts  3.16 us
    dot_general x2, matrix products, compact_features(): return jnp.einsum('cf,hft->hct', fold, full, precision=THREE)  2.53 us
    all_gather x1, blocking collectives, exclusive_prefix(): pair = lax.all_gather(flat, 'cc')  2.28 us
  transfers between devices with their start and end apart: 4, of which 2 were waited for; matrix products, arithmetic and copies ran while one was open for 21% of the time, Pallas kernels for 0%

profile of v13, /device:TPU:6, one launch (start us, length us, event | category | flops | bytes accessed | tf_op | source)
XLA Modules:
  0.0 91.0 jit_solution(12423969635430680292)
XLA Ops:
  0.0 0.8 convert_bitcast_fusion
  0.8 0.8 broadcast_multiply_fusion
  1.6 0.1 multiply_multiply_fusion
  1.8 1.0 %fusion.62 = (f32[4,153]{1,0:T(4,128)S(1)}, f32[4,256,153]{1,2,0:T(8,128)S(1)}) fusion(f32[153,273,1]{1,0,2:T(8,128)S(1)} %copy-done.7, f32[4,256,256]{2,1,0:T(8,128)S(1)} %bitcast.92, f32[4,16,256]{2,1,0:T(8,128)S(1)} %broadcast_multiply_fusion, f32[273]{0:T(512)S(1)} %pad.17.clone), kind=kOutput, calls=%fused_computation.94 | convolution fusion | flops 257343904 | bytes 1911416 | tf_op jit(solution)/shard_map/cf,hft->hct/dot_general | solution.py:53
  2.8 0.1 pad.13.clone
  2.9 0.3 fusion.35
  3.3 0.1 maximum_maximum_fusion
  3.4 2.3 %all-gather.1 = f32[2,1,81920]{2,1,0:T(1,128)S(1)} all-gather(f32[1,1,81920]{2,1,0:T(1,128)S(1)} %bitcast.95), channel_id=1, replica_groups=mesh['cx'=4,'cz'=16,'cc'=2,'head'=4] {'cc'}, dimensions={0}, use_global_device_ids=true | all-gather | bytes 983040 | tf_op jit(solution)/shard_map/all_gather | solution.py:65
  5.6 0.9 %reduce_sum.66 = f32[81920]{0:T(1024)S(1)} reduce(f32[2,1,81920]{2,1,0:T(1,128)S(1)} %all-gather.1, f32[]{:T(128)} %constant.28.clone.1), dimensions={0,1}, to_apply=%region_1.2 | reduce | flops 81920 | bytes 983044 | tf_op jit(solution)/shard_map/reduce_sum | solution.py:67
  6.6 0.2 reshape.171
  6.8 0.8 constant_dynamic-slice_fusion
  7.6 19.1 %all-to-all-start = ((f32[64,1,640]{2,1,0:T(1,128)}), f32[64,1,640]{2,1,0:T(1,128)}, u32[]{:S(2)}, u32[]{:S(2)}) async-start(f32[64,1,640]{2,1,0:T(1,128)} %bitcast.9), calls=%async_computation | async-start | bytes 327680 | tf_op jit(solution)/shard_map/all_to_all | solution.py:69
  26.7 0.6 slice.44
  27.3 1.9 %collective-permute-start.1 = (bf16[64,512]{1,0:T(8,128)(2,1)}, bf16[64,512]{1,0:T(8,128)(2,1)S(1)}, u32[]{:S(2)}, u32[]{:S(2)}) collective-permute-start(bf16[64,512]{1,0:T(8,128)(2,1)} %slice.44), channel_id=1, source_target_pairs={{0,4},{4,8},{8,12},{12,16},{16,20},{20,24},{24,28},{28,32},{32,36}... | collective-permute-start | bytes 196616 | tf_op jit(solution)/shard_map/ppermute | solution.py:24
  29.2 0.6 slice.42
  29.9 3.5 %collective-permute-start = (bf16[64,512]{1,0:T(8,128)(2,1)}, bf16[64,512]{1,0:T(8,128)(2,1)}, u32[]{:S(2)}, u32[]{:S(2)}) collective-permute-start(bf16[64,512]{1,0:T(8,128)(2,1)} %slice.42), channel_id=1, source_target_pairs={{0,4},{4,8},{8,12},{12,16},{16,20},{20,24},{24,28},{28,32},{32,36}... | collective-permute-start | bytes 196616 | tf_op jit(solution)/shard_map/ppermute | solution.py:24
  33.3 0.6 iota_compare_fusion.3
  34.0 0.1 multiply_multiply_fusion.1
  34.2 1.1 %fusion.63 = (f32[4,256]{1,0:T(4,128)}, bf16[4,256,256]{1,2,0:T(8,128)(2,1)S(1)}) fusion(bf16[256,4,16]{0,2,1:T(8,128)(2,1)S(1)} %bitcast.100, bf16[256,4,16]{0,2,1:T(8,128)(2,1)S(1)} %bitcast.101, pred[256,256]{0,1:T(8,128)(4,1)S(1)} %iota_compare_fusion), kind=kOutput, calls=%fused_computation.95 | convolution fusion | flops 10484736 | bytes 659456 | tf_op jit(solution)/shard_map/thf,shf->hts/dot_general | solution.py:118
  35.3 1.1 %fusion.31 = f32[4,256,128]{1,2,0:T(8,128)} fusion(bf16[4,256,256]{1,2,0:T(8,128)(2,1)S(1)} %get-tuple-element.17, bf16[256,512]{1,0:T(8,128)(2,1)S(1)} %copy-done), kind=kOutput, calls=%fused_computation.46 | convolution fusion | flops 67108864 | bytes 1310720 | tf_op jit(solution)/shard_map/hts,shv->htv/dot_general | solution.py:123
  36.4 0.1 add_compare_fusion
  36.4 0.1 fusion.47
  36.6 1.5 %fusion.7 = f32[4,256,153]{1,2,0:T(8,128)S(1)} fusion(f32[153,273,1]{1,0,2:T(8,128)S(1)} %copy-done.6, f32[4,256,256]{2,1,0:T(8,128)S(1)} %bitcast.91, f32[4,16,256]{2,1,0:T(8,128)S(1)} %broadcast_multiply_fusion.1, f32[273]{0:T(512)} %copy-done.11), kind=kOutput, calls=%fused_computation.10 | convolution fusion | flops 257187840 | bytes 1908968 | tf_op jit(solution)/shard_map/cf,hft->hct/dot_general | solution.py:53
  38.1 0.8 fusion.61
  38.9 1.9 %fusion.18 = f32[81920]{0:T(1024)S(1)} fusion(f32[2,1,81920]{2,1,0:T(1,128)S(1)} %all-gather.1, pred[2]{0:T(512)(128)(4,1)} %iota_compare_fusion.3), kind=kLoop, calls=%fused_computation.27 | loop fusion | flops 245760 | bytes 983042 | tf_op jit(solution)/shard_map/reduce_sum | solution.py:58
  41.0 0.8 copy.32
  41.8 0.8 constant_dynamic-update-slice_fusion.1
  42.7 1.6 %all-to-all-done = f32[64,1,640]{2,1,0:T(1,128)} async-done(((f32[64,1,640]{2,1,0:T(1,128)}), f32[64,1,640]{2,1,0:T(1,128)}, u32[]{:S(2)}, u32[]{:S(2)}) %all-to-all-start) | async-done | bytes 163872 | tf_op jit(solution)/shard_map/all_to_all | solution.py:69
  44.3 0.9 %copy.64 = f32[64,1,640]{2,0,1:T(8,128)S(1)} copy(f32[64,1,640]{2,1,0:T(1,128)} %all-to-all-done) | data formatting | bytes 327680
  45.2 0.3 convolution_bitcast_fusion.1
  45.5 0.8 copy.30
  46.4 12.6 %all-to-all-start.1 = ((f32[64,1,640]{2,1,0:T(1,128)}), f32[64,1,640]{2,1,0:T(1,128)S(1)}, u32[]{:S(2)}, u32[]{:S(2)}) async-start(f32[64,1,640]{2,1,0:T(1,128)} %copy.30), calls=%async_computation.1 | async-start | bytes 327680 | tf_op jit(solution)/shard_map/all_to_all | solution.py:73
  59.0 0.7 pad_maximum_fusion
  59.8 0.9 copy-done.3
  60.9 0.8 copy.31
  61.7 0.5 convolution_multiply_fusion
  62.2 0.4 fusion.64
  62.5 2.2 %fusion.6 = f32[4,64,4,128]{3,1,2,0:T(8,128)} fusion(bf16[4,64,4,128]{3,1,2,0:T(8,128)(2,1)} %copy.32, bf16[4,64,4,128]{3,1,2,0:T(8,128)(2,1)} %copy.31, f32[4,64,4]{1,2,0:T(4,128)S(1)} %bitcast.107, f32[4,4,64,128]{3,2,1,0:T(8,128)S(1)} %convolution_multiply_fusion, pred[4,64,128]{2,1,0:T(8,128)(4,1)S(1)} %broadcast_and_fusion), kind=kOutput, calls=%fused_computation.8 | convolution fusion | flops 35259520 | bytes 1609728 | tf_op jit(solution)/shard_map/bhij,bjhe->bihe/dot_general | solution.py:109
  64.7 1.4 %copy.36 = f32[4,64,4,128]{3,2,1,0:T(4,128)S(1)} copy(f32[4,64,4,128]{3,1,2,0:T(8,128)} %fusion.6) | data formatting | bytes 1048576 | tf_op jit(solution)/shard_map/div | solution.py:112
  66.1 9.8 %all-to-all-done.1 = f32[64,1,640]{2,1,0:T(1,128)S(1)} async-done(((f32[64,1,640]{2,1,0:T(1,128)}), f32[64,1,640]{2,1,0:T(1,128)S(1)}, u32[]{:S(2)}, u32[]{:S(2)}) %all-to-all-start.1) | async-done | bytes 163872 | tf_op jit(solution)/shard_map/all_to_all | solution.py:73
  75.9 2.2 %all-gather.2 = f32[2,1,40960]{2,1,0:T(1,128)S(1)} all-gather(f32[1,1,40960]{2,1,0:T(1,128)S(1)} %bitcast.98), channel_id=1, replica_groups=mesh['cx'=4,'cz'=16,'cc'=2,'head'=4] {'cc'}, dimensions={0}, use_global_device_ids=true | all-gather | bytes 491520 | tf_op jit(solution)/shard_map/all_gather | solution.py:74
  78.2 0.3 fusion.49
  78.5 0.7 fusion.2
  79.1 0.2 copy.37
  79.3 0.5 copy-done.13
  79.8 0.3 multiply_reduce_fusion
  80.1 10.0 %all-gather.3 = f32[4,1,256]{2,1,0:T(1,128)S(1)} all-gather(f32[1,1,256]{2,1,0:T(1,128)S(1)} %bitcast.106), channel_id=2, replica_groups=mesh['cx'=4,'cz'=16,'cc'=2,'head'=4] {'head'}, dimensions={0}, use_global_device_ids=true | all-gather | bytes 5120 | tf_op jit(solution)/shard_map/all_gather | solution.py:182
  90.2 0.8 multiply_convert_fusion
  (55 shorter events, 0.8 us)
Async XLA Ops:
  0.0 2.9 %copy-start = (bf16[256,512]{1,0:T(8,128)(2,1)S(1)}, bf16[256,512]{1,0:T(8,128)(2,1)}, u32[]{:S(2)}) copy-start(bf16[256,512]{1,0:T(8,128)(2,1)} %param.13) | copy-start | bytes 786436
  0.0 1.8 %copy-start.7 = (f32[153,273,1]{1,0,2:T(8,128)S(1)}, f32[153,273,1]{1,0,2:T(8,128)}, u32[]{:S(2)}) copy-start(f32[153,273,1]{1,0,2:T(8,128)} %constant.74) | copy-start | bytes 501232
  1.7 1.0 %copy-start.11 = (f32[273]{0:T(512)}, f32[273]{0:T(512)S(1)}, u32[]{:S(2)}) copy-start(f32[273]{0:T(512)S(1)} %pad.17.clone) | copy-start | bytes 3280
  5.6 21.1 %copy-start.2 = (bf16[256,512]{1,0:T(8,128)(2,1)S(1)}, bf16[256,512]{1,0:T(8,128)(2,1)}, u32[]{:S(2)}) copy-start(bf16[256,512]{1,0:T(8,128)(2,1)} %param.15) | copy-start | bytes 786436
  5.6 23.6 %copy-start.1 = (bf16[256,512]{1,0:T(8,128)(2,1)S(1)}, bf16[256,512]{1,0:T(8,128)(2,1)}, u32[]{:S(2)}) copy-start(bf16[256,512]{1,0:T(8,128)(2,1)} %param.16) | copy-start | bytes 786436
  5.6 28.3 %copy-start.8 = (bf16[256,64]{0,1:T(8,128)(2,1)S(1)}, bf16[256,64]{0,1:T(8,128)(2,1)}, u32[]{:S(2)}) copy-start(bf16[256,64]{0,1:T(8,128)(2,1)} %param.11) | copy-start | bytes 98308
  7.6 26.6 %copy-start.9 = (bf16[256,64]{0,1:T(8,128)(2,1)S(1)}, bf16[256,64]{0,1:T(8,128)(2,1)}, u32[]{:S(2)}) copy-start(bf16[256,64]{0,1:T(8,128)(2,1)} %param.12) | copy-start | bytes 98308
  7.6 36.7 %all-to-all-start = ((f32[64,1,640]{2,1,0:T(1,128)}), f32[64,1,640]{2,1,0:T(1,128)}, u32[]{:S(2)}, u32[]{:S(2)}) async-start(f32[64,1,640]{2,1,0:T(1,128)} %bitcast.9), calls=%async_computation | async-start | bytes 327680 | tf_op jit(solution)/shard_map/all_to_all | solution.py:69
  27.3 31.7 %collective-permute-start.1 = (bf16[64,512]{1,0:T(8,128)(2,1)}, bf16[64,512]{1,0:T(8,128)(2,1)S(1)}, u32[]{:S(2)}, u32[]{:S(2)}) collective-permute-start(bf16[64,512]{1,0:T(8,128)(2,1)} %slice.44), channel_id=1, source_target_pairs={{0,4},{4,8},{8,12},{12,16},{16,20},{20,24},{24,28},{28,32},{32,36}... | collective-permute-start | bytes 196616 | tf_op jit(solution)/shard_map/ppermute | solution.py:24
  29.9 11.9 %collective-permute-start = (bf16[64,512]{1,0:T(8,128)(2,1)}, bf16[64,512]{1,0:T(8,128)(2,1)}, u32[]{:S(2)}, u32[]{:S(2)}) collective-permute-start(bf16[64,512]{1,0:T(8,128)(2,1)} %slice.42), channel_id=1, source_target_pairs={{0,4},{4,8},{8,12},{12,16},{16,20},{20,24},{24,28},{28,32},{32,36}... | collective-permute-start | bytes 196616 | tf_op jit(solution)/shard_map/ppermute | solution.py:24
  35.3 1.3 %copy-start.6 = (f32[153,273,1]{1,0,2:T(8,128)S(1)}, f32[153,273,1]{1,0,2:T(8,128)}, u32[]{:S(2)}) copy-start(f32[153,273,1]{1,0,2:T(8,128)} %constant.73) | copy-start | bytes 501232
  41.0 4.2 %copy-start.10 = (f32[64,64]{1,0:T(8,128)S(1)}, f32[64,64]{1,0:T(8,128)}, u32[]{:S(2)}) copy-start(f32[64,64]{1,0:T(8,128)} %constant.70.clone) | copy-start | bytes 49156
  46.4 29.5 %all-to-all-start.1 = ((f32[64,1,640]{2,1,0:T(1,128)}), f32[64,1,640]{2,1,0:T(1,128)S(1)}, u32[]{:S(2)}, u32[]{:S(2)}) async-start(f32[64,1,640]{2,1,0:T(1,128)} %copy.30), calls=%async_computation.1 | async-start | bytes 327680 | tf_op jit(solution)/shard_map/all_to_all | solution.py:73
  59.7 0.9 %copy-start.3 = (bf16[256,512]{1,0:T(8,128)(2,1)S(1)}, bf16[256,512]{1,0:T(8,128)(2,1)}, u32[]{:S(2)}) copy-start(bf16[256,512]{1,0:T(8,128)(2,1)} %pad_maximum_fusion) | copy-start | bytes 786436
  60.7 1.0 %copy-start.5 = (bf16[256,512]{1,0:T(8,128)(2,1)S(1)}, bf16[256,512]{1,0:T(8,128)(2,1)}, u32[]{:S(2)}) copy-start(bf16[256,512]{1,0:T(8,128)(2,1)} %param.14) | copy-start | bytes 786436
  75.9 2.5 %copy-start.12 = (f32[4,256]{1,0:T(4,128)S(1)}, f32[4,256]{1,0:T(4,128)}, u32[]{:S(2)}) copy-start(f32[4,256]{1,0:T(4,128)} %get-tuple-element.16) | copy-start | bytes 12292
  75.9 2.5 %copy-start.4 = (f32[4,256,128]{1,2,0:T(8,128)S(1)}, f32[4,256,128]{1,2,0:T(8,128)}, u32[]{:S(2)}) copy-start(f32[4,256,128]{1,2,0:T(8,128)} %fusion.31) | copy-start | bytes 1572868
  79.1 0.7 copy-start.13

commit v14 on v12

--- a/solution.py
+++ b/solution.py
@@ -63,11 +63,11 @@
     core = lax.axis_index("cc")
     chips = lax.axis_size("cx") * lax.axis_size("cz")
     pair = lax.all_gather(flat, "cc")
-    below_core = masked_rows(pair, core)
     chip = jnp.sum(pair, axis=0)
     share = lax.dynamic_index_in_dim(chip.reshape(cores, -1), core, 0, False)
     recv = lax.all_to_all(share.reshape(chips, -1), ("cx", "cz"), 0, 0, tiled=True)
-    recv, later = lax.optimization_barrier((recv, later))
+    recv, later, pair = lax.optimization_barrier((recv, later, pair))
+    below_core = masked_rows(pair, core)
     lower = jnp.asarray(np.tril(np.ones((chips, chips), np.float32), -1))
     pref = jnp.dot(lower, recv, precision=HIGH, preferred_element_type=jnp.float32)
     back = lax.all_to_all(pref, ("cx", "cz"), 0, 0, tiled=True)

time: 87.3 us -> 94.9 us (1.087)
  waiting for transfers between devices: 18.4 us -> 10.3 us
  starting transfers between devices: 31.5 us -> 38.7 us
  local copies, waits for them, and re-layouts: 8 us -> 12.4 us
  other arithmetic: 5.53 us -> 8.22 us
  matrix products: 8.63 us -> 9.64 us
    all_to_all x1, starting transfers between devices: 7.15 us -> 14.4 us  [exclusive_prefix(): back = lax.all_to_all(pref, ('cx', 'cz'), 0, 0, tiled=True)]
    all_to_all x1, waiting for transfers between devices: 6.46 us -> 0.01 us  [exclusive_prefix(): lax.all_to_all(share.reshape(chips, -1), ('cx', 'cz'), 0, 0, tiled=True)]
    unnamed x26 -> x32, local copies, waits for them, and re-layouts: 0.59 us -> 4.46 us
    ppermute x2, waiting for transfers between devices: 1.17 us -> 0.01 us  [passed_along(): return lax.ppermute(shard, axis, pairs)]
    dot_general x1, matrix products: 1.65 us -> 0.66 us  [body(): jnp.einsum('hft,hfv->htv', phi_q, prior_state, precision=THREE)]
    dot_general x2, matrix products: 1.86 us -> 2.83 us  [compact_features(): return jnp.einsum('cf,hft->hct', fold, full, precision=THREE)]
  transfers between devices with their start and end apart: 4 -> 4, of which waited for: 3 -> 1; matrix products, arithmetic and copies ran while one was open for 13% -> 19% of each run, Pallas kernels for 0% -> 0%
where the time goes in v14:
time: 94.9 us; the launch traced here: 94.1 us
  starting transfers between devices  38.7 us (41%)
  blocking collectives  14.3 us (15%)
  local copies, waits for them, and re-layouts  12.4 us (13%)
  waiting for transfers between devices  10.3 us (11%)
  matrix products  9.64 us (10%)
  other arithmetic  8.22 us (9%)
    all_to_all x1, starting transfers between devices, exclusive_prefix(): lax.all_to_all(share.reshape(chips, -1), ('cx', 'cz'), 0, 0, tiled=True)  19 us
    all_to_all x1, starting transfers between devices, exclusive_prefix(): back = lax.all_to_all(pref, ('cx', 'cz'), 0, 0, tiled=True)  14.4 us
    all_to_all x1, waiting for transfers between devices, exclusive_prefix(): back = lax.all_to_all(pref, ('cx', 'cz'), 0, 0, tiled=True)  10.3 us
    all_gather x1, blocking collectives, body(): lax.all_gather(jnp.sum(mixed * mixed, axis=-1), 'head')  9.99 us
    ppermute x2, starting transfers between devices, passed_along(): return lax.ppermute(shard, axis, pairs)  5.38 us
    unnamed x32, local copies, waits for them, and re-layouts  4.46 us
    dot_general x2, matrix products, compact_features(): return jnp.einsum('cf,hft->hct', fold, full, precision=THREE)  2.83 us
    dot_general x1, matrix products, window_slab(): jnp.einsum('bhij,bjhe->bihe', prob.astype(jnp.bfloat16), vals, preferred_...  2.46 us
  transfers between devices with their start and end apart: 4, of which 1 were waited for; matrix products, arithmetic and copies ran while one was open for 19% of the time, Pallas kernels for 0%

profile of v14, /device:TPU:6, one launch (start us, length us, event | category | flops | bytes accessed | tf_op | source)
XLA Modules:
  0.0 94.1 jit_solution(18365260861932119756)
XLA Ops:
  0.0 0.8 convert_bitcast_fusion
  0.8 0.8 broadcast_multiply_fusion
  1.6 0.1 multiply_multiply_fusion
  1.8 1.0 %fusion.58 = (f32[4,153]{1,0:T(4,128)S(1)}, f32[4,256,153]{1,2,0:T(8,128)S(1)}) fusion(f32[153,273,1]{1,0,2:T(8,128)S(1)} %copy-done.8, f32[4,256,256]{2,1,0:T(8,128)S(1)} %bitcast.81, f32[4,16,256]{2,1,0:T(8,128)S(1)} %broadcast_multiply_fusion, f32[273]{0:T(512)S(1)} %pad.16.clone), kind=kOutput, calls=%fused_computation.88 | convolution fusion | flops 257343904 | bytes 1911416 | tf_op jit(solution)/shard_map/cf,hft->hct/dot_general | solution.py:53
  2.8 0.3 fusion.33
  3.3 2.3 %all-gather = f32[163840]{0:T(1024)S(1)} all-gather(f32[81920]{0:T(1024)S(1)} %select_maximum_fusion), channel_id=2, replica_groups=mesh['cx'=4,'cz'=16,'cc'=2,'head'=4] {'cc'}, dimensions={0}, use_global_device_ids=true | all-gather | bytes 983040 | tf_op jit(solution)/shard_map/all_gather | solution.py:65
  5.6 0.4 reshape.186
  6.0 0.8 reduce_sum.64
  6.8 0.2 reshape.175
  7.0 0.8 constant_dynamic-slice_fusion
  7.8 19.0 %all-to-all-start = ((f32[64,1,640]{2,1,0:T(1,128)}), f32[64,1,640]{2,1,0:T(1,128)}, u32[]{:S(2)}, u32[]{:S(2)}) async-start(f32[64,1,640]{2,1,0:T(1,128)} %bitcast.8), calls=%async_computation | async-start | bytes 327680 | tf_op jit(solution)/shard_map/all_to_all | solution.py:68
  26.8 0.6 slice.40
  27.4 1.9 %collective-permute-start.1 = (bf16[64,512]{1,0:T(8,128)(2,1)}, bf16[64,512]{1,0:T(8,128)(2,1)}, u32[]{:S(2)}, u32[]{:S(2)}) collective-permute-start(bf16[64,512]{1,0:T(8,128)(2,1)} %slice.40), channel_id=1, source_target_pairs={{0,4},{4,8},{8,12},{12,16},{16,20},{20,24},{24,28},{28,32},{32,36}... | collective-permute-start | bytes 196616 | tf_op jit(solution)/shard_map/ppermute | solution.py:24
  29.3 0.6 slice.38
  29.9 3.5 %collective-permute-start = (bf16[64,512]{1,0:T(8,128)(2,1)}, bf16[64,512]{1,0:T(8,128)(2,1)}, u32[]{:S(2)}, u32[]{:S(2)}) collective-permute-start(bf16[64,512]{1,0:T(8,128)(2,1)} %slice.38), channel_id=1, source_target_pairs={{0,4},{4,8},{8,12},{12,16},{16,20},{20,24},{24,28},{28,32},{32,36}... | collective-permute-start | bytes 196616 | tf_op jit(solution)/shard_map/ppermute | solution.py:24
  33.4 0.6 broadcast_multiply_fusion.1
  34.1 0.7 iota_compare_fusion.1
  34.9 0.1 multiply_multiply_fusion.1
  35.0 0.7 copy-done.10
  35.7 1.3 %fusion.59 = (f32[4,256]{1,0:T(4,128)S(1)}, bf16[4,256,256]{1,2,0:T(8,128)(2,1)S(1)}) fusion(bf16[256,4,16]{0,2,1:T(8,128)(2,1)} %bitcast.87, bf16[256,4,16]{0,2,1:T(8,128)(2,1)} %bitcast.88, pred[256,256]{0,1:T(8,128)(4,1)S(1)} %copy-done.10), kind=kOutput, calls=%fused_computation.89 | convolution fusion | flops 10484736 | bytes 659456 | tf_op jit(solution)/shard_map/thf,shf->hts/dot_general | solution.py:118
  37.0 1.1 %fusion.30 = f32[4,256,128]{1,2,0:T(8,128)} fusion(bf16[4,256,256]{1,2,0:T(8,128)(2,1)S(1)} %get-tuple-element.19, bf16[256,512]{1,0:T(8,128)(2,1)S(1)} %copy-done), kind=kOutput, calls=%fused_computation.45 | convolution fusion | flops 67108864 | bytes 1310720 | tf_op jit(solution)/shard_map/hts,shv->htv/dot_general | solution.py:123
  38.1 0.8 copy.45
  39.0 0.8 copy.43
  39.7 0.6 broadcast_and_fusion
  40.4 1.8 %fusion.7 = f32[4,256,153]{1,2,0:T(8,128)S(1)} fusion(f32[153,273,1]{1,0,2:T(8,128)} %constant.72, f32[4,256,256]{2,1,0:T(8,128)S(1)} %bitcast.80, f32[4,16,256]{2,1,0:T(8,128)} %broadcast_multiply_fusion.1, f32[273]{0:T(512)S(1)} %pad.16.clone), kind=kOutput, calls=%fused_computation.10 | convolution fusion | flops 257187840 | bytes 1908968 | tf_op jit(solution)/shard_map/cf,hft->hct/dot_general | solution.py:53
  42.2 0.8 constant_dynamic-update-slice_fusion.1
  43.2 0.9 pad_maximum_fusion
  44.3 0.8 copy.42
  45.0 1.0 %copy.69 = f32[64,1,640]{2,0,1:T(8,128)S(1)} copy(f32[64,1,640]{2,1,0:T(1,128)} %all-to-all-done) | data formatting | bytes 327680
  46.0 0.3 convolution_bitcast_fusion.1
  46.3 0.8 copy.41
  47.2 14.4 %all-to-all-start.1 = ((f32[64,1,640]{2,1,0:T(1,128)}), f32[64,1,640]{2,1,0:T(1,128)S(1)}, u32[]{:S(2)}, u32[]{:S(2)}) async-start(f32[64,1,640]{2,1,0:T(1,128)} %copy.41), calls=%async_computation.1 | async-start | bytes 327680 | tf_op jit(solution)/shard_map/all_to_all | solution.py:73
  61.6 0.5 convolution_multiply_fusion
  62.1 0.8 copy-done.5
  62.9 0.4 fusion.60
  63.3 2.5 %fusion.6 = f32[4,64,4,128]{3,1,2,0:T(8,128)} fusion(bf16[4,64,4,128]{3,1,2,0:T(8,128)(2,1)S(1)} %copy-done.7, bf16[4,64,4,128]{3,1,2,0:T(8,128)(2,1)} %copy.42, f32[4,64,4]{1,2,0:T(4,128)S(1)} %bitcast.93, f32[4,4,64,128]{3,2,1,0:T(8,128)} %copy-done.5, pred[4,64,128]{2,1,0:T(8,128)(4,1)S(1)} %copy-done.11), kind=kOutput, calls=%fused_computation.8 | convolution fusion | flops 35259520 | bytes 1609728 | tf_op jit(solution)/shard_map/bhij,bjhe->bihe/dot_general | solution.py:109
  65.8 1.4 %copy.47 = f32[4,64,4,128]{3,2,1,0:T(4,128)S(1)} copy(f32[4,64,4,128]{3,1,2,0:T(8,128)} %fusion.6) | data formatting | bytes 1048576 | tf_op jit(solution)/shard_map/div | solution.py:112
  67.1 1.0 %select_reduce_fusion.1 = f32[81920]{0:T(1024)S(1)} fusion(f32[2,81920]{1,0:T(2,128)S(1)} %reshape.186, pred[2]{0:T(512)(128)(4,1)S(1)} %iota_compare_fusion.4), kind=kLoop, calls=%fused_computation.26 | loop fusion | flops 245760 | bytes 983042 | tf_op jit(solution)/shard_map/reduce_sum | solution.py:58
  68.1 10.3 %all-to-all-done.1 = f32[64,1,640]{2,1,0:T(1,128)S(1)} async-done(((f32[64,1,640]{2,1,0:T(1,128)}), f32[64,1,640]{2,1,0:T(1,128)S(1)}, u32[]{:S(2)}, u32[]{:S(2)}) %all-to-all-start.1) | async-done | bytes 163872 | tf_op jit(solution)/shard_map/all_to_all | solution.py:73
  78.5 2.0 %all-gather.2 = f32[2,1,40960]{2,1,0:T(1,128)S(1)} all-gather(f32[1,1,40960]{2,1,0:T(1,128)S(1)} %bitcast.85), channel_id=1, replica_groups=mesh['cx'=4,'cz'=16,'cc'=2,'head'=4] {'cc'}, dimensions={0}, use_global_device_ids=true | all-gather | bytes 491520 | tf_op jit(solution)/shard_map/all_gather | solution.py:74
  80.7 0.3 fusion.61
  81.0 0.6 copy-done.4
  81.6 0.7 fusion.2
  82.3 0.2 copy.48
  82.5 0.5 copy-done.14
  82.9 0.3 multiply_reduce_fusion
  83.2 10.0 %all-gather.3 = f32[4,1,256]{2,1,0:T(1,128)S(1)} all-gather(f32[1,1,256]{2,1,0:T(1,128)S(1)} %bitcast.92), channel_id=3, replica_groups=mesh['cx'=4,'cz'=16,'cc'=2,'head'=4] {'head'}, dimensions={0}, use_global_device_ids=true | all-gather | bytes 5120 | tf_op jit(solution)/shard_map/all_gather | solution.py:177
  93.3 0.8 multiply_convert_fusion
  (57 shorter events, 1.1 us)
Async XLA Ops:
  0.0 2.8 %copy-start = (bf16[256,512]{1,0:T(8,128)(2,1)S(1)}, bf16[256,512]{1,0:T(8,128)(2,1)}, u32[]{:S(2)}) copy-start(bf16[256,512]{1,0:T(8,128)(2,1)} %param.13) | copy-start | bytes 786436
  0.0 1.7 %copy-start.8 = (f32[153,273,1]{1,0,2:T(8,128)S(1)}, f32[153,273,1]{1,0,2:T(8,128)}, u32[]{:S(2)}) copy-start(f32[153,273,1]{1,0,2:T(8,128)} %constant.73) | copy-start | bytes 501232
  6.0 20.8 %copy-start.2 = (bf16[256,512]{1,0:T(8,128)(2,1)S(1)}, bf16[256,512]{1,0:T(8,128)(2,1)}, u32[]{:S(2)}) copy-start(bf16[256,512]{1,0:T(8,128)(2,1)} %param.15) | copy-start | bytes 786436
  6.0 23.3 %copy-start.1 = (bf16[256,512]{1,0:T(8,128)(2,1)S(1)}, bf16[256,512]{1,0:T(8,128)(2,1)}, u32[]{:S(2)}) copy-start(bf16[256,512]{1,0:T(8,128)(2,1)} %param.16) | copy-start | bytes 786436
  6.0 27.4 %copy-start.9 = (bf16[256,64]{0,1:T(8,128)(2,1)S(1)}, bf16[256,64]{0,1:T(8,128)(2,1)}, u32[]{:S(2)}) copy-start(bf16[256,64]{0,1:T(8,128)(2,1)} %param.11) | copy-start | bytes 98308
  7.8 37.3 %all-to-all-start = ((f32[64,1,640]{2,1,0:T(1,128)}), f32[64,1,640]{2,1,0:T(1,128)}, u32[]{:S(2)}, u32[]{:S(2)}) async-start(f32[64,1,640]{2,1,0:T(1,128)} %bitcast.8), calls=%async_computation | async-start | bytes 327680 | tf_op jit(solution)/shard_map/all_to_all | solution.py:68
  27.4 15.8 %collective-permute-start.1 = (bf16[64,512]{1,0:T(8,128)(2,1)}, bf16[64,512]{1,0:T(8,128)(2,1)}, u32[]{:S(2)}, u32[]{:S(2)}) collective-permute-start(bf16[64,512]{1,0:T(8,128)(2,1)} %slice.40), channel_id=1, source_target_pairs={{0,4},{4,8},{8,12},{12,16},{16,20},{20,24},{24,28},{28,32},{32,36}... | collective-permute-start | bytes 196616 | tf_op jit(solution)/shard_map/ppermute | solution.py:24
  29.9 12.3 %collective-permute-start = (bf16[64,512]{1,0:T(8,128)(2,1)}, bf16[64,512]{1,0:T(8,128)(2,1)}, u32[]{:S(2)}, u32[]{:S(2)}) collective-permute-start(bf16[64,512]{1,0:T(8,128)(2,1)} %slice.38), channel_id=1, source_target_pairs={{0,4},{4,8},{8,12},{12,16},{16,20},{20,24},{24,28},{28,32},{32,36}... | collective-permute-start | bytes 196616 | tf_op jit(solution)/shard_map/ppermute | solution.py:24
  34.9 0.8 copy-start.10
  39.7 2.4 %copy-start.13 = (bf16[3,512]{1,0:T(4,128)(2,1)S(1)}, bf16[3,512]{1,0:T(4,128)(2,1)}, u32[]{:S(2)}) copy-start(bf16[3,512]{1,0:T(4,128)(2,1)} %param.17) | copy-start | bytes 9220
  44.1 1.9 %copy-start.12 = (f32[64,64]{1,0:T(8,128)S(1)}, f32[64,64]{1,0:T(8,128)}, u32[]{:S(2)}) copy-start(f32[64,64]{1,0:T(8,128)} %constant.69.clone) | copy-start | bytes 49156
  44.3 17.2 %copy-start.6 = (bf16[256,512]{1,0:T(8,128)(2,1)S(1)}, bf16[256,512]{1,0:T(8,128)(2,1)}, u32[]{:S(2)}) copy-start(bf16[256,512]{1,0:T(8,128)(2,1)} %param.14) | copy-start | bytes 786436
  45.0 16.6 %copy-start.3 = (bf16[4,64,4,128]{3,1,2,0:T(8,128)(2,1)S(1)}, bf16[4,64,4,128]{3,1,2,0:T(8,128)(2,1)}, u32[]{:S(2)}) copy-start(bf16[4,64,4,128]{3,1,2,0:T(8,128)(2,1)} %copy.45) | copy-start | bytes 786436
  47.1 15.8 %copy-start.11 = (pred[4,64,128]{2,1,0:T(8,128)(4,1)S(1)}, pred[4,64,128]{2,1,0:T(8,128)(4,1)}, u32[]{:S(2)}) copy-start(pred[4,64,128]{2,1,0:T(8,128)(4,1)} %broadcast_and_fusion) | copy-start | bytes 98308
  47.2 31.3 %all-to-all-start.1 = ((f32[64,1,640]{2,1,0:T(1,128)}), f32[64,1,640]{2,1,0:T(1,128)S(1)}, u32[]{:S(2)}, u32[]{:S(2)}) async-start(f32[64,1,640]{2,1,0:T(1,128)} %copy.41), calls=%async_computation.1 | async-start | bytes 327680 | tf_op jit(solution)/shard_map/all_to_all | solution.py:73
  61.6 1.7 %copy-start.7 = (bf16[4,64,4,128]{3,1,2,0:T(8,128)(2,1)S(1)}, bf16[4,64,4,128]{3,1,2,0:T(8,128)(2,1)}, u32[]{:S(2)}) copy-start(bf16[4,64,4,128]{3,1,2,0:T(8,128)(2,1)} %copy.43) | copy-start | bytes 786436
  62.1 0.8 copy-start.5
  80.5 1.0 %copy-start.4 = (f32[4,256,128]{1,2,0:T(8,128)S(1)}, f32[4,256,128]{1,2,0:T(8,128)}, u32[]{:S(2)}) copy-start(f32[4,256,128]{1,2,0:T(8,128)} %fusion.30) | copy-start | bytes 1572868
  82.2 0.7 copy-start.14

commit v15 on v12

--- a/solution.py
+++ b/solution.py
@@ -155,7 +155,7 @@
     quantum = size * 128
     padded = -(-used // quantum) * quantum
     packed = jnp.pad(packed, (0, padded - used))
-    prior, win_query = exclusive_prefix(packed, win_query)
+    prior, (win_query, lin_q_late, lin_k_late) = exclusive_prefix(packed, (win_query, queries, keys))
     split = heads * feat * VDIM
     prior_state = prior[:split].reshape(heads, feat, VDIM)
     prior_norm = prior[split:used].reshape(heads, feat)
@@ -169,7 +169,7 @@
     conv_out = jnp.zeros((count, value_ext.shape[1]), jnp.float32)
     for tap in range(TAPS):
         conv_out = conv_out + taps[tap][None, :] * value_f32[WIN - tap : WIN - tap + count]
-    inner_num, inner_den = inner_causal(queries, keys, values)
+    inner_num, inner_den = inner_causal(lin_q_late, lin_k_late, values)
     numer = inner_num + jnp.einsum("hft,hfv->htv", phi_q, prior_state, precision=THREE)
     denom = inner_den + jnp.einsum("hft,hf->ht", phi_q, prior_norm, precision=THREE)
     lin_out = jnp.transpose(numer / denom[..., None], (1, 0, 2)).reshape(count, heads * VDIM)

time: 87.3 us -> 90.6 us (1.038)
  waiting for transfers between devices: 18.4 us -> 12.5 us
  starting transfers between devices: 31.5 us -> 34.8 us
  other arithmetic: 5.53 us -> 8.12 us
  matrix products: 8.63 us -> 10.2 us
  local copies, waits for them, and re-layouts: 8 us -> 9.53 us
    all_to_all x1, starting transfers between devices: 7.15 us -> 10.7 us  [exclusive_prefix(): back = lax.all_to_all(pref, ('cx', 'cz'), 0, 0, tiled=True)]
    all_to_all x1, waiting for transfers between devices: 6.46 us -> 3.43 us  [exclusive_prefix(): lax.all_to_all(share.reshape(chips, -1), ('cx', 'cz'), 0, 0, tiled=True)]
    all_to_all x1, waiting for transfers between devices: 10.7 us -> 7.81 us  [exclusive_prefix(): back = lax.all_to_all(pref, ('cx', 'cz'), 0, 0, tiled=True)]
    sub x1, other arithmetic: 0.39 us -> 1.55 us  [window_slab(): prob = jnp.where(allowed, jnp.exp(scores - top), jnp.float32(0.0))]
  transfers between devices with their start and end apart: 4 -> 4, of which waited for: 3 -> 3; matrix products, arithmetic and copies ran while one was open for 13% -> 17% of each run, Pallas kernels for 0% -> 0%
where the time goes in v15:
time: 90.6 us; the launch traced here: 90 us
  starting transfers between devices  34.8 us (38%)
  blocking collectives  14.3 us (16%)
  waiting for transfers between devices  12.5 us (14%)
  matrix products  10.2 us (11%)
  local copies, waits for them, and re-layouts  9.53 us (11%)
  other arithmetic  8.12 us (9%)
    all_to_all x1, starting transfers between devices, exclusive_prefix(): lax.all_to_all(share.reshape(chips, -1), ('cx', 'cz'), 0, 0, tiled=True)  18.8 us
    all_to_all x1, starting transfers between devices, exclusive_prefix(): back = lax.all_to_all(pref, ('cx', 'cz'), 0, 0, tiled=True)  10.7 us
    all_gather x1, blocking collectives, body(): lax.all_gather(jnp.sum(mixed * mixed, axis=-1), 'head')  9.99 us
    all_to_all x1, waiting for transfers between devices, exclusive_prefix(): back = lax.all_to_all(pref, ('cx', 'cz'), 0, 0, tiled=True)  7.81 us
    ppermute x2, starting transfers between devices, passed_along(): return lax.ppermute(shard, axis, pairs)  5.38 us
    all_to_all x1, waiting for transfers between devices, exclusive_prefix(): lax.all_to_all(share.reshape(chips, -1), ('cx', 'cz'), 0, 0, tiled=True)  3.43 us
    dot_general x2, matrix products, compact_features(): return jnp.einsum('cf,hft->hct', fold, full, precision=THREE)  2.52 us
    dot_general x1, matrix products, window_slab(): jnp.einsum('bhij,bjhe->bihe', prob.astype(jnp.bfloat16), vals, preferred_...  2.35 us
  transfers between devices with their start and end apart: 4, of which 3 were waited for; matrix products, arithmetic and copies ran while one was open for 17% of the time, Pallas kernels for 0%

profile of v15, /device:TPU:6, one launch (start us, length us, event | category | flops | bytes accessed | tf_op | source)
XLA Modules:
  0.0 90.0 jit_solution(11759188743882735758)
XLA Ops:
  0.0 0.8 convert_bitcast_fusion.1
  0.8 0.8 broadcast_multiply_fusion.1
  1.6 0.1 multiply_multiply_fusion.1
  1.7 0.1 copy.53
  1.9 1.0 %fusion.53 = (f32[4,153]{1,0:T(4,128)S(1)}, f32[4,256,153]{1,2,0:T(8,128)S(1)}) fusion(f32[153,273,1]{1,0,2:T(8,128)S(1)} %copy-done.8, f32[4,256,256]{2,1,0:T(8,128)S(1)} %bitcast.68, f32[4,16,256]{2,1,0:T(8,128)S(1)} %broadcast_multiply_fusion.1, f32[273]{0:T(512)S(1)} %pad.16.clone), kind=kOutput, calls=%fused_computation.83 | convolution fusion | flops 257343904 | bytes 1911416 | tf_op jit(solution)/shard_map/cf,hft->hct/dot_general | solution.py:53
  2.9 0.3 fusion.56
  3.3 0.1 reshape.173
  3.4 2.3 %all-gather = f32[163840]{0:T(1024)S(1)} all-gather(f32[81920]{0:T(1024)S(1)} %select_maximum_fusion), channel_id=2, replica_groups=mesh['cx'=4,'cz'=16,'cc'=2,'head'=4] {'cc'}, dimensions={0}, use_global_device_ids=true | all-gather | bytes 983040 | tf_op jit(solution)/shard_map/all_gather | solution.py:65
  5.7 0.4 reshape.186
  6.1 1.7 %select_reduce_fusion.1 = (f32[81920]{0:T(1024)S(1)}, f32[81920]{0:T(1024)S(1)}) fusion(f32[2,81920]{1,0:T(2,128)S(1)} %reshape.186, pred[2]{0:T(512)(128)(4,1)S(1)} %iota_compare_fusion.4), kind=kLoop, calls=%fused_computation.26 | loop fusion | flops 327680 | bytes 1310722 | tf_op jit(solution)/shard_map/reduce_sum | solution.py:58
  7.9 0.2 reshape.174
  8.1 0.8 constant_dynamic-slice_fusion
  8.9 18.8 %all-to-all-start = ((f32[64,1,640]{2,1,0:T(1,128)}), f32[64,1,640]{2,1,0:T(1,128)S(1)}, u32[]{:S(2)}, u32[]{:S(2)}) async-start(f32[64,1,640]{2,1,0:T(1,128)} %bitcast.4), calls=%async_computation | async-start | bytes 327680 | tf_op jit(solution)/shard_map/all_to_all | solution.py:69
  27.7 0.6 slice.40
  28.3 1.9 %collective-permute-start.1 = (bf16[64,512]{1,0:T(8,128)(2,1)}, bf16[64,512]{1,0:T(8,128)(2,1)}, u32[]{:S(2)}, u32[]{:S(2)}) collective-permute-start(bf16[64,512]{1,0:T(8,128)(2,1)} %slice.40), channel_id=1, source_target_pairs={{0,4},{4,8},{8,12},{12,16},{16,20},{20,24},{24,28},{28,32},{32,36}... | collective-permute-start | bytes 196616 | tf_op jit(solution)/shard_map/ppermute | solution.py:24
  30.3 0.6 slice.38
  30.9 3.5 %collective-permute-start = (bf16[64,512]{1,0:T(8,128)(2,1)}, bf16[64,512]{1,0:T(8,128)(2,1)}, u32[]{:S(2)}, u32[]{:S(2)}) collective-permute-start(bf16[64,512]{1,0:T(8,128)(2,1)} %slice.38), channel_id=1, source_target_pairs={{0,4},{4,8},{8,12},{12,16},{16,20},{20,24},{24,28},{28,32},{32,36}... | collective-permute-start | bytes 196616 | tf_op jit(solution)/shard_map/ppermute | solution.py:24
  34.6 0.1 multiply_multiply_fusion
  34.8 0.1 add_compare_fusion
  34.9 0.1 fusion.40
  35.0 0.8 copy.43
  35.7 0.6 broadcast_and_fusion
  36.3 1.5 %fusion.12 = f32[4,256,153]{1,2,0:T(8,128)S(1)} fusion(f32[153,273,1]{1,0,2:T(8,128)S(1)} %copy-done.7, f32[4,256,256]{2,1,0:T(8,128)S(1)} %bitcast.67, f32[4,16,256]{2,1,0:T(8,128)S(1)} %broadcast_multiply_fusion, f32[273]{0:T(512)} %copy-done.14), kind=kOutput, calls=%fused_computation.15 | convolution fusion | flops 257187840 | bytes 1908968 | tf_op jit(solution)/shard_map/cf,hft->hct/dot_general | solution.py:53
  37.9 1.2 %collective-permute-done = bf16[64,512]{1,0:T(8,128)(2,1)} collective-permute-done((bf16[64,512]{1,0:T(8,128)(2,1)}, bf16[64,512]{1,0:T(8,128)(2,1)}, u32[]{:S(2)}, u32[]{:S(2)}) %collective-permute-start) | collective-permute-done | bytes 65568 | tf_op jit(solution)/shard_map/ppermute | solution.py:24
  39.1 0.8 constant_dynamic-update-slice_fusion.1
  40.1 0.9 pad_maximum_fusion
  41.2 0.7 copy.42
  41.9 3.4 %all-to-all-done = f32[64,1,640]{2,1,0:T(1,128)S(1)} async-done(((f32[64,1,640]{2,1,0:T(1,128)}), f32[64,1,640]{2,1,0:T(1,128)S(1)}, u32[]{:S(2)}, u32[]{:S(2)}) %all-to-all-start) | async-done | bytes 163872 | tf_op jit(solution)/shard_map/all_to_all | solution.py:69
  45.4 0.3 convolution_bitcast_fusion.1
  45.7 0.8 copy.41
  46.5 10.7 %all-to-all-start.1 = ((f32[64,1,640]{2,1,0:T(1,128)}), f32[64,1,640]{2,1,0:T(1,128)S(1)}, u32[]{:S(2)}, u32[]{:S(2)}) async-start(f32[64,1,640]{2,1,0:T(1,128)} %copy.41), calls=%async_computation.1 | async-start | bytes 327680 | tf_op jit(solution)/shard_map/all_to_all | solution.py:73
  57.3 1.2 %convolution_multiply_fusion = f32[4,4,64,128]{3,2,1,0:T(8,128)} fusion(bf16[4,64,4,128]{3,1,2,0:T(8,128)(2,1)S(1)} %copy.45, bf16[4,64,4,128]{3,1,2,0:T(8,128)(2,1)S(1)} %copy.44, bf16[4,64,4,128]{3,2,1,0:T(4,128)(2,1)S(1)} %reshape.182), kind=kOutput, calls=%fused_computation.9 | convolution fusion | flops 34734080 | bytes 1310720 | tf_op jit(solution)/shard_map/bihe,bjhe->bhij/dot_general | solution.py:97
  58.6 1.6 %fusion.55 = f32[4,4,64]{2,1,0:T(4,128)S(1)} fusion(f32[4,4,64,128]{3,2,1,0:T(8,128)} %convolution_multiply_fusion, pred[4,64,128]{2,1,0:T(8,128)(4,1)S(1)} %copy-done.12), kind=kOutput, calls=%fused_computation.85 | output fusion | flops 524415 | bytes 561152 | tf_op jit(solution)/shard_map/sub | solution.py:107
  60.1 2.4 %fusion.6 = f32[4,64,4,128]{3,1,2,0:T(8,128)} fusion(bf16[4,64,4,128]{3,1,2,0:T(8,128)(2,1)S(1)} %copy-done.5, bf16[4,64,4,128]{3,1,2,0:T(8,128)(2,1)S(1)} %copy-done.6, f32[4,64,4]{1,2,0:T(4,128)S(1)} %bitcast.86, f32[4,4,64,128]{3,2,1,0:T(8,128)} %convolution_multiply_fusion, pred[4,64,128]{2,1,0:T(8,128)(4,1)S(1)} %copy-done.12), kind=kOutput, calls=%fused_computation.8 | convolution fusion | flops 35259520 | bytes 1609728 | tf_op jit(solution)/shard_map/bhij,bjhe->bihe/dot_general | solution.py:109
  62.5 1.4 %copy.47 = f32[4,64,4,128]{3,2,1,0:T(4,128)S(1)} copy(f32[4,64,4,128]{3,1,2,0:T(8,128)} %fusion.6) | data formatting | bytes 1048576 | tf_op jit(solution)/shard_map/div | solution.py:112
  63.9 0.5 fusion.54
  64.4 1.0 %fusion.30 = f32[4,256,128]{1,2,0:T(8,128)} fusion(bf16[256,4,128]{0,2,1:T(8,128)(2,1)S(1)} %bitcast.70, bf16[4,256,256]{1,2,0:T(8,128)(2,1)S(1)} %get-tuple-element.23), kind=kOutput, calls=%fused_computation.45 | convolution fusion | flops 67108864 | bytes 1310720 | tf_op jit(solution)/shard_map/hts,shv->htv/dot_general | solution.py:123
  65.5 7.8 %all-to-all-done.1 = f32[64,1,640]{2,1,0:T(1,128)S(1)} async-done(((f32[64,1,640]{2,1,0:T(1,128)}), f32[64,1,640]{2,1,0:T(1,128)S(1)}, u32[]{:S(2)}, u32[]{:S(2)}) %all-to-all-start.1) | async-done | bytes 163872 | tf_op jit(solution)/shard_map/all_to_all | solution.py:73
  73.3 2.0 %all-gather.2 = f32[2,1,40960]{2,1,0:T(1,128)S(1)} all-gather(f32[1,1,40960]{2,1,0:T(1,128)S(1)} %bitcast.74), channel_id=1, replica_groups=mesh['cx'=4,'cz'=16,'cc'=2,'head'=4] {'cc'}, dimensions={0}, use_global_device_ids=true | all-gather | bytes 491520 | tf_op jit(solution)/shard_map/all_gather | solution.py:74
  75.4 0.1 reshape.200
  75.5 0.7 reshape.177
  76.2 0.3 fusion.57
  76.5 1.7 %fusion.2 = f32[256,4,128]{0,2,1:T(8,128)S(1)} fusion(f32[4,256,128]{1,2,0:T(8,128)S(1)} %copy-done.2, f32[4,256,153]{1,2,0:T(8,128)S(1)} %fusion.12, f32[4,153,128]{2,1,0:T(8,128)} %reshape.177, f32[256,4]{0,1:T(4,128)S(1)} %fusion.41), kind=kOutput, calls=%fused_computation.4 | convolution fusion | flops 120586240 | bytes 1992704 | tf_op jit(solution)/shard_map/hft,hfv->htv/dot_general | solution.py:173
  78.2 0.2 copy.48
  78.4 0.5 copy-done.16
  78.8 0.3 multiply_reduce_fusion
  79.2 10.0 %all-gather.3 = f32[4,1,256]{2,1,0:T(1,128)S(1)} all-gather(f32[1,1,256]{2,1,0:T(1,128)S(1)} %bitcast.85), channel_id=3, replica_groups=mesh['cx'=4,'cz'=16,'cc'=2,'head'=4] {'head'}, dimensions={0}, use_global_device_ids=true | all-gather | bytes 5120 | tf_op jit(solution)/shard_map/all_gather | solution.py:177
  89.2 0.8 multiply_convert_fusion
  (61 shorter events, 0.8 us)
Async XLA Ops:
  0.0 1.9 %copy-start.8 = (f32[153,273,1]{1,0,2:T(8,128)S(1)}, f32[153,273,1]{1,0,2:T(8,128)}, u32[]{:S(2)}) copy-start(f32[153,273,1]{1,0,2:T(8,128)} %constant.72) | copy-start | bytes 501232
  0.0 1.7 %copy-start.3 = (bf16[256,512]{1,0:T(8,128)(2,1)S(1)}, bf16[256,512]{1,0:T(8,128)(2,1)}, u32[]{:S(2)}) copy-start(bf16[256,512]{1,0:T(8,128)(2,1)} %param.13) | copy-start | bytes 786436
  1.9 1.4 %copy-start.14 = (f32[273]{0:T(512)}, f32[273]{0:T(512)S(1)}, u32[]{:S(2)}) copy-start(f32[273]{0:T(512)S(1)} %pad.16.clone) | copy-start | bytes 3280
  6.1 21.6 %copy-start.1 = (bf16[256,512]{1,0:T(8,128)(2,1)S(1)}, bf16[256,512]{1,0:T(8,128)(2,1)}, u32[]{:S(2)}) copy-start(bf16[256,512]{1,0:T(8,128)(2,1)} %param.15) | copy-start | bytes 786436
  7.9 22.4 %copy-start = (bf16[256,512]{1,0:T(8,128)(2,1)S(1)}, bf16[256,512]{1,0:T(8,128)(2,1)}, u32[]{:S(2)}) copy-start(bf16[256,512]{1,0:T(8,128)(2,1)} %param.16) | copy-start | bytes 786436
  7.9 26.5 %copy-start.9 = (bf16[256,64]{0,1:T(8,128)(2,1)S(1)}, bf16[256,64]{0,1:T(8,128)(2,1)}, u32[]{:S(2)}) copy-start(bf16[256,64]{0,1:T(8,128)(2,1)} %param.11) | copy-start | bytes 98308
  8.9 36.5 %all-to-all-start = ((f32[64,1,640]{2,1,0:T(1,128)}), f32[64,1,640]{2,1,0:T(1,128)S(1)}, u32[]{:S(2)}, u32[]{:S(2)}) async-start(f32[64,1,640]{2,1,0:T(1,128)} %bitcast.4), calls=%async_computation | async-start | bytes 327680 | tf_op jit(solution)/shard_map/all_to_all | solution.py:69
  28.3 11.8 %collective-permute-start.1 = (bf16[64,512]{1,0:T(8,128)(2,1)}, bf16[64,512]{1,0:T(8,128)(2,1)}, u32[]{:S(2)}, u32[]{:S(2)}) collective-permute-start(bf16[64,512]{1,0:T(8,128)(2,1)} %slice.40), channel_id=1, source_target_pairs={{0,4},{4,8},{8,12},{12,16},{16,20},{20,24},{24,28},{28,32},{32,36}... | collective-permute-start | bytes 196616 | tf_op jit(solution)/shard_map/ppermute | solution.py:24
  30.9 8.2 %collective-permute-start = (bf16[64,512]{1,0:T(8,128)(2,1)}, bf16[64,512]{1,0:T(8,128)(2,1)}, u32[]{:S(2)}, u32[]{:S(2)}) collective-permute-start(bf16[64,512]{1,0:T(8,128)(2,1)} %slice.38), channel_id=1, source_target_pairs={{0,4},{4,8},{8,12},{12,16},{16,20},{20,24},{24,28},{28,32},{32,36}... | collective-permute-start | bytes 196616 | tf_op jit(solution)/shard_map/ppermute | solution.py:24
  34.6 1.8 %copy-start.7 = (f32[153,273,1]{1,0,2:T(8,128)S(1)}, f32[153,273,1]{1,0,2:T(8,128)}, u32[]{:S(2)}) copy-start(f32[153,273,1]{1,0,2:T(8,128)} %constant.73) | copy-start | bytes 501232
  35.7 2.1 %copy-start.15 = (bf16[3,512]{1,0:T(4,128)(2,1)S(1)}, bf16[3,512]{1,0:T(4,128)(2,1)}, u32[]{:S(2)}) copy-start(bf16[3,512]{1,0:T(4,128)(2,1)} %param.17) | copy-start | bytes 9220
  41.1 4.3 %copy-start.13 = (f32[64,64]{1,0:T(8,128)S(1)}, f32[64,64]{1,0:T(8,128)}, u32[]{:S(2)}) copy-start(f32[64,64]{1,0:T(8,128)} %constant.69.clone) | copy-start | bytes 49156
  41.2 16.0 %copy-start.4 = (bf16[256,512]{1,0:T(8,128)(2,1)S(1)}, bf16[256,512]{1,0:T(8,128)(2,1)}, u32[]{:S(2)}) copy-start(bf16[256,512]{1,0:T(8,128)(2,1)} %param.14) | copy-start | bytes 786436
  46.5 12.0 %copy-start.12 = (pred[4,64,128]{2,1,0:T(8,128)(4,1)S(1)}, pred[4,64,128]{2,1,0:T(8,128)(4,1)}, u32[]{:S(2)}) copy-start(pred[4,64,128]{2,1,0:T(8,128)(4,1)} %broadcast_and_fusion) | copy-start | bytes 98308
  46.5 26.7 %all-to-all-start.1 = ((f32[64,1,640]{2,1,0:T(1,128)}), f32[64,1,640]{2,1,0:T(1,128)S(1)}, u32[]{:S(2)}, u32[]{:S(2)}) async-start(f32[64,1,640]{2,1,0:T(1,128)} %copy.41), calls=%async_computation.1 | async-start | bytes 327680 | tf_op jit(solution)/shard_map/all_to_all | solution.py:73
  57.3 2.8 %copy-start.5 = (bf16[4,64,4,128]{3,1,2,0:T(8,128)(2,1)S(1)}, bf16[4,64,4,128]{3,1,2,0:T(8,128)(2,1)}, u32[]{:S(2)}) copy-start(bf16[4,64,4,128]{3,1,2,0:T(8,128)(2,1)} %copy.43) | copy-start | bytes 786436
  57.3 2.8 %copy-start.6 = (bf16[4,64,4,128]{3,1,2,0:T(8,128)(2,1)S(1)}, bf16[4,64,4,128]{3,1,2,0:T(8,128)(2,1)}, u32[]{:S(2)}) copy-start(bf16[4,64,4,128]{3,1,2,0:T(8,128)(2,1)} %copy.42) | copy-start | bytes 786436
  62.5 1.4 %copy-start.10 = (bf16[256,64]{0,1:T(8,128)(2,1)S(1)}, bf16[256,64]{0,1:T(8,128)(2,1)}, u32[]{:S(2)}) copy-start(bf16[256,64]{0,1:T(8,128)(2,1)} %param.11) | copy-start | bytes 98308
  62.5 1.4 %copy-start.11 = (bf16[256,64]{0,1:T(8,128)(2,1)S(1)}, bf16[256,64]{0,1:T(8,128)(2,1)}, u32[]{:S(2)}) copy-start(bf16[256,64]{0,1:T(8,128)(2,1)} %param.12) | copy-start | bytes 98308
  75.3 1.2 %copy-start.2 = (f32[4,256,128]{1,2,0:T(8,128)S(1)}, f32[4,256,128]{1,2,0:T(8,128)}, u32[]{:S(2)}) copy-start(f32[4,256,128]{1,2,0:T(8,128)} %fusion.30) | copy-start | bytes 1572868
  78.1 0.7 copy-start.16

commit v16 on v12

--- a/solution.py
+++ b/solution.py
@@ -174,7 +174,7 @@
     denom = inner_den + jnp.einsum("hft,hf->ht", phi_q, prior_norm, precision=THREE)
     lin_out = jnp.transpose(numer / denom[..., None], (1, 0, 2)).reshape(count, heads * VDIM)
     mixed = head_gain[None, :] * (lin_out + window_out + conv_out)
-    squares = jnp.sum(lax.all_gather(jnp.sum(mixed * mixed, axis=-1), "head"), axis=0)
+    squares = lax.psum(jnp.sum(mixed * mixed, axis=-1), "head")
     msq = squares / D
     return (mixed * lax.rsqrt(msq + 1e-06)[:, None]).astype(jnp.bfloat16)
 

time: 87.3 us -> 88 us (level)
    psum x0 -> x1, blocking collectives: none -> 10.7 us  [body(): squares = lax.psum(jnp.sum(mixed * mixed, axis=-1), 'head')]
    all_gather x1 -> x0, blocking collectives: 9.99 us -> none  [body(): lax.all_gather(jnp.sum(mixed * mixed, axis=-1), 'head')]
where the time goes in v16:
time: 88 us; the launch traced here: 87.5 us
  starting transfers between devices  31.5 us (36%)
  waiting for transfers between devices  18.4 us (21%)
  blocking collectives  15 us (17%)
  matrix products  8.63 us (10%)
  local copies, waits for them, and re-layouts  8 us (9%)
  other arithmetic  5.51 us (6%)
    all_to_all x1, starting transfers between devices, exclusive_prefix(): lax.all_to_all(share.reshape(chips, -1), ('cx', 'cz'), 0, 0, tiled=True)  18.9 us
    psum x1, blocking collectives, body(): squares = lax.psum(jnp.sum(mixed * mixed, axis=-1), 'head')  10.7 us
    all_to_all x1, waiting for transfers between devices, exclusive_prefix(): back = lax.all_to_all(pref, ('cx', 'cz'), 0, 0, tiled=True)  10.7 us
    all_to_all x1, starting transfers between devices, exclusive_prefix(): back = lax.all_to_all(pref, ('cx', 'cz'), 0, 0, tiled=True)  7.15 us
    all_to_all x1, waiting for transfers between devices, exclusive_prefix(): lax.all_to_all(share.reshape(chips, -1), ('cx', 'cz'), 0, 0, tiled=True)  6.46 us
    ppermute x2, starting transfers between devices, passed_along(): return lax.ppermute(shard, axis, pairs)  5.39 us
    all_gather x1, blocking collectives, exclusive_prefix(): pair = lax.all_gather(flat, 'cc')  2.28 us
    dot_general x1, matrix products, window_slab(): jnp.einsum('bhij,bjhe->bihe', prob.astype(jnp.bfloat16), vals, preferred_...  2.21 us
  transfers between devices with their start and end apart: 4, of which 3 were waited for; matrix products, arithmetic and copies ran while one was open for 13% of the time, Pallas kernels for 0%

profile of v16, /device:TPU:6, one launch (start us, length us, event | category | flops | bytes accessed | tf_op | source)
XLA Modules:
  0.0 87.5 jit_solution(8667127888139320124)
XLA Ops:
  0.0 0.8 convert_bitcast_fusion
  0.8 0.8 broadcast_multiply_fusion
  1.6 0.1 multiply_multiply_fusion
  1.8 1.0 %fusion.58 = (f32[4,153]{1,0:T(4,128)S(1)}, f32[4,256,153]{1,2,0:T(8,128)S(1)}) fusion(f32[153,273,1]{1,0,2:T(8,128)S(1)} %copy-done.6, f32[4,256,256]{2,1,0:T(8,128)S(1)} %bitcast.80, f32[4,16,256]{2,1,0:T(8,128)S(1)} %broadcast_multiply_fusion, f32[273]{0:T(512)S(1)} %pad.16.clone), kind=kOutput, calls=%fused_computation.88 | convolution fusion | flops 257343904 | bytes 1911416 | tf_op jit(solution)/shard_map/cf,hft->hct/dot_general | solution.py:53
  2.8 0.3 fusion.33
  3.2 0.1 reshape.170
  3.3 2.3 %all-gather = f32[163840]{0:T(1024)S(1)} all-gather(f32[81920]{0:T(1024)S(1)} %select_maximum_fusion), channel_id=2, replica_groups=mesh['cx'=4,'cz'=16,'cc'=2,'head'=4] {'cc'}, dimensions={0}, use_global_device_ids=true | all-gather | bytes 983040 | tf_op jit(solution)/shard_map/all_gather | solution.py:65
  5.6 0.4 reshape.182
  6.0 1.7 %select_reduce_fusion.1 = (f32[81920]{0:T(1024)S(1)}, f32[81920]{0:T(1024)S(1)}) fusion(f32[2,81920]{1,0:T(2,128)S(1)} %reshape.182, pred[2]{0:T(512)(128)(4,1)S(1)} %iota_compare_fusion.4), kind=kLoop, calls=%fused_computation.26 | loop fusion | flops 327680 | bytes 1310722 | tf_op jit(solution)/shard_map/reduce_sum | solution.py:58
  7.7 0.2 reshape.171
  7.9 0.8 constant_dynamic-slice_fusion
  8.8 18.9 %all-to-all-start = ((f32[64,1,640]{2,1,0:T(1,128)}), f32[64,1,640]{2,1,0:T(1,128)S(1)}, u32[]{:S(2)}, u32[]{:S(2)}) async-start(f32[64,1,640]{2,1,0:T(1,128)} %bitcast.8), calls=%async_computation | async-start | bytes 327680 | tf_op jit(solution)/shard_map/all_to_all | solution.py:69
  27.7 1.9 %collective-permute-start.1 = (bf16[64,512]{1,0:T(8,128)(2,1)S(1)}, bf16[64,512]{1,0:T(8,128)(2,1)S(1)}, u32[]{:S(2)}, u32[]{:S(2)}) collective-permute-start(bf16[64,512]{1,0:T(8,128)(2,1)S(1)} %slice.40), channel_id=1, source_target_pairs={{0,4},{4,8},{8,12},{12,16},{16,20},{20,24},{24,28},{28,32},{32,36}... | collective-permute-start | bytes 196616 | tf_op jit(solution)/shard_map/ppermute | solution.py:24
  29.7 0.6 slice.38
  30.3 3.5 %collective-permute-start = (bf16[64,512]{1,0:T(8,128)(2,1)}, bf16[64,512]{1,0:T(8,128)(2,1)S(1)}, u32[]{:S(2)}, u32[]{:S(2)}) collective-permute-start(bf16[64,512]{1,0:T(8,128)(2,1)} %slice.38), channel_id=1, source_target_pairs={{0,4},{4,8},{8,12},{12,16},{16,20},{20,24},{24,28},{28,32},{32,36}... | collective-permute-start | bytes 196616 | tf_op jit(solution)/shard_map/ppermute | solution.py:24
  33.9 0.1 multiply_multiply_fusion.1
  34.0 0.5 fusion.59
  34.5 1.1 %fusion.30 = f32[4,256,128]{1,2,0:T(8,128)} fusion(bf16[4,256,256]{1,2,0:T(8,128)(2,1)S(1)} %get-tuple-element.19, bf16[256,512]{1,0:T(8,128)(2,1)S(1)} %copy-done), kind=kOutput, calls=%fused_computation.45 | convolution fusion | flops 67108864 | bytes 1310720 | tf_op jit(solution)/shard_map/hts,shv->htv/dot_general | solution.py:123
  35.6 0.1 add_compare_fusion
  35.7 0.1 fusion.45
  35.8 0.8 fusion.7
  36.7 0.1 reshape.180
  36.7 0.1 reshape.177
  36.9 0.8 copy.43
  37.6 1.2 %collective-permute-done = bf16[64,512]{1,0:T(8,128)(2,1)S(1)} collective-permute-done((bf16[64,512]{1,0:T(8,128)(2,1)}, bf16[64,512]{1,0:T(8,128)(2,1)S(1)}, u32[]{:S(2)}, u32[]{:S(2)}) %collective-permute-start) | collective-permute-done | bytes 65568 | tf_op jit(solution)/shard_map/ppermute | solution.py:24
  38.8 6.5 %all-to-all-done = f32[64,1,640]{2,1,0:T(1,128)S(1)} async-done(((f32[64,1,640]{2,1,0:T(1,128)}), f32[64,1,640]{2,1,0:T(1,128)S(1)}, u32[]{:S(2)}, u32[]{:S(2)}) %all-to-all-start) | async-done | bytes 163872 | tf_op jit(solution)/shard_map/all_to_all | solution.py:69
  45.3 0.3 convolution_bitcast_fusion.1
  45.6 0.8 copy.41
  46.4 7.1 %all-to-all-start.1 = ((f32[64,1,640]{2,1,0:T(1,128)}), f32[64,1,640]{2,1,0:T(1,128)S(1)}, u32[]{:S(2)}, u32[]{:S(2)}) async-start(f32[64,1,640]{2,1,0:T(1,128)} %copy.41), calls=%async_computation.1 | async-start | bytes 327680 | tf_op jit(solution)/shard_map/all_to_all | solution.py:73
  53.7 0.1 convert_element_type.23
  53.7 0.1 reshape.179
  53.9 0.1 reshape.176
  54.0 0.8 copy.42
  54.8 0.4 convolution_multiply_fusion
  55.3 0.4 fusion.60
  55.7 2.2 %fusion.6 = f32[4,64,4,128]{3,1,2,0:T(8,128)} fusion(bf16[4,64,4,128]{3,1,2,0:T(8,128)(2,1)} %copy.43, bf16[4,64,4,128]{3,1,2,0:T(8,128)(2,1)} %copy.42, f32[4,64,4]{1,2,0:T(4,128)S(1)} %bitcast.91, f32[4,4,64,128]{3,2,1,0:T(8,128)S(1)} %convolution_multiply_fusion, pred[4,64,128]{2,1,0:T(8,128)(4,1)S(1)} %broadcast_and_fusion), kind=kOutput, calls=%fused_computation.8 | convolution fusion | flops 35259520 | bytes 1609728 | tf_op jit(solution)/shard_map/bhij,bjhe->bihe/dot_general | solution.py:109
  57.9 1.4 %copy.47 = f32[4,64,4,128]{3,2,1,0:T(4,128)S(1)} copy(f32[4,64,4,128]{3,1,2,0:T(8,128)} %fusion.6) | data formatting | bytes 1048576 | tf_op jit(solution)/shard_map/div | solution.py:112
  59.3 10.7 %all-to-all-done.1 = f32[64,1,640]{2,1,0:T(1,128)S(1)} async-done(((f32[64,1,640]{2,1,0:T(1,128)}), f32[64,1,640]{2,1,0:T(1,128)S(1)}, u32[]{:S(2)}, u32[]{:S(2)}) %all-to-all-start.1) | async-done | bytes 163872 | tf_op jit(solution)/shard_map/all_to_all | solution.py:73
  70.0 2.0 %all-gather.1 = f32[2,1,40960]{2,1,0:T(1,128)S(1)} all-gather(f32[1,1,40960]{2,1,0:T(1,128)S(1)} %bitcast.84), channel_id=1, replica_groups=mesh['cx'=4,'cz'=16,'cc'=2,'head'=4] {'cc'}, dimensions={0}, use_global_device_ids=true | all-gather | bytes 491520 | tf_op jit(solution)/shard_map/all_gather | solution.py:74
  72.1 0.1 reshape.192
  72.2 0.7 reshape.173
  72.9 0.3 fusion.61
  73.2 1.6 %fusion.2 = f32[256,4,128]{0,2,1:T(8,128)S(1)} fusion(f32[4,256,128]{1,2,0:T(8,128)S(1)} %copy-done.3, f32[4,256,153]{1,2,0:T(8,128)S(1)} %fusion.7, f32[4,153,128]{2,1,0:T(8,128)} %reshape.173, f32[256,4]{0,1:T(4,128)S(1)} %fusion.46), kind=kOutput, calls=%fused_computation.4 | convolution fusion | flops 120586240 | bytes 1992704 | tf_op jit(solution)/shard_map/hft,hfv->htv/dot_general | solution.py:173
  74.9 0.2 copy.48
  75.1 0.5 copy-done.11
  75.6 0.3 multiply_reduce_fusion
  75.9 10.7 %psum.7 = f32[256]{0:T(256)S(1)} all-reduce(f32[256]{0:T(256)S(1)} %get-tuple-element.11), channel_id=1, replica_groups=mesh['cx'=4,'cz'=16,'cc'=2,'head'=4] {'head'}, use_global_device_ids=true, to_apply=%region_7.8 | all-reduce | flops 256 | bytes 2048 | tf_op jit(solution)/shard_map/psum | solution.py:177
  86.6 0.8 multiply_convert_fusion
  (49 shorter events, 0.6 us)
Async XLA Ops:
  0.0 2.8 %copy-start = (bf16[256,512]{1,0:T(8,128)(2,1)S(1)}, bf16[256,512]{1,0:T(8,128)(2,1)}, u32[]{:S(2)}) copy-start(bf16[256,512]{1,0:T(8,128)(2,1)} %param.13) | copy-start | bytes 786436
  0.0 1.8 %copy-start.6 = (f32[153,273,1]{1,0,2:T(8,128)S(1)}, f32[153,273,1]{1,0,2:T(8,128)}, u32[]{:S(2)}) copy-start(f32[153,273,1]{1,0,2:T(8,128)} %constant.73) | copy-start | bytes 501232
  6.0 21.7 %copy-start.2 = (bf16[256,512]{1,0:T(8,128)(2,1)S(1)}, bf16[256,512]{1,0:T(8,128)(2,1)}, u32[]{:S(2)}) copy-start(bf16[256,512]{1,0:T(8,128)(2,1)} %param.15) | copy-start | bytes 786436
  7.7 21.9 %copy-start.1 = (bf16[256,512]{1,0:T(8,128)(2,1)S(1)}, bf16[256,512]{1,0:T(8,128)(2,1)}, u32[]{:S(2)}) copy-start(bf16[256,512]{1,0:T(8,128)(2,1)} %param.16) | copy-start | bytes 786436
  7.7 26.0 %copy-start.7 = (bf16[256,64]{0,1:T(8,128)(2,1)S(1)}, bf16[256,64]{0,1:T(8,128)(2,1)}, u32[]{:S(2)}) copy-start(bf16[256,64]{0,1:T(8,128)(2,1)} %param.11) | copy-start | bytes 98308
  8.8 25.2 %copy-start.8 = (bf16[256,64]{0,1:T(8,128)(2,1)S(1)}, bf16[256,64]{0,1:T(8,128)(2,1)}, u32[]{:S(2)}) copy-start(bf16[256,64]{0,1:T(8,128)(2,1)} %param.12) | copy-start | bytes 98308
  8.8 36.5 %all-to-all-start = ((f32[64,1,640]{2,1,0:T(1,128)}), f32[64,1,640]{2,1,0:T(1,128)S(1)}, u32[]{:S(2)}, u32[]{:S(2)}) async-start(f32[64,1,640]{2,1,0:T(1,128)} %bitcast.8), calls=%async_computation | async-start | bytes 327680 | tf_op jit(solution)/shard_map/all_to_all | solution.py:69
  27.7 25.9 %collective-permute-start.1 = (bf16[64,512]{1,0:T(8,128)(2,1)S(1)}, bf16[64,512]{1,0:T(8,128)(2,1)S(1)}, u32[]{:S(2)}, u32[]{:S(2)}) collective-permute-start(bf16[64,512]{1,0:T(8,128)(2,1)S(1)} %slice.40), channel_id=1, source_target_pairs={{0,4},{4,8},{8,12},{12,16},{16,20},{20,24},{24,28},{28,32},{32,36}... | collective-permute-start | bytes 196616 | tf_op jit(solution)/shard_map/ppermute | solution.py:24
  30.3 8.5 %collective-permute-start = (bf16[64,512]{1,0:T(8,128)(2,1)}, bf16[64,512]{1,0:T(8,128)(2,1)S(1)}, u32[]{:S(2)}, u32[]{:S(2)}) collective-permute-start(bf16[64,512]{1,0:T(8,128)(2,1)} %slice.38), channel_id=1, source_target_pairs={{0,4},{4,8},{8,12},{12,16},{16,20},{20,24},{24,28},{28,32},{32,36}... | collective-permute-start | bytes 196616 | tf_op jit(solution)/shard_map/ppermute | solution.py:24
  34.5 1.2 %copy-start.5 = (f32[153,273,1]{1,0,2:T(8,128)S(1)}, f32[153,273,1]{1,0,2:T(8,128)}, u32[]{:S(2)}) copy-start(f32[153,273,1]{1,0,2:T(8,128)} %constant.72) | copy-start | bytes 501232
  35.6 1.1 %copy-start.10 = (bf16[3,512]{1,0:T(4,128)(2,1)S(1)}, bf16[3,512]{1,0:T(4,128)(2,1)}, u32[]{:S(2)}) copy-start(bf16[3,512]{1,0:T(4,128)(2,1)} %param.17) | copy-start | bytes 9220
  36.8 8.5 %copy-start.9 = (f32[64,64]{1,0:T(8,128)S(1)}, f32[64,64]{1,0:T(8,128)}, u32[]{:S(2)}) copy-start(f32[64,64]{1,0:T(8,128)} %constant.69.clone) | copy-start | bytes 49156
  46.4 23.6 %all-to-all-start.1 = ((f32[64,1,640]{2,1,0:T(1,128)}), f32[64,1,640]{2,1,0:T(1,128)S(1)}, u32[]{:S(2)}, u32[]{:S(2)}) async-start(f32[64,1,640]{2,1,0:T(1,128)} %copy.41), calls=%async_computation.1 | async-start | bytes 327680 | tf_op jit(solution)/shard_map/all_to_all | solution.py:73
  53.8 1.0 %copy-start.4 = (bf16[256,512]{1,0:T(8,128)(2,1)S(1)}, bf16[256,512]{1,0:T(8,128)(2,1)}, u32[]{:S(2)}) copy-start(bf16[256,512]{1,0:T(8,128)(2,1)} %param.14) | copy-start | bytes 786436
  72.1 1.2 %copy-start.3 = (f32[4,256,128]{1,2,0:T(8,128)S(1)}, f32[4,256,128]{1,2,0:T(8,128)}, u32[]{:S(2)}) copy-start(f32[4,256,128]{1,2,0:T(8,128)} %fusion.30) | copy-start | bytes 1572868
  74.9 0.7 copy-start.11
